TPU v7x, 128 devices: a whole 4x4x4 slice. The times are simulated.
128 devices in a mesh: req: 8 (over y, x_hi), row: 4 (over x_lo, core), col: 4 (over z).
Axes of the slice: x: 4 (x_hi: 2, x_lo: 2; x = x_hi * 2 + x_lo), y: 4, z: 4, core: 2. Of those that a mesh axis runs over, the one named last changes fastest.
Arguments:
- text_embed: bfloat16 [6144, 4096], P(('req', 'col'), 'row')
- vis_embed: bfloat16 [4096, 4096], P(('req', 'col'), 'row')
- vis_segment: int32 [4096], P(('req', 'col')), may hold values from 0 to 20, never falling along the last dimension, each value on 1 to 256 neighbouring positions
- vis_valid: int32 [4096], P(('req', 'col')), may hold values 0 or 1
- vis_gain: bfloat16 [4096], P('row'), may hold values from 0.25 to 1.75
- vis_wq: bfloat16 [4096, 4096], P('row', 'col')
- vis_wk: bfloat16 [4096, 4096], P('row', 'col')
- vis_wv: bfloat16 [4096, 4096], P('row', 'col'), may hold values from -0.09375 to 0.09375
- vis_wo: bfloat16 [4096, 4096], P('col', 'row'), may hold values from -0.09375 to 0.09375
- dec_gain: bfloat16 [4096], P('row'), may hold values from 0.25 to 1.75
- dec_wq: bfloat16 [4096, 4096], P('row', 'col')
- dec_wk: bfloat16 [4096, 4096], P('row', 'col')
- dec_wv: bfloat16 [4096, 4096], P('row', 'col'), may hold values from -0.09375 to 0.09375
- dec_wo: bfloat16 [4096, 4096], P('col', 'row'), may hold values from -0.09375 to 0.09375
Outputs:
- hidden_out: bfloat16 [6144, 4096], P(('req', 'col'), 'row')
Inputs may be any that keep to these rules, and one draw needn't show every extreme that they name: `vis_segment`: images take consecutive slots in order, each 1 to 256 slots, one exactly 256.
All inputs are finite; a program needn't handle non-finite values. No bound on the sum of `vis_valid` on one device may be relied on, other than what follows from the above.
Results may differ from a plain program's by a relative error of at most 0.008.
Values may be sent and summed in bfloat16 or wider, within the bound.
No kernel may reach another device: no remote copies, remote signals or barrier semaphores. Data moves between devices by JAX's collectives and lax.ppermute only.
A program may use at most 192 MiB of HBM per device.

v0:
```python
import jax
import jax.numpy as jnp
from jax import lax
from jax.sharding import PartitionSpec as P
from jax.experimental import pallas as pl
from jax.experimental.pallas import tpu as pltpu

D = 4096
HD = 128
MAXIMG = 256


def with_halo(cells, sides, width):
    for axis, dim in sides:
        count = lax.axis_size(axis)
        ends = count - 1
        head = lax.slice_in_dim(cells, 0, width, axis=dim)
        tail = lax.slice_in_dim(cells, cells.shape[dim] - width, cells.shape[dim], axis=dim)
        cells = jnp.concatenate(
            [
                lax.ppermute(tail, axis, [(i, (i + 1) % count) for i in range(ends)]),
                cells,
                lax.ppermute(head, axis, [((i + 1) % count, i) for i in range(ends)]),
            ],
            axis=dim,
        )
    return cells


def passed_along(shard, axis, by):
    size = lax.axis_size(axis)
    pairs = [(i, i + by) for i in range(size) if 0 <= i + by < size]
    return lax.ppermute(shard, axis, pairs)


def norm_local(values, gain):
    floats = values.astype(jnp.float32)
    squares = jnp.sum(floats * floats, axis=-1)
    totals = squares + flip(squares, "row", 1)
    totals = totals + flip(totals, "row", 2)
    factor = lax.rsqrt(totals / D + 1e-05)
    return (floats * factor[:, None] * gain.astype(jnp.float32)[None, :]).astype(jnp.bfloat16)


def gather_permute(values, axis):
    count = lax.axis_size(axis)
    index = lax.axis_index(axis)
    rows = values.shape[0]
    got = [values] + [
        lax.ppermute(values, axis, [(j, (j + s) % count) for j in range(count)])
        for s in range(1, count)
    ]
    ahead = jnp.concatenate([got[0]] + got[:0:-1], axis=0)
    twice = jnp.concatenate([ahead, ahead], axis=0)
    start = ((count - index) % count) * rows
    return lax.dynamic_slice_in_dim(twice, start, count * rows, axis=0)


def scatter_permute(values, axis):
    count = lax.axis_size(axis)
    index = lax.axis_index(axis)
    rows = values.shape[0] // count
    total = lax.dynamic_slice_in_dim(values, index * rows, rows, axis=0).astype(jnp.float32)
    for s in range(1, count):
        chunk = lax.dynamic_slice_in_dim(values, ((index + s) % count) * rows, rows, axis=0)
        total = total + lax.ppermute(
            chunk, axis, [(j, (j + s) % count) for j in range(count)]
        ).astype(jnp.float32)
    return total


def gather_cols(values):
    return gather_permute(values, "col")


def out_project(attended, weight):
    whole = lax.all_gather(attended, "row", axis=0, tiled=True)
    return lax.psum_scatter(
        jnp.dot(whole, weight, preferred_element_type=jnp.float32).astype(jnp.bfloat16),
        "col",
        scatter_dimension=0,
        tiled=True,
    ).astype(jnp.float32)


def split_heads(values):
    return values.reshape(values.shape[0], values.shape[1] // HD, HD)


def attend_block(queries, keys, values, allowed):
    query_heads = split_heads(queries)
    scores = jnp.einsum(
        "qhd,khd->hqk", query_heads, split_heads(keys), preferred_element_type=jnp.float32
    ) * HD ** (-0.5)
    scores = jnp.where(allowed[None], scores, -1e30)
    peak = jnp.max(scores, axis=-1, keepdims=True)
    weights = jnp.where(allowed[None], jnp.exp(scores - peak), 0.0)
    mass = jnp.sum(weights, axis=-1)
    summed = jnp.einsum(
        "hqk,khd->qhd",
        weights.astype(jnp.bfloat16),
        split_heads(values),
        preferred_element_type=jnp.float32,
    )
    result = summed / jnp.transpose(mass)[:, :, None]
    return result.reshape(queries.shape[0], queries.shape[1]).astype(jnp.bfloat16)


def fold_step(carry, query_heads, query_slots, key_heads, value_heads):
    peak, mass, accum = carry
    piece_slots = jnp.arange(key_heads.shape[0], dtype=jnp.int32)
    allowed = query_slots[:, None] >= piece_slots[None, :]
    scores = jnp.einsum(
        "qhd,khd->hqk", query_heads, key_heads, preferred_element_type=jnp.float32
    ) * HD ** (-0.5)
    scores = jnp.where(allowed[None], scores, -1e30)
    new_peak = jnp.maximum(peak, jnp.max(scores, axis=-1))
    weights = jnp.where(allowed[None], jnp.exp(scores - new_peak[:, :, None]), 0.0)
    summed = jnp.einsum(
        "hqk,khd->hqd",
        weights.astype(jnp.bfloat16),
        value_heads,
        preferred_element_type=jnp.float32,
    )
    return (new_peak, jnp.sum(weights, axis=-1), summed)


def start_state(head_count, query_count):
    return (
        jnp.full((head_count, query_count), -1e30, jnp.float32),
        jnp.zeros((head_count, query_count), jnp.float32),
        jnp.zeros((head_count, query_count, HD), jnp.float32),
    )


def flip(values, axis, bit):
    count = lax.axis_size(axis)
    return lax.ppermute(values, axis, [(j, j ^ bit) for j in range(count)])


def scatter_row(values):
    rows = values.shape[0] // 4
    chunk = [values[k * rows : (k + 1) * rows] for k in range(4)]
    sent = flip(jnp.concatenate([chunk[1], chunk[3]], axis=0), "row", 1)
    near = chunk[0].astype(jnp.float32) + sent[:rows].astype(jnp.float32)
    far = (chunk[2].astype(jnp.float32) + sent[rows:].astype(jnp.float32)).astype(jnp.bfloat16)
    return (near + flip(far, "row", 2).astype(jnp.float32)).astype(jnp.bfloat16)


def gather_row(values):
    count = lax.axis_size("row")
    index = lax.axis_index("row")
    got = [values] + [flip(values, "row", b) for b in range(1, count)]
    stacked = jnp.stack(got)
    order = jnp.arange(count, dtype=jnp.int32) ^ index
    return jnp.take(stacked, order, axis=0)


def received(values, axis):
    count = lax.axis_size(axis)
    return [values] + [
        lax.ppermute(values, axis, [(j, (j + s) % count) for j in range(count)])
        for s in range(1, count)
    ]


def head_project(pieces, weights, axis):
    row_count = lax.axis_size("row")
    count = len(pieces)
    rows, depth = pieces[0].shape
    part = weights[0].shape[1] // row_count
    groups = len(weights)
    index = jnp.stack([lax.axis_index(axis), lax.axis_index("row")]).astype(jnp.int32)

    def body(index_ref, *refs):
        x_refs = refs[:count]
        w_refs = refs[count : count + groups]
        o_ref = refs[-1]
        own = index_ref[0]
        for s in range(count):
            start = pl.multiple_of(((own - s + count) % count) * rows, 8)
            for g in range(groups):
                o_ref[0, pl.ds(start, rows), g * part : (g + 1) * part] = jnp.dot(
                    x_refs[s][...], w_refs[g][...], preferred_element_type=jnp.float32
                ).astype(o_ref.dtype)

    grid_spec = pltpu.PrefetchScalarGridSpec(
        num_scalar_prefetch=1,
        grid=(row_count,),
        in_specs=[pl.BlockSpec((rows, depth), lambda r, i: (0, 0)) for _ in pieces]
        + [pl.BlockSpec((depth, part), lambda r, i: (0, r)) for _ in weights],
        out_specs=pl.BlockSpec(
            (1, count * rows, groups * part),
            lambda r, i: ((r % 2 + i[1] % 2) % 2 + 2 * ((r // 2 + i[1] // 2) % 2), 0, 0),
        ),
    )
    summed = pl.pallas_call(
        body,
        grid_spec=grid_spec,
        out_shape=jax.ShapeDtypeStruct((row_count, count * rows, groups * part), jnp.bfloat16),
    )(index, *pieces, *weights)
    summed = summed.reshape(row_count * count * rows, groups * part)
    return scatter_row(summed)


def out_project_heads(attended, weight):
    row_count = lax.axis_size("row")
    whole = gather_row(attended)
    shaped = weight.reshape(row_count, weight.shape[0] // row_count, weight.shape[1])
    summed = jnp.einsum("rtf,rfo->to", whole, shaped, preferred_element_type=jnp.float32)
    return scatter_permute(summed.astype(jnp.bfloat16), "col")


def causal_attend(proj, blocks, shifts, place, carry=None, last=True):
    count = proj.shape[0]
    heads = proj.shape[1] // (3 * HD)
    steps = blocks.shape[0]
    scale = HD ** (-0.5)
    shift_table = jnp.asarray(shifts, jnp.int32)

    def body(place_ref, shift_ref, q_ref, kv_ref, *refs):
        if carry is None:
            outs = refs[:-3]
        else:
            peak_in, mass_in, acc_in = refs[:3]
            outs = refs[3:-3]
        peak_ref, mass_ref, acc_ref = refs[-3:]
        step = pl.program_id(0)
        shift = shift_ref[step]
        own = place_ref[0]

        @pl.when(step == 0)
        def _():
            if carry is None:
                peak_ref[...] = jnp.full(peak_ref.shape, -1e30, jnp.float32)
                mass_ref[...] = jnp.zeros(mass_ref.shape, jnp.float32)
                acc_ref[...] = jnp.zeros(acc_ref.shape, jnp.float32)
            else:
                peak_ref[...] = peak_in[...]
                mass_ref[...] = mass_in[...]
                acc_ref[...] = acc_in[...]

        def fold(masked):
            def one(h, unused):
                lane = pl.multiple_of(h * HD, HD)
                scores = lax.dot_general(
                    q_ref[:, pl.ds(lane, HD)],
                    kv_ref[:, pl.ds(lane, HD)],
                    (((1,), (1,)), ((), ())),
                    preferred_element_type=jnp.float32,
                ) * scale
                if masked:
                    rows = lax.broadcasted_iota(jnp.int32, scores.shape, 0)
                    cols = lax.broadcasted_iota(jnp.int32, scores.shape, 1)
                    allowed = cols <= rows
                    scores = jnp.where(allowed, scores, -1e30)
                old = peak_ref[h]
                new = jnp.maximum(old, jnp.max(scores, axis=1, keepdims=True))
                weights = jnp.exp(scores - new)
                if masked:
                    weights = jnp.where(allowed, weights, 0.0)
                shrink = jnp.exp(old - new)
                mass_ref[h] = shrink * mass_ref[h] + jnp.sum(weights, axis=1, keepdims=True)
                acc_ref[h] = shrink * acc_ref[h] + jnp.dot(
                    weights.astype(jnp.bfloat16),
                    kv_ref[:, pl.ds(lane + heads * HD, HD)],
                    preferred_element_type=jnp.float32,
                )
                peak_ref[h] = new
                return unused

            lax.fori_loop(0, heads, one, 0)

        @pl.when((shift > 0) & (shift <= own))
        def _():
            fold(False)

        @pl.when(shift == 0)
        def _():
            fold(True)

        @pl.when(step == steps - 1)
        def _():
            if last:
                for h in range(heads):
                    outs[0][:, h * HD : (h + 1) * HD] = (acc_ref[h] / mass_ref[h]).astype(
                        outs[0].dtype
                    )
            else:
                outs[0][...] = peak_ref[...]
                outs[1][...] = mass_ref[...]
                outs[2][...] = acc_ref[...]

    state_specs = [
        pl.BlockSpec((heads, count, 1), lambda j, p, s: (0, 0, 0)),
        pl.BlockSpec((heads, count, 1), lambda j, p, s: (0, 0, 0)),
        pl.BlockSpec((heads, count, HD), lambda j, p, s: (0, 0, 0)),
    ]
    state_shapes = [
        jax.ShapeDtypeStruct((heads, count, 1), jnp.float32),
        jax.ShapeDtypeStruct((heads, count, 1), jnp.float32),
        jax.ShapeDtypeStruct((heads, count, HD), jnp.float32),
    ]
    in_specs = [
        pl.BlockSpec((count, heads * HD), lambda j, p, s: (0, 0)),
        pl.BlockSpec((None, count, 2 * heads * HD), lambda j, p, s: (j, 0, 0)),
    ]
    if carry is not None:
        in_specs = in_specs + state_specs
    if last:
        out_specs = pl.BlockSpec((count, heads * HD), lambda j, p, s: (0, 0))
        out_shape = jax.ShapeDtypeStruct((count, heads * HD), jnp.bfloat16)
    else:
        out_specs = state_specs
        out_shape = state_shapes
    grid_spec = pltpu.PrefetchScalarGridSpec(
        num_scalar_prefetch=2,
        grid=(steps,),
        in_specs=in_specs,
        out_specs=out_specs,
        scratch_shapes=[
            pltpu.VMEM((heads, count, 1), jnp.float32),
            pltpu.VMEM((heads, count, 1), jnp.float32),
            pltpu.VMEM((heads, count, HD), jnp.float32),
        ],
    )
    extra = () if carry is None else tuple(carry)
    return pl.pallas_call(
        body,
        grid_spec=grid_spec,
        out_shape=out_shape,
    )(place, shift_table, proj, blocks, *extra)


def per_device(
    text_embed,
    vis_embed,
    vis_segment,
    vis_valid,
    vis_gain,
    vis_wq,
    vis_wk,
    vis_wv,
    vis_wo,
    dec_gain,
    dec_wq,
    dec_wk,
    dec_wv,
    dec_wo,
):
    row_count = lax.axis_size("row")
    col_count = lax.axis_size("col")
    width = vis_wq.shape[1]
    local = width // row_count
    margin = MAXIMG - 1
    piece_ids = gather_permute(jnp.stack([vis_segment, vis_valid], axis=1), "col").T
    piece_len = piece_ids.shape[1]
    framed_ids = with_halo(piece_ids, (("req", 1),), margin)
    total_slots = piece_len * lax.axis_size("req")
    prompt_rows = text_embed.shape[0]
    prompt_total = prompt_rows * lax.axis_size("req") * col_count
    window_len = piece_len + 2 * margin
    window_start = lax.axis_index("req") * piece_len - margin
    window_index = jnp.arange(window_len, dtype=jnp.int32)
    key_slots = window_start + window_index
    inside = (key_slots >= 0) & (key_slots < total_slots)
    key_segment = framed_ids[0]
    key_valid = framed_ids[1]
    begins = jnp.concatenate([jnp.ones((1,), jnp.bool_), key_segment[1:] != key_segment[:-1]])
    begins = begins | (key_slots == 0)
    image_first = lax.cummax(jnp.where(begins, key_slots, window_start), axis=0)
    target_window = image_first * prompt_total // total_slots + key_slots - image_first
    vis_cols = received(norm_local(vis_embed, vis_gain), "col")
    vis_proj = head_project(vis_cols, (vis_wq, vis_wk, vis_wv), "col")
    vis_pairs = jnp.stack([vis_proj[:, local : 2 * local], vis_proj[:, 2 * local :]])
    framed = with_halo(vis_pairs, (("req", 1),), margin)
    query_local = margin + jnp.arange(piece_len, dtype=jnp.int32)
    query_slots = window_start + query_local
    query_segment = key_segment[query_local]
    seen = (
        inside[None, :]
        & (query_segment[:, None] == key_segment[None, :])
        & ((key_valid[None, :] == 1) | (query_slots[:, None] == key_slots[None, :]))
    )
    vis_att = attend_block(vis_proj[:, :local], framed[0], framed[1], seen)
    vis_out = (vis_embed.astype(jnp.float32) + out_project_heads(vis_att, vis_wo)).astype(
        jnp.bfloat16
    )
    device_place = lax.axis_index("req") * col_count + lax.axis_index("col")
    owned = device_place * prompt_rows + jnp.arange(prompt_rows, dtype=jnp.int32)
    slot_rows = vis_out.shape[0]
    following = passed_along(vis_out, ("req", "col"), -1)
    near_rows = jnp.concatenate([vis_out, following], axis=0)
    near_local = (
        margin + lax.axis_index("col") * slot_rows + jnp.arange(2 * slot_rows, dtype=jnp.int32)
    )
    near_slots = window_start + near_local
    present = near_slots < total_slots
    near_target = jnp.where(present, target_window[near_local], -1)
    near_valid = key_valid[near_local]
    onehot = ((owned[:, None] == near_target[None, :]) & (near_valid[None, :] == 1)).astype(
        jnp.bfloat16
    )
    carried = jnp.dot(onehot, near_rows, preferred_element_type=jnp.float32)
    mixed = (text_embed.astype(jnp.float32) + carried).astype(jnp.bfloat16)
    dec_cols = received(norm_local(mixed, dec_gain), "col")
    dec_proj = head_project(dec_cols, (dec_wq, dec_wk, dec_wv), "col")
    dec_rows = dec_proj.shape[0]
    keyvals = dec_proj[:, local:]
    req_count = lax.axis_size("req")
    earlier = [keyvals] + [
        lax.ppermute(keyvals, "req", [(j, j + s) for j in range(req_count - s)])
        for s in range(1, req_count)
    ]
    place = lax.axis_index("req").astype(jnp.int32).reshape(1)
    near = [s for s in range(0, req_count, 2)]
    far = [s for s in range(1, req_count, 2)]
    state = causal_attend(
        dec_proj, jnp.stack([earlier[s] for s in near]), near, place, last=False
    )
    dec_att = causal_attend(
        dec_proj, jnp.stack([earlier[s] for s in far]), far, place, carry=state
    )
    return (mixed.astype(jnp.float32) + out_project_heads(dec_att, dec_wo)).astype(jnp.bfloat16)


def solution(mesh):
    return jax.shard_map(
        per_device,
        mesh=mesh,
        in_specs=(
            P(("req", "col"), "row"),
            P(("req", "col"), "row"),
            P(("req", "col")),
            P(("req", "col")),
            P("row"),
            P("row", "col"),
            P("row", "col"),
            P("row", "col"),
            P("col", "row"),
            P("row"),
            P("row", "col"),
            P("row", "col"),
            P("row", "col"),
            P("col", "row"),
        ),
        out_specs=P(("req", "col"), "row"),
        check_vma=False,
    )
```

profile of v0, /device:TPU:28, one launch (start us, length us, event | category | flops | bytes accessed | tf_op | source)
XLA Modules:
  0.0 399.3 jit_solution(7536141493201329188)
XLA Ops:
  15.7 4.8 %collective-permute-done.9.refs_3_ = bf16[128,1024]{1,0:T(8,128)(2,1)S(1)} collective-permute-done((bf16[128,1024]{1,0:T(8,128)(2,1)S(1)}, bf16[128,1024]{1,0:T(8,128)(2,1)S(1)}, u32[]{:S(2)}, u32[]{:S(2)}) %collective-permute-start.9) | collective-permute-done | bytes 262176 | tf_op jit(solution)/shard_map/ppermute | solution.py:162
  26.3 8.5 %shard_map.154 = bf16[4,512,768]{2,1,0:T(8,128)(2,1)} custom-call(s32[2]{0:T(128)} %pad_add_fusion.2.index_ref, bf16[128,1024]{1,0:T(8,128)(2,1)} %copy-done.6, bf16[128,1024]{1,0:T(8,128)(2,1)} %copy-done.15, bf16[128,1024]{1,0:T(8,128)(2,1)} %copy-done.14, bf16[128,1024]{1,0:T(8,128)(2,1)} %copy-done.13, bf16[1024,1024]{1,0:T(8,128)(2,1)} %refs_4_.2, ...), custom_call_target="tpu_custom_call" | custom-call | tf_op jit(solution)/shard_map/pallas_call | solution.py:197
  46.3 6.1 %collective-permute-start.4 = (s32[2,255]{1,0:T(2,128)S(1)}, s32[2,255]{1,0:T(2,128)S(1)}, u32[]{:S(2)}, u32[]{:S(2)}) collective-permute-start(s32[2,255]{1,0:T(2,128)S(1)} %get-tuple-element.33), channel_id=1, source_target_pairs={{16,0},{32,16},{48,32},{64,48},{80,64},{96,80},{112,96},{17,1},{33... | collective-permute-start | bytes 6128 | tf_op jit(solution)/shard_map/ppermute | solution.py:23
  52.4 11.2 %collective-permute-done.3 = s32[2,255]{1,0:T(2,128)S(1)} collective-permute-done((s32[2,255]{1,0:T(2,128)S(1)}, s32[2,255]{1,0:T(2,128)S(1)}, u32[]{:S(2)}, u32[]{:S(2)}) %collective-permute-start.3) | collective-permute-done | bytes 2072 | tf_op jit(solution)/shard_map/ppermute | solution.py:21
  67.6 6.8 %collective-permute-start.13 = (bf16[2,255,256]{2,1,0:T(8,128)(2,1)S(1)}, bf16[2,255,256]{2,1,0:T(8,128)(2,1)}, u32[]{:S(2)}, u32[]{:S(2)}) collective-permute-start(bf16[2,255,256]{2,1,0:T(8,128)(2,1)S(1)} %get-tuple-element.29), channel_id=1, source_target_pairs={{16,0},{32,16},{48,32},{64,48},{80,64},{96,80},{112,96},{17,1},{33... | collective-permute-start | bytes 783368 | tf_op jit(solution)/shard_map/ppermute | solution.py:23
  90.3 6.0 %collective-permute-done.16 = bf16[512,256]{1,0:T(8,128)(2,1)S(1)} collective-permute-done((bf16[512,256]{1,0:T(8,128)(2,1)S(1)}, bf16[512,256]{1,0:T(8,128)(2,1)S(1)}, u32[]{:S(2)}, u32[]{:S(2)}) %collective-permute-start.16) | collective-permute-done | bytes 262176 | tf_op jit(solution)/shard_map/ppermute | solution.py:138
  96.3 5.0 %collective-permute-done.15 = bf16[512,256]{1,0:T(8,128)(2,1)S(1)} collective-permute-done((bf16[512,256]{1,0:T(8,128)(2,1)S(1)}, bf16[512,256]{1,0:T(8,128)(2,1)S(1)}, u32[]{:S(2)}, u32[]{:S(2)}) %collective-permute-start.15) | collective-permute-done | bytes 262176 | tf_op jit(solution)/shard_map/ppermute | solution.py:138
  114.5 5.2 %collective-permute-done.17 = bf16[128,1024]{1,0:T(8,128)(2,1)} collective-permute-done((bf16[128,1024]{1,0:T(8,128)(2,1)}, bf16[128,1024]{1,0:T(8,128)(2,1)}, u32[]{:S(2)}, u32[]{:S(2)}) %collective-permute-start.17) | collective-permute-done | bytes 262176 | tf_op jit(solution)/shard_map/ppermute | solution.py:66
  120.1 4.4 %collective-permute-done.18 = bf16[128,1024]{1,0:T(8,128)(2,1)} collective-permute-done((bf16[128,1024]{1,0:T(8,128)(2,1)}, bf16[128,1024]{1,0:T(8,128)(2,1)}, u32[]{:S(2)}, u32[]{:S(2)}) %collective-permute-start.18) | collective-permute-done | bytes 262176 | tf_op jit(solution)/shard_map/ppermute | solution.py:66
  126.6 8.2 %collective-permute-start.20 = (bf16[128,1024]{1,0:T(8,128)(2,1)}, bf16[128,1024]{1,0:T(8,128)(2,1)S(1)}, u32[]{:S(2)}, u32[]{:S(2)}) collective-permute-start(bf16[128,1024]{1,0:T(8,128)(2,1)} %fusion.32), channel_id=1, source_target_pairs={{1,0},{2,1},{3,2},{16,3},{17,16},{18,17},{19,18},{32,19},{33,32},{... | collective-permute-start | bytes 786440 | tf_op jit(solution)/shard_map/ppermute | solution.py:33
  136.2 4.2 %collective-permute-done.20 = bf16[128,1024]{1,0:T(8,128)(2,1)S(1)} collective-permute-done((bf16[128,1024]{1,0:T(8,128)(2,1)}, bf16[128,1024]{1,0:T(8,128)(2,1)S(1)}, u32[]{:S(2)}, u32[]{:S(2)}) %collective-permute-start.20) | collective-permute-done | bytes 262176 | tf_op jit(solution)/shard_map/ppermute | solution.py:33
  149.0 10.0 %collective-permute-done.25.refs_3_ = bf16[192,1024]{1,0:T(8,128)(2,1)S(1)} collective-permute-done((bf16[192,1024]{1,0:T(8,128)(2,1)S(1)}, bf16[192,1024]{1,0:T(8,128)(2,1)S(1)}, u32[]{:S(2)}, u32[]{:S(2)}) %collective-permute-start.25) | collective-permute-done | bytes 393248 | tf_op jit(solution)/shard_map/ppermute | solution.py:162
  161.4 5.7 %collective-permute-done.23.refs_1_ = bf16[192,1024]{1,0:T(8,128)(2,1)} collective-permute-done((bf16[192,1024]{1,0:T(8,128)(2,1)S(1)}, bf16[192,1024]{1,0:T(8,128)(2,1)}, u32[]{:S(2)}, u32[]{:S(2)}) %collective-permute-start.23) | collective-permute-done | bytes 393248 | tf_op jit(solution)/shard_map/ppermute | solution.py:162
  167.1 10.1 %shard_map.155 = bf16[4,768,768]{2,1,0:T(8,128)(2,1)} custom-call(s32[2]{0:T(128)} %pad_add_fusion.2.index_ref, bf16[192,1024]{1,0:T(8,128)(2,1)} %copy-done.4, bf16[192,1024]{1,0:T(8,128)(2,1)} %collective-permute-done.23.refs_1_, bf16[192,1024]{1,0:T(8,128)(2,1)} %copy-done.10, bf16[192,1024]{1,0:T(8,128)(2,1)} %copy-done.9, bf16[1024,1024]{1,0:T(8,128)(2,1)} %refs_4_.3, ...), custom_call_target="tpu_custom_call" | custom-call | tf_op jit(solution)/shard_map/pallas_call | solution.py:197
  179.3 4.5 %collective-permute-done.26 = bf16[1536,768]{1,0:T(8,128)(2,1)S(1)} collective-permute-done((bf16[1536,768]{1,0:T(8,128)(2,1)S(1)}, bf16[1536,768]{1,0:T(8,128)(2,1)S(1)}, u32[]{:S(2)}, u32[]{:S(2)}) %collective-permute-start.26) | collective-permute-done | bytes 2359328 | tf_op jit(solution)/shard_map/ppermute | solution.py:138
  185.1 27.1 %collective-permute-done.27 = bf16[768,768]{1,0:T(8,128)(2,1)S(1)} collective-permute-done((bf16[768,768]{1,0:T(8,128)(2,1)S(1)}, bf16[768,768]{1,0:T(8,128)(2,1)S(1)}, u32[]{:S(2)}, u32[]{:S(2)}) %collective-permute-start.27) | collective-permute-done | bytes 1179680 | tf_op jit(solution)/shard_map/ppermute | solution.py:138
  220.3 55.5 %collective-permute-done.33 = bf16[768,512]{1,0:T(8,128)(2,1)S(1)} collective-permute-done((bf16[768,512]{1,0:T(8,128)(2,1)}, bf16[768,512]{1,0:T(8,128)(2,1)S(1)}, u32[]{:S(2)}, u32[]{:S(2)}) %collective-permute-start.33) | collective-permute-done | bytes 786464 | tf_op jit(solution)/shard_map/ppermute | solution.py:412
  279.1 13.4 %collective-permute-done.34 = bf16[768,512]{1,0:T(8,128)(2,1)S(1)} collective-permute-done((bf16[768,512]{1,0:T(8,128)(2,1)}, bf16[768,512]{1,0:T(8,128)(2,1)S(1)}, u32[]{:S(2)}, u32[]{:S(2)}) %collective-permute-start.34) | collective-permute-done | bytes 786464 | tf_op jit(solution)/shard_map/ppermute | solution.py:412
  294.3 22.9 %shard_map.156 = (f32[2,768,1]{2,1,0:T(8,128)}, f32[2,768,1]{2,1,0:T(8,128)}, f32[2,768,128]{2,1,0:T(8,128)}) custom-call(s32[1]{0:T(128)} %bitcast.28.place_ref, s32[4]{0:T(128)} %iota_multiply_fusion.shift_ref, bf16[768,768]{1,0:T(8,128)(2,1)} %copy-done.2, bf16[4,768,512]{2,1,0:T(8,128)(2,1)} %pad_maximum_fusion.1.kv_ref), custom_call_target="tpu_custom_call" | custom-call | tf_op jit(solution)/shard_map/pallas_call | solution.py:328
  320.4 24.3 %shard_map.157 = bf16[768,256]{1,0:T(8,128)(2,1)} custom-call(s32[1]{0:T(128)} %bitcast.28.place_ref, s32[4]{0:T(128)} %constant.147.clone.shift_ref, bf16[768,768]{1,0:T(8,128)(2,1)} %copy-done.2, bf16[4,768,512]{2,1,0:T(8,128)(2,1)} %pad_maximum_fusion.kv_ref, f32[2,768,1]{2,1,0:T(8,128)} %get-tuple-element.8.refs_0_, ...), custom_call_target="tpu_custom_call" | custom-call | tf_op jit(solution)/shard_map/pallas_call | solution.py:328
  346.6 9.5 %collective-permute-done.37 = bf16[768,256]{1,0:T(8,128)(2,1)S(1)} collective-permute-done((bf16[768,256]{1,0:T(8,128)(2,1)}, bf16[768,256]{1,0:T(8,128)(2,1)S(1)}, u32[]{:S(2)}, u32[]{:S(2)}) %collective-permute-start.37) | collective-permute-done | bytes 393248 | tf_op jit(solution)/shard_map/ppermute | solution.py:138
  356.1 8.8 %collective-permute-done.36 = bf16[768,256]{1,0:T(8,128)(2,1)} collective-permute-done((bf16[768,256]{1,0:T(8,128)(2,1)}, bf16[768,256]{1,0:T(8,128)(2,1)}, u32[]{:S(2)}, u32[]{:S(2)}) %collective-permute-start.36) | collective-permute-done | bytes 393248 | tf_op jit(solution)/shard_map/ppermute | solution.py:138
  379.4 10.3 %collective-permute-done.38 = bf16[192,1024]{1,0:T(8,128)(2,1)} collective-permute-done((bf16[192,1024]{1,0:T(8,128)(2,1)}, bf16[192,1024]{1,0:T(8,128)(2,1)}, u32[]{:S(2)}, u32[]{:S(2)}) %collective-permute-start.38) | collective-permute-done | bytes 393248 | tf_op jit(solution)/shard_map/ppermute | solution.py:66
  389.7 6.5 %collective-permute-done.40 = bf16[192,1024]{1,0:T(8,128)(2,1)} collective-permute-done((bf16[192,1024]{1,0:T(8,128)(2,1)}, bf16[192,1024]{1,0:T(8,128)(2,1)}, u32[]{:S(2)}, u32[]{:S(2)}) %collective-permute-start.40) | collective-permute-done | bytes 393248 | tf_op jit(solution)/shard_map/ppermute | solution.py:66
  (183 shorter events, 119.6 us)
Async XLA Ops:
  2.0 35.6 %collective-permute-start.1 = (s32[128,2]{0,1:T(2,128)S(1)}, s32[128,2]{0,1:T(2,128)S(1)}, u32[]{:S(2)}, u32[]{:S(2)}) collective-permute-start(s32[128,2]{0,1:T(2,128)S(1)} %get-tuple-element.34), channel_id=1, source_target_pairs={{0,2},{1,3},{2,0},{3,1},{4,6},{5,7},{6,4},{7,5},{8,10},{9,11},{10,... | collective-permute-start | bytes 3080 | tf_op jit(solution)/shard_map/ppermute | solution.py:50
  5.9 31.7 %collective-permute-start = (s32[128,2]{0,1:T(2,128)S(1)}, s32[128,2]{0,1:T(2,128)S(1)}, u32[]{:S(2)}, u32[]{:S(2)}) collective-permute-start(s32[128,2]{0,1:T(2,128)S(1)} %get-tuple-element.34), channel_id=1, source_target_pairs={{0,3},{1,0},{2,1},{3,2},{4,7},{5,4},{6,5},{7,6},{8,11},{9,8},{10,9... | collective-permute-start | bytes 3080 | tf_op jit(solution)/shard_map/ppermute | solution.py:50
  20.6 17.1 %collective-permute-start.2 = (s32[128,2]{0,1:T(2,128)S(1)}, s32[128,2]{0,1:T(2,128)S(1)}, u32[]{:S(2)}, u32[]{:S(2)}) collective-permute-start(s32[128,2]{0,1:T(2,128)S(1)} %get-tuple-element.34), channel_id=1, source_target_pairs={{0,1},{1,2},{2,3},{3,0},{4,5},{5,6},{6,7},{7,4},{8,9},{9,10},{10,1... | collective-permute-start | bytes 3080 | tf_op jit(solution)/shard_map/ppermute | solution.py:50
  43.7 20.0 %collective-permute-start.11 = (bf16[512,768]{1,0:T(8,128)(2,1)}, bf16[512,768]{1,0:T(8,128)(2,1)S(1)}, u32[]{:S(2)}, u32[]{:S(2)}) collective-permute-start(bf16[512,768]{1,0:T(8,128)(2,1)} %fusion.10), channel_id=1, source_target_pairs={{0,8},{4,12},{8,0},{12,4},{1,9},{5,13},{9,1},{13,5},{2,10},{6,14},... | collective-permute-start | bytes 2359304 | tf_op jit(solution)/shard_map/ppermute | solution.py:138
  45.0 18.6 %collective-permute-start.3 = (s32[2,255]{1,0:T(2,128)S(1)}, s32[2,255]{1,0:T(2,128)S(1)}, u32[]{:S(2)}, u32[]{:S(2)}) collective-permute-start(s32[2,255]{1,0:T(2,128)S(1)} %get-tuple-element.32), channel_id=1, source_target_pairs={{0,16},{16,32},{32,48},{48,64},{64,80},{80,96},{96,112},{1,17},{17... | collective-permute-start | bytes 6128 | tf_op jit(solution)/shard_map/ppermute | solution.py:21
  46.3 17.3 %collective-permute-start.4 = (s32[2,255]{1,0:T(2,128)S(1)}, s32[2,255]{1,0:T(2,128)S(1)}, u32[]{:S(2)}, u32[]{:S(2)}) collective-permute-start(s32[2,255]{1,0:T(2,128)S(1)} %get-tuple-element.33), channel_id=1, source_target_pairs={{16,0},{32,16},{48,32},{64,48},{80,64},{96,80},{112,96},{17,1},{33... | collective-permute-start | bytes 6128 | tf_op jit(solution)/shard_map/ppermute | solution.py:23
  87.7 13.6 %collective-permute-start.15 = (bf16[512,256]{1,0:T(8,128)(2,1)S(1)}, bf16[512,256]{1,0:T(8,128)(2,1)S(1)}, u32[]{:S(2)}, u32[]{:S(2)}) collective-permute-start(bf16[512,256]{1,0:T(8,128)(2,1)S(1)} %copy.23), channel_id=1, source_target_pairs={{0,8},{4,12},{8,0},{12,4},{1,9},{5,13},{9,1},{13,5},{2,10},{6,14},... | collective-permute-start | bytes 786440 | tf_op jit(solution)/shard_map/ppermute | solution.py:138
  89.0 12.4 %collective-permute-start.14 = (bf16[512,256]{1,0:T(8,128)(2,1)S(1)}, bf16[512,256]{1,0:T(8,128)(2,1)}, u32[]{:S(2)}, u32[]{:S(2)}) collective-permute-start(bf16[512,256]{1,0:T(8,128)(2,1)S(1)} %copy.23), channel_id=1, source_target_pairs={{0,4},{4,0},{8,12},{12,8},{1,5},{5,1},{9,13},{13,9},{2,6},{6,2},{1... | collective-permute-start | bytes 786440 | tf_op jit(solution)/shard_map/ppermute | solution.py:138
  126.6 13.9 %collective-permute-start.20 = (bf16[128,1024]{1,0:T(8,128)(2,1)}, bf16[128,1024]{1,0:T(8,128)(2,1)S(1)}, u32[]{:S(2)}, u32[]{:S(2)}) collective-permute-start(bf16[128,1024]{1,0:T(8,128)(2,1)} %fusion.32), channel_id=1, source_target_pairs={{1,0},{2,1},{3,2},{16,3},{17,16},{18,17},{19,18},{32,19},{33,32},{... | collective-permute-start | bytes 786440 | tf_op jit(solution)/shard_map/ppermute | solution.py:33
  147.0 13.7 %collective-permute-start.24 = (bf16[192,1024]{1,0:T(8,128)(2,1)S(1)}, bf16[192,1024]{1,0:T(8,128)(2,1)S(1)}, u32[]{:S(2)}, u32[]{:S(2)}) collective-permute-start(bf16[192,1024]{1,0:T(8,128)(2,1)S(1)} %multiply_convert_fusion.refs_0_), channel_id=1, source_target_pairs={{0,2},{1,3},{2,0},{3,1},{4,6},{5,7},{6,4},{7,5},{8,10},{9,11},{10,... | collective-permute-start | bytes 1179656 | tf_op jit(solution)/shard_map/ppermute | solution.py:162
  147.1 20.1 %collective-permute-start.23 = (bf16[192,1024]{1,0:T(8,128)(2,1)S(1)}, bf16[192,1024]{1,0:T(8,128)(2,1)}, u32[]{:S(2)}, u32[]{:S(2)}) collective-permute-start(bf16[192,1024]{1,0:T(8,128)(2,1)S(1)} %multiply_convert_fusion.refs_0_), channel_id=1, source_target_pairs={{0,1},{1,2},{2,3},{3,0},{4,5},{5,6},{6,7},{7,4},{8,9},{9,10},{10,1... | collective-permute-start | bytes 1179656 | tf_op jit(solution)/shard_map/ppermute | solution.py:162
  184.1 28.1 %collective-permute-start.27 = (bf16[768,768]{1,0:T(8,128)(2,1)S(1)}, bf16[768,768]{1,0:T(8,128)(2,1)S(1)}, u32[]{:S(2)}, u32[]{:S(2)}) collective-permute-start(bf16[768,768]{1,0:T(8,128)(2,1)S(1)} %fusion.2), channel_id=1, source_target_pairs={{0,8},{4,12},{8,0},{12,4},{1,9},{5,13},{9,1},{13,5},{2,10},{6,14},... | collective-permute-start | bytes 3538952 | tf_op jit(solution)/shard_map/ppermute | solution.py:138
  213.8 62.0 %collective-permute-start.33 = (bf16[768,512]{1,0:T(8,128)(2,1)}, bf16[768,512]{1,0:T(8,128)(2,1)S(1)}, u32[]{:S(2)}, u32[]{:S(2)}) collective-permute-start(bf16[768,512]{1,0:T(8,128)(2,1)} %get-tuple-element.19), channel_id=1, source_target_pairs={{0,64},{16,80},{32,96},{48,112},{1,65},{17,81},{33,97},{49,113},{2... | collective-permute-start | bytes 2359304 | tf_op jit(solution)/shard_map/ppermute | solution.py:412
  215.1 62.0 %collective-permute-start.32 = (bf16[768,512]{1,0:T(8,128)(2,1)}, bf16[768,512]{1,0:T(8,128)(2,1)S(1)}, u32[]{:S(2)}, u32[]{:S(2)}) collective-permute-start(bf16[768,512]{1,0:T(8,128)(2,1)} %get-tuple-element.19), channel_id=1, source_target_pairs={{0,32},{16,48},{32,64},{48,80},{64,96},{80,112},{1,33},{17,49},{33... | collective-permute-start | bytes 2359304 | tf_op jit(solution)/shard_map/ppermute | solution.py:412
  216.4 76.1 %collective-permute-start.34 = (bf16[768,512]{1,0:T(8,128)(2,1)}, bf16[768,512]{1,0:T(8,128)(2,1)S(1)}, u32[]{:S(2)}, u32[]{:S(2)}) collective-permute-start(bf16[768,512]{1,0:T(8,128)(2,1)} %get-tuple-element.19), channel_id=1, source_target_pairs={{0,96},{16,112},{1,97},{17,113},{2,98},{18,114},{3,99},{19,115},{4... | collective-permute-start | bytes 2359304 | tf_op jit(solution)/shard_map/ppermute | solution.py:412
  217.7 99.5 %collective-permute-start.31 = (bf16[768,512]{1,0:T(8,128)(2,1)}, bf16[768,512]{1,0:T(8,128)(2,1)}, u32[]{:S(2)}, u32[]{:S(2)}) collective-permute-start(bf16[768,512]{1,0:T(8,128)(2,1)} %get-tuple-element.19), channel_id=1, source_target_pairs={{0,112},{1,113},{2,114},{3,115},{4,116},{5,117},{6,118},{7,119},{8... | collective-permute-start | bytes 2359304 | tf_op jit(solution)/shard_map/ppermute | solution.py:412
  219.0 98.2 %collective-permute-start.30 = (bf16[768,512]{1,0:T(8,128)(2,1)}, bf16[768,512]{1,0:T(8,128)(2,1)}, u32[]{:S(2)}, u32[]{:S(2)}) collective-permute-start(bf16[768,512]{1,0:T(8,128)(2,1)} %get-tuple-element.19), channel_id=1, source_target_pairs={{0,80},{16,96},{32,112},{1,81},{17,97},{33,113},{2,82},{18,98},{34... | collective-permute-start | bytes 2359304 | tf_op jit(solution)/shard_map/ppermute | solution.py:412
  275.7 41.5 %collective-permute-start.29 = (bf16[768,512]{1,0:T(8,128)(2,1)}, bf16[768,512]{1,0:T(8,128)(2,1)}, u32[]{:S(2)}, u32[]{:S(2)}) collective-permute-start(bf16[768,512]{1,0:T(8,128)(2,1)} %get-tuple-element.19), channel_id=1, source_target_pairs={{0,48},{16,64},{32,80},{48,96},{64,112},{1,49},{17,65},{33,81},{49... | collective-permute-start | bytes 2359304 | tf_op jit(solution)/shard_map/ppermute | solution.py:412
  277.0 40.2 %collective-permute-start.28 = (bf16[768,512]{1,0:T(8,128)(2,1)}, bf16[768,512]{1,0:T(8,128)(2,1)}, u32[]{:S(2)}, u32[]{:S(2)}) collective-permute-start(bf16[768,512]{1,0:T(8,128)(2,1)} %get-tuple-element.19), channel_id=1, source_target_pairs={{0,16},{16,32},{32,48},{48,64},{64,80},{80,96},{96,112},{1,17},{17... | collective-permute-start | bytes 2359304 | tf_op jit(solution)/shard_map/ppermute | solution.py:412
  345.6 19.3 %collective-permute-start.36 = (bf16[768,256]{1,0:T(8,128)(2,1)}, bf16[768,256]{1,0:T(8,128)(2,1)}, u32[]{:S(2)}, u32[]{:S(2)}) collective-permute-start(bf16[768,256]{1,0:T(8,128)(2,1)} %shard_map.157), channel_id=1, source_target_pairs={{0,8},{4,12},{8,0},{12,4},{1,9},{5,13},{9,1},{13,5},{2,10},{6,14},... | collective-permute-start | bytes 1179656 | tf_op jit(solution)/shard_map/ppermute | solution.py:138
  346.6 18.4 %collective-permute-start.35 = (bf16[768,256]{1,0:T(8,128)(2,1)}, bf16[768,256]{1,0:T(8,128)(2,1)}, u32[]{:S(2)}, u32[]{:S(2)}) collective-permute-start(bf16[768,256]{1,0:T(8,128)(2,1)} %shard_map.157), channel_id=1, source_target_pairs={{0,4},{4,0},{8,12},{12,8},{1,5},{5,1},{9,13},{13,9},{2,6},{6,2},{1... | collective-permute-start | bytes 1179656 | tf_op jit(solution)/shard_map/ppermute | solution.py:138
  376.1 13.5 %collective-permute-start.38 = (bf16[192,1024]{1,0:T(8,128)(2,1)}, bf16[192,1024]{1,0:T(8,128)(2,1)}, u32[]{:S(2)}, u32[]{:S(2)}) collective-permute-start(bf16[192,1024]{1,0:T(8,128)(2,1)} %get-tuple-element.15), channel_id=1, source_target_pairs={{0,1},{1,2},{2,3},{3,0},{4,5},{5,6},{6,7},{7,4},{8,9},{9,10},{10,1... | collective-permute-start | bytes 1179656 | tf_op jit(solution)/shard_map/ppermute | solution.py:66
  376.1 20.0 %collective-permute-start.40 = (bf16[192,1024]{1,0:T(8,128)(2,1)}, bf16[192,1024]{1,0:T(8,128)(2,1)}, u32[]{:S(2)}, u32[]{:S(2)}) collective-permute-start(bf16[192,1024]{1,0:T(8,128)(2,1)} %get-tuple-element.16), channel_id=1, source_target_pairs={{0,3},{1,0},{2,1},{3,2},{4,7},{5,4},{6,5},{7,6},{8,11},{9,8},{10,9... | collective-permute-start | bytes 1179656 | tf_op jit(solution)/shard_map/ppermute | solution.py:66
  379.4 17.5 %collective-permute-start.39 = (bf16[192,1024]{1,0:T(8,128)(2,1)S(1)}, bf16[192,1024]{1,0:T(8,128)(2,1)}, u32[]{:S(2)}, u32[]{:S(2)}) collective-permute-start(bf16[192,1024]{1,0:T(8,128)(2,1)S(1)} %get-tuple-element.17), channel_id=1, source_target_pairs={{0,2},{1,3},{2,0},{3,1},{4,6},{5,7},{6,4},{7,5},{8,10},{9,11},{10,... | collective-permute-start | bytes 1179656 | tf_op jit(solution)/shard_map/ppermute | solution.py:66
  (36 other events, 702.7 us)
where the time goes:
time: 400 us; the launch traced here: 399 us
  waiting for transfers between devices  208 us (52%)
  Pallas kernels  65.8 us (16%)
  starting transfers between devices  60 us (15%)
  other arithmetic  31.3 us (8%)
  local copies, waits for them, and re-layouts  24 us (6%)
  matrix products  9.45 us (2%)
    ppermute x14, waiting for transfers between devices, flip(): return lax.ppermute(values, axis, [(j, j ^ bit) for j in range(count)])  69.9 us
    ppermute x7, waiting for transfers between devices, per_device(): lax.ppermute(keyvals, 'req', [(j, j + s) for j in range(req_count - s)])  68.9 us
    pallas_call x2, Pallas kernels, causal_attend(): pl.pallas_call(body, grid_spec=grid_spec, out_shape=out_shape)  47.2 us
    ppermute x6, waiting for transfers between devices, scatter_permute(): lax.ppermute(chunk, axis, [(j, (j + s) % count) for j in range(count)])  27.5 us
    ppermute x6, waiting for transfers between devices, received(): lax.ppermute(values, axis, [(j, (j + s) % count) for j in range(count)])  26.3 us
    pallas_call x2, Pallas kernels, head_project(): pl.pallas_call(body, grid_spec=grid_spec, out_shape=jax.ShapeDtypeStruct(...  18.5 us
    ppermute x2, starting transfers between devices, with_halo(): lax.ppermute(head, axis, [((i + 1) % count, i) for i in range(ends)])  12.8 us
    ppermute x2, waiting for transfers between devices, with_halo(): lax.ppermute(tail, axis, [(i, (i + 1) % count) for i in range(ends)])  11.2 us
  transfers between devices with their start and end apart: 41, of which 26 were waited for; matrix products, arithmetic and copies ran while one was open for 4% of the time, Pallas kernels for 8%

commit v1 on v0

--- a/solution.py
+++ b/solution.py
@@ -212,6 +212,7 @@
 
 
 def causal_attend(proj, blocks, shifts, place, carry=None, last=True):
+    diagonal = 0 in shifts
     count = proj.shape[0]
     heads = proj.shape[1] // (3 * HD)
     steps = blocks.shape[0]
@@ -269,15 +270,21 @@
                 peak_ref[h] = new
                 return unused
 
-            lax.fori_loop(0, heads, one, 0)
+            if diagonal:
+                lax.fori_loop(0, heads, one, 0)
+            else:
+                for h in range(heads):
+                    one(h, 0)
 
         @pl.when((shift > 0) & (shift <= own))
         def _():
             fold(False)
 
-        @pl.when(shift == 0)
-        def _():
-            fold(True)
+        if diagonal:
+
+            @pl.when(shift == 0)
+            def _():
+                fold(True)
 
         @pl.when(step == steps - 1)
         def _():

time: 400 us -> 395 us (0.988)
  Pallas kernels: 65.8 us -> 60.6 us
    pallas_call x2, Pallas kernels: 47.2 us -> 42 us  [causal_attend(): pl.pallas_call(body, grid_spec=grid_spec, out_shape=out_shape)]
where the time goes in v1:
time: 395 us; the launch traced here: 394 us
  waiting for transfers between devices  208 us (53%)
  Pallas kernels  60.6 us (15%)
  starting transfers between devices  60 us (15%)
  other arithmetic  31.3 us (8%)
  local copies, waits for them, and re-layouts  24 us (6%)
  matrix products  9.45 us (2%)
    ppermute x14, waiting for transfers between devices, flip(): return lax.ppermute(values, axis, [(j, j ^ bit) for j in range(count)])  69.9 us
    ppermute x7, waiting for transfers between devices, per_device(): lax.ppermute(keyvals, 'req', [(j, j + s) for j in range(req_count - s)])  68.9 us
    pallas_call x2, Pallas kernels, causal_attend(): pl.pallas_call(body, grid_spec=grid_spec, out_shape=out_shape)  42 us
    ppermute x6, waiting for transfers between devices, scatter_permute(): lax.ppermute(chunk, axis, [(j, (j + s) % count) for j in range(count)])  27.5 us
    ppermute x6, waiting for transfers between devices, received(): lax.ppermute(values, axis, [(j, (j + s) % count) for j in range(count)])  26.3 us
    pallas_call x2, Pallas kernels, head_project(): pl.pallas_call(body, grid_spec=grid_spec, out_shape=jax.ShapeDtypeStruct(...  18.5 us
    ppermute x2, starting transfers between devices, with_halo(): lax.ppermute(head, axis, [((i + 1) % count, i) for i in range(ends)])  12.8 us
    ppermute x2, waiting for transfers between devices, with_halo(): lax.ppermute(tail, axis, [(i, (i + 1) % count) for i in range(ends)])  11.2 us
  transfers between devices with their start and end apart: 41, of which 26 were waited for; matrix products, arithmetic and copies ran while one was open for 4% of the time, Pallas kernels for 8%

profile of v1, /device:TPU:28, one launch (start us, length us, event | category | flops | bytes accessed | tf_op | source)
XLA Modules:
  0.0 394.1 jit_solution(18227332847718032168)
XLA Ops:
  15.7 4.8 %collective-permute-done.9.refs_3_ = bf16[128,1024]{1,0:T(8,128)(2,1)S(1)} collective-permute-done((bf16[128,1024]{1,0:T(8,128)(2,1)S(1)}, bf16[128,1024]{1,0:T(8,128)(2,1)S(1)}, u32[]{:S(2)}, u32[]{:S(2)}) %collective-permute-start.9) | collective-permute-done | bytes 262176 | tf_op jit(solution)/shard_map/ppermute | solution.py:162
  26.3 8.5 %shard_map.154 = bf16[4,512,768]{2,1,0:T(8,128)(2,1)} custom-call(s32[2]{0:T(128)} %pad_add_fusion.2.index_ref, bf16[128,1024]{1,0:T(8,128)(2,1)} %copy-done.6, bf16[128,1024]{1,0:T(8,128)(2,1)} %copy-done.15, bf16[128,1024]{1,0:T(8,128)(2,1)} %copy-done.14, bf16[128,1024]{1,0:T(8,128)(2,1)} %copy-done.13, bf16[1024,1024]{1,0:T(8,128)(2,1)} %refs_4_.2, ...), custom_call_target="tpu_custom_call" | custom-call | tf_op jit(solution)/shard_map/pallas_call | solution.py:197
  46.3 6.1 %collective-permute-start.4 = (s32[2,255]{1,0:T(2,128)S(1)}, s32[2,255]{1,0:T(2,128)S(1)}, u32[]{:S(2)}, u32[]{:S(2)}) collective-permute-start(s32[2,255]{1,0:T(2,128)S(1)} %get-tuple-element.33), channel_id=1, source_target_pairs={{16,0},{32,16},{48,32},{64,48},{80,64},{96,80},{112,96},{17,1},{33... | collective-permute-start | bytes 6128 | tf_op jit(solution)/shard_map/ppermute | solution.py:23
  52.4 11.2 %collective-permute-done.3 = s32[2,255]{1,0:T(2,128)S(1)} collective-permute-done((s32[2,255]{1,0:T(2,128)S(1)}, s32[2,255]{1,0:T(2,128)S(1)}, u32[]{:S(2)}, u32[]{:S(2)}) %collective-permute-start.3) | collective-permute-done | bytes 2072 | tf_op jit(solution)/shard_map/ppermute | solution.py:21
  67.6 6.8 %collective-permute-start.13 = (bf16[2,255,256]{2,1,0:T(8,128)(2,1)S(1)}, bf16[2,255,256]{2,1,0:T(8,128)(2,1)}, u32[]{:S(2)}, u32[]{:S(2)}) collective-permute-start(bf16[2,255,256]{2,1,0:T(8,128)(2,1)S(1)} %get-tuple-element.29), channel_id=1, source_target_pairs={{16,0},{32,16},{48,32},{64,48},{80,64},{96,80},{112,96},{17,1},{33... | collective-permute-start | bytes 783368 | tf_op jit(solution)/shard_map/ppermute | solution.py:23
  90.3 6.0 %collective-permute-done.16 = bf16[512,256]{1,0:T(8,128)(2,1)S(1)} collective-permute-done((bf16[512,256]{1,0:T(8,128)(2,1)S(1)}, bf16[512,256]{1,0:T(8,128)(2,1)S(1)}, u32[]{:S(2)}, u32[]{:S(2)}) %collective-permute-start.16) | collective-permute-done | bytes 262176 | tf_op jit(solution)/shard_map/ppermute | solution.py:138
  96.3 5.0 %collective-permute-done.15 = bf16[512,256]{1,0:T(8,128)(2,1)S(1)} collective-permute-done((bf16[512,256]{1,0:T(8,128)(2,1)S(1)}, bf16[512,256]{1,0:T(8,128)(2,1)S(1)}, u32[]{:S(2)}, u32[]{:S(2)}) %collective-permute-start.15) | collective-permute-done | bytes 262176 | tf_op jit(solution)/shard_map/ppermute | solution.py:138
  114.5 5.2 %collective-permute-done.17 = bf16[128,1024]{1,0:T(8,128)(2,1)} collective-permute-done((bf16[128,1024]{1,0:T(8,128)(2,1)}, bf16[128,1024]{1,0:T(8,128)(2,1)}, u32[]{:S(2)}, u32[]{:S(2)}) %collective-permute-start.17) | collective-permute-done | bytes 262176 | tf_op jit(solution)/shard_map/ppermute | solution.py:66
  120.1 4.4 %collective-permute-done.18 = bf16[128,1024]{1,0:T(8,128)(2,1)} collective-permute-done((bf16[128,1024]{1,0:T(8,128)(2,1)}, bf16[128,1024]{1,0:T(8,128)(2,1)}, u32[]{:S(2)}, u32[]{:S(2)}) %collective-permute-start.18) | collective-permute-done | bytes 262176 | tf_op jit(solution)/shard_map/ppermute | solution.py:66
  126.6 8.2 %collective-permute-start.20 = (bf16[128,1024]{1,0:T(8,128)(2,1)}, bf16[128,1024]{1,0:T(8,128)(2,1)S(1)}, u32[]{:S(2)}, u32[]{:S(2)}) collective-permute-start(bf16[128,1024]{1,0:T(8,128)(2,1)} %fusion.32), channel_id=1, source_target_pairs={{1,0},{2,1},{3,2},{16,3},{17,16},{18,17},{19,18},{32,19},{33,32},{... | collective-permute-start | bytes 786440 | tf_op jit(solution)/shard_map/ppermute | solution.py:33
  136.2 4.2 %collective-permute-done.20 = bf16[128,1024]{1,0:T(8,128)(2,1)S(1)} collective-permute-done((bf16[128,1024]{1,0:T(8,128)(2,1)}, bf16[128,1024]{1,0:T(8,128)(2,1)S(1)}, u32[]{:S(2)}, u32[]{:S(2)}) %collective-permute-start.20) | collective-permute-done | bytes 262176 | tf_op jit(solution)/shard_map/ppermute | solution.py:33
  149.0 10.0 %collective-permute-done.25.refs_3_ = bf16[192,1024]{1,0:T(8,128)(2,1)S(1)} collective-permute-done((bf16[192,1024]{1,0:T(8,128)(2,1)S(1)}, bf16[192,1024]{1,0:T(8,128)(2,1)S(1)}, u32[]{:S(2)}, u32[]{:S(2)}) %collective-permute-start.25) | collective-permute-done | bytes 393248 | tf_op jit(solution)/shard_map/ppermute | solution.py:162
  161.4 5.7 %collective-permute-done.23.refs_1_ = bf16[192,1024]{1,0:T(8,128)(2,1)} collective-permute-done((bf16[192,1024]{1,0:T(8,128)(2,1)S(1)}, bf16[192,1024]{1,0:T(8,128)(2,1)}, u32[]{:S(2)}, u32[]{:S(2)}) %collective-permute-start.23) | collective-permute-done | bytes 393248 | tf_op jit(solution)/shard_map/ppermute | solution.py:162
  167.1 10.1 %shard_map.155 = bf16[4,768,768]{2,1,0:T(8,128)(2,1)} custom-call(s32[2]{0:T(128)} %pad_add_fusion.2.index_ref, bf16[192,1024]{1,0:T(8,128)(2,1)} %copy-done.4, bf16[192,1024]{1,0:T(8,128)(2,1)} %collective-permute-done.23.refs_1_, bf16[192,1024]{1,0:T(8,128)(2,1)} %copy-done.10, bf16[192,1024]{1,0:T(8,128)(2,1)} %copy-done.9, bf16[1024,1024]{1,0:T(8,128)(2,1)} %refs_4_.3, ...), custom_call_target="tpu_custom_call" | custom-call | tf_op jit(solution)/shard_map/pallas_call | solution.py:197
  179.3 4.5 %collective-permute-done.26 = bf16[1536,768]{1,0:T(8,128)(2,1)S(1)} collective-permute-done((bf16[1536,768]{1,0:T(8,128)(2,1)S(1)}, bf16[1536,768]{1,0:T(8,128)(2,1)S(1)}, u32[]{:S(2)}, u32[]{:S(2)}) %collective-permute-start.26) | collective-permute-done | bytes 2359328 | tf_op jit(solution)/shard_map/ppermute | solution.py:138
  185.1 27.1 %collective-permute-done.27 = bf16[768,768]{1,0:T(8,128)(2,1)S(1)} collective-permute-done((bf16[768,768]{1,0:T(8,128)(2,1)S(1)}, bf16[768,768]{1,0:T(8,128)(2,1)S(1)}, u32[]{:S(2)}, u32[]{:S(2)}) %collective-permute-start.27) | collective-permute-done | bytes 1179680 | tf_op jit(solution)/shard_map/ppermute | solution.py:138
  220.3 55.5 %collective-permute-done.33 = bf16[768,512]{1,0:T(8,128)(2,1)S(1)} collective-permute-done((bf16[768,512]{1,0:T(8,128)(2,1)}, bf16[768,512]{1,0:T(8,128)(2,1)S(1)}, u32[]{:S(2)}, u32[]{:S(2)}) %collective-permute-start.33) | collective-permute-done | bytes 786464 | tf_op jit(solution)/shard_map/ppermute | solution.py:419
  279.1 13.4 %collective-permute-done.34 = bf16[768,512]{1,0:T(8,128)(2,1)S(1)} collective-permute-done((bf16[768,512]{1,0:T(8,128)(2,1)}, bf16[768,512]{1,0:T(8,128)(2,1)S(1)}, u32[]{:S(2)}, u32[]{:S(2)}) %collective-permute-start.34) | collective-permute-done | bytes 786464 | tf_op jit(solution)/shard_map/ppermute | solution.py:419
  294.3 22.9 %shard_map.156 = (f32[2,768,1]{2,1,0:T(8,128)}, f32[2,768,1]{2,1,0:T(8,128)}, f32[2,768,128]{2,1,0:T(8,128)}) custom-call(s32[1]{0:T(128)} %bitcast.28.place_ref, s32[4]{0:T(128)} %iota_multiply_fusion.shift_ref, bf16[768,768]{1,0:T(8,128)(2,1)} %copy-done.2, bf16[4,768,512]{2,1,0:T(8,128)(2,1)} %pad_maximum_fusion.1.kv_ref), custom_call_target="tpu_custom_call" | custom-call | tf_op jit(solution)/shard_map/pallas_call | solution.py:335
  320.4 19.2 %shard_map.157 = bf16[768,256]{1,0:T(8,128)(2,1)} custom-call(s32[1]{0:T(128)} %bitcast.28.place_ref, s32[4]{0:T(128)} %constant.147.clone.shift_ref, bf16[768,768]{1,0:T(8,128)(2,1)} %copy-done.2, bf16[4,768,512]{2,1,0:T(8,128)(2,1)} %pad_maximum_fusion.kv_ref, f32[2,768,1]{2,1,0:T(8,128)} %get-tuple-element.8.refs_0_, ...), custom_call_target="tpu_custom_call" | custom-call | tf_op jit(solution)/shard_map/pallas_call | solution.py:335
  341.4 9.5 %collective-permute-done.37 = bf16[768,256]{1,0:T(8,128)(2,1)S(1)} collective-permute-done((bf16[768,256]{1,0:T(8,128)(2,1)}, bf16[768,256]{1,0:T(8,128)(2,1)S(1)}, u32[]{:S(2)}, u32[]{:S(2)}) %collective-permute-start.37) | collective-permute-done | bytes 393248 | tf_op jit(solution)/shard_map/ppermute | solution.py:138
  350.9 8.8 %collective-permute-done.36 = bf16[768,256]{1,0:T(8,128)(2,1)} collective-permute-done((bf16[768,256]{1,0:T(8,128)(2,1)}, bf16[768,256]{1,0:T(8,128)(2,1)}, u32[]{:S(2)}, u32[]{:S(2)}) %collective-permute-start.36) | collective-permute-done | bytes 393248 | tf_op jit(solution)/shard_map/ppermute | solution.py:138
  374.2 10.3 %collective-permute-done.38 = bf16[192,1024]{1,0:T(8,128)(2,1)} collective-permute-done((bf16[192,1024]{1,0:T(8,128)(2,1)}, bf16[192,1024]{1,0:T(8,128)(2,1)}, u32[]{:S(2)}, u32[]{:S(2)}) %collective-permute-start.38) | collective-permute-done | bytes 393248 | tf_op jit(solution)/shard_map/ppermute | solution.py:66
  384.5 6.5 %collective-permute-done.40 = bf16[192,1024]{1,0:T(8,128)(2,1)} collective-permute-done((bf16[192,1024]{1,0:T(8,128)(2,1)}, bf16[192,1024]{1,0:T(8,128)(2,1)}, u32[]{:S(2)}, u32[]{:S(2)}) %collective-permute-start.40) | collective-permute-done | bytes 393248 | tf_op jit(solution)/shard_map/ppermute | solution.py:66
  (183 shorter events, 119.6 us)
Async XLA Ops:
  2.0 35.6 %collective-permute-start.1 = (s32[128,2]{0,1:T(2,128)S(1)}, s32[128,2]{0,1:T(2,128)S(1)}, u32[]{:S(2)}, u32[]{:S(2)}) collective-permute-start(s32[128,2]{0,1:T(2,128)S(1)} %get-tuple-element.34), channel_id=1, source_target_pairs={{0,2},{1,3},{2,0},{3,1},{4,6},{5,7},{6,4},{7,5},{8,10},{9,11},{10,... | collective-permute-start | bytes 3080 | tf_op jit(solution)/shard_map/ppermute | solution.py:50
  5.9 31.7 %collective-permute-start = (s32[128,2]{0,1:T(2,128)S(1)}, s32[128,2]{0,1:T(2,128)S(1)}, u32[]{:S(2)}, u32[]{:S(2)}) collective-permute-start(s32[128,2]{0,1:T(2,128)S(1)} %get-tuple-element.34), channel_id=1, source_target_pairs={{0,3},{1,0},{2,1},{3,2},{4,7},{5,4},{6,5},{7,6},{8,11},{9,8},{10,9... | collective-permute-start | bytes 3080 | tf_op jit(solution)/shard_map/ppermute | solution.py:50
  20.6 17.1 %collective-permute-start.2 = (s32[128,2]{0,1:T(2,128)S(1)}, s32[128,2]{0,1:T(2,128)S(1)}, u32[]{:S(2)}, u32[]{:S(2)}) collective-permute-start(s32[128,2]{0,1:T(2,128)S(1)} %get-tuple-element.34), channel_id=1, source_target_pairs={{0,1},{1,2},{2,3},{3,0},{4,5},{5,6},{6,7},{7,4},{8,9},{9,10},{10,1... | collective-permute-start | bytes 3080 | tf_op jit(solution)/shard_map/ppermute | solution.py:50
  43.7 20.0 %collective-permute-start.11 = (bf16[512,768]{1,0:T(8,128)(2,1)}, bf16[512,768]{1,0:T(8,128)(2,1)S(1)}, u32[]{:S(2)}, u32[]{:S(2)}) collective-permute-start(bf16[512,768]{1,0:T(8,128)(2,1)} %fusion.10), channel_id=1, source_target_pairs={{0,8},{4,12},{8,0},{12,4},{1,9},{5,13},{9,1},{13,5},{2,10},{6,14},... | collective-permute-start | bytes 2359304 | tf_op jit(solution)/shard_map/ppermute | solution.py:138
  45.0 18.6 %collective-permute-start.3 = (s32[2,255]{1,0:T(2,128)S(1)}, s32[2,255]{1,0:T(2,128)S(1)}, u32[]{:S(2)}, u32[]{:S(2)}) collective-permute-start(s32[2,255]{1,0:T(2,128)S(1)} %get-tuple-element.32), channel_id=1, source_target_pairs={{0,16},{16,32},{32,48},{48,64},{64,80},{80,96},{96,112},{1,17},{17... | collective-permute-start | bytes 6128 | tf_op jit(solution)/shard_map/ppermute | solution.py:21
  46.3 17.3 %collective-permute-start.4 = (s32[2,255]{1,0:T(2,128)S(1)}, s32[2,255]{1,0:T(2,128)S(1)}, u32[]{:S(2)}, u32[]{:S(2)}) collective-permute-start(s32[2,255]{1,0:T(2,128)S(1)} %get-tuple-element.33), channel_id=1, source_target_pairs={{16,0},{32,16},{48,32},{64,48},{80,64},{96,80},{112,96},{17,1},{33... | collective-permute-start | bytes 6128 | tf_op jit(solution)/shard_map/ppermute | solution.py:23
  87.7 13.6 %collective-permute-start.15 = (bf16[512,256]{1,0:T(8,128)(2,1)S(1)}, bf16[512,256]{1,0:T(8,128)(2,1)S(1)}, u32[]{:S(2)}, u32[]{:S(2)}) collective-permute-start(bf16[512,256]{1,0:T(8,128)(2,1)S(1)} %copy.23), channel_id=1, source_target_pairs={{0,8},{4,12},{8,0},{12,4},{1,9},{5,13},{9,1},{13,5},{2,10},{6,14},... | collective-permute-start | bytes 786440 | tf_op jit(solution)/shard_map/ppermute | solution.py:138
  89.0 12.4 %collective-permute-start.14 = (bf16[512,256]{1,0:T(8,128)(2,1)S(1)}, bf16[512,256]{1,0:T(8,128)(2,1)}, u32[]{:S(2)}, u32[]{:S(2)}) collective-permute-start(bf16[512,256]{1,0:T(8,128)(2,1)S(1)} %copy.23), channel_id=1, source_target_pairs={{0,4},{4,0},{8,12},{12,8},{1,5},{5,1},{9,13},{13,9},{2,6},{6,2},{1... | collective-permute-start | bytes 786440 | tf_op jit(solution)/shard_map/ppermute | solution.py:138
  126.6 13.9 %collective-permute-start.20 = (bf16[128,1024]{1,0:T(8,128)(2,1)}, bf16[128,1024]{1,0:T(8,128)(2,1)S(1)}, u32[]{:S(2)}, u32[]{:S(2)}) collective-permute-start(bf16[128,1024]{1,0:T(8,128)(2,1)} %fusion.32), channel_id=1, source_target_pairs={{1,0},{2,1},{3,2},{16,3},{17,16},{18,17},{19,18},{32,19},{33,32},{... | collective-permute-start | bytes 786440 | tf_op jit(solution)/shard_map/ppermute | solution.py:33
  147.0 13.7 %collective-permute-start.24 = (bf16[192,1024]{1,0:T(8,128)(2,1)S(1)}, bf16[192,1024]{1,0:T(8,128)(2,1)S(1)}, u32[]{:S(2)}, u32[]{:S(2)}) collective-permute-start(bf16[192,1024]{1,0:T(8,128)(2,1)S(1)} %multiply_convert_fusion.refs_0_), channel_id=1, source_target_pairs={{0,2},{1,3},{2,0},{3,1},{4,6},{5,7},{6,4},{7,5},{8,10},{9,11},{10,... | collective-permute-start | bytes 1179656 | tf_op jit(solution)/shard_map/ppermute | solution.py:162
  147.1 20.1 %collective-permute-start.23 = (bf16[192,1024]{1,0:T(8,128)(2,1)S(1)}, bf16[192,1024]{1,0:T(8,128)(2,1)}, u32[]{:S(2)}, u32[]{:S(2)}) collective-permute-start(bf16[192,1024]{1,0:T(8,128)(2,1)S(1)} %multiply_convert_fusion.refs_0_), channel_id=1, source_target_pairs={{0,1},{1,2},{2,3},{3,0},{4,5},{5,6},{6,7},{7,4},{8,9},{9,10},{10,1... | collective-permute-start | bytes 1179656 | tf_op jit(solution)/shard_map/ppermute | solution.py:162
  184.1 28.1 %collective-permute-start.27 = (bf16[768,768]{1,0:T(8,128)(2,1)S(1)}, bf16[768,768]{1,0:T(8,128)(2,1)S(1)}, u32[]{:S(2)}, u32[]{:S(2)}) collective-permute-start(bf16[768,768]{1,0:T(8,128)(2,1)S(1)} %fusion.2), channel_id=1, source_target_pairs={{0,8},{4,12},{8,0},{12,4},{1,9},{5,13},{9,1},{13,5},{2,10},{6,14},... | collective-permute-start | bytes 3538952 | tf_op jit(solution)/shard_map/ppermute | solution.py:138
  213.8 62.0 %collective-permute-start.33 = (bf16[768,512]{1,0:T(8,128)(2,1)}, bf16[768,512]{1,0:T(8,128)(2,1)S(1)}, u32[]{:S(2)}, u32[]{:S(2)}) collective-permute-start(bf16[768,512]{1,0:T(8,128)(2,1)} %get-tuple-element.19), channel_id=1, source_target_pairs={{0,64},{16,80},{32,96},{48,112},{1,65},{17,81},{33,97},{49,113},{2... | collective-permute-start | bytes 2359304 | tf_op jit(solution)/shard_map/ppermute | solution.py:419
  215.1 62.0 %collective-permute-start.32 = (bf16[768,512]{1,0:T(8,128)(2,1)}, bf16[768,512]{1,0:T(8,128)(2,1)S(1)}, u32[]{:S(2)}, u32[]{:S(2)}) collective-permute-start(bf16[768,512]{1,0:T(8,128)(2,1)} %get-tuple-element.19), channel_id=1, source_target_pairs={{0,32},{16,48},{32,64},{48,80},{64,96},{80,112},{1,33},{17,49},{33... | collective-permute-start | bytes 2359304 | tf_op jit(solution)/shard_map/ppermute | solution.py:419
  216.4 76.1 %collective-permute-start.34 = (bf16[768,512]{1,0:T(8,128)(2,1)}, bf16[768,512]{1,0:T(8,128)(2,1)S(1)}, u32[]{:S(2)}, u32[]{:S(2)}) collective-permute-start(bf16[768,512]{1,0:T(8,128)(2,1)} %get-tuple-element.19), channel_id=1, source_target_pairs={{0,96},{16,112},{1,97},{17,113},{2,98},{18,114},{3,99},{19,115},{4... | collective-permute-start | bytes 2359304 | tf_op jit(solution)/shard_map/ppermute | solution.py:419
  217.7 99.5 %collective-permute-start.31 = (bf16[768,512]{1,0:T(8,128)(2,1)}, bf16[768,512]{1,0:T(8,128)(2,1)}, u32[]{:S(2)}, u32[]{:S(2)}) collective-permute-start(bf16[768,512]{1,0:T(8,128)(2,1)} %get-tuple-element.19), channel_id=1, source_target_pairs={{0,112},{1,113},{2,114},{3,115},{4,116},{5,117},{6,118},{7,119},{8... | collective-permute-start | bytes 2359304 | tf_op jit(solution)/shard_map/ppermute | solution.py:419
  219.0 98.2 %collective-permute-start.30 = (bf16[768,512]{1,0:T(8,128)(2,1)}, bf16[768,512]{1,0:T(8,128)(2,1)}, u32[]{:S(2)}, u32[]{:S(2)}) collective-permute-start(bf16[768,512]{1,0:T(8,128)(2,1)} %get-tuple-element.19), channel_id=1, source_target_pairs={{0,80},{16,96},{32,112},{1,81},{17,97},{33,113},{2,82},{18,98},{34... | collective-permute-start | bytes 2359304 | tf_op jit(solution)/shard_map/ppermute | solution.py:419
  275.7 41.5 %collective-permute-start.29 = (bf16[768,512]{1,0:T(8,128)(2,1)}, bf16[768,512]{1,0:T(8,128)(2,1)}, u32[]{:S(2)}, u32[]{:S(2)}) collective-permute-start(bf16[768,512]{1,0:T(8,128)(2,1)} %get-tuple-element.19), channel_id=1, source_target_pairs={{0,48},{16,64},{32,80},{48,96},{64,112},{1,49},{17,65},{33,81},{49... | collective-permute-start | bytes 2359304 | tf_op jit(solution)/shard_map/ppermute | solution.py:419
  277.0 40.2 %collective-permute-start.28 = (bf16[768,512]{1,0:T(8,128)(2,1)}, bf16[768,512]{1,0:T(8,128)(2,1)}, u32[]{:S(2)}, u32[]{:S(2)}) collective-permute-start(bf16[768,512]{1,0:T(8,128)(2,1)} %get-tuple-element.19), channel_id=1, source_target_pairs={{0,16},{16,32},{32,48},{48,64},{64,80},{80,96},{96,112},{1,17},{17... | collective-permute-start | bytes 2359304 | tf_op jit(solution)/shard_map/ppermute | solution.py:419
  340.4 19.3 %collective-permute-start.36 = (bf16[768,256]{1,0:T(8,128)(2,1)}, bf16[768,256]{1,0:T(8,128)(2,1)}, u32[]{:S(2)}, u32[]{:S(2)}) collective-permute-start(bf16[768,256]{1,0:T(8,128)(2,1)} %shard_map.157), channel_id=1, source_target_pairs={{0,8},{4,12},{8,0},{12,4},{1,9},{5,13},{9,1},{13,5},{2,10},{6,14},... | collective-permute-start | bytes 1179656 | tf_op jit(solution)/shard_map/ppermute | solution.py:138
  341.4 18.4 %collective-permute-start.35 = (bf16[768,256]{1,0:T(8,128)(2,1)}, bf16[768,256]{1,0:T(8,128)(2,1)}, u32[]{:S(2)}, u32[]{:S(2)}) collective-permute-start(bf16[768,256]{1,0:T(8,128)(2,1)} %shard_map.157), channel_id=1, source_target_pairs={{0,4},{4,0},{8,12},{12,8},{1,5},{5,1},{9,13},{13,9},{2,6},{6,2},{1... | collective-permute-start | bytes 1179656 | tf_op jit(solution)/shard_map/ppermute | solution.py:138
  370.9 13.5 %collective-permute-start.38 = (bf16[192,1024]{1,0:T(8,128)(2,1)}, bf16[192,1024]{1,0:T(8,128)(2,1)}, u32[]{:S(2)}, u32[]{:S(2)}) collective-permute-start(bf16[192,1024]{1,0:T(8,128)(2,1)} %get-tuple-element.15), channel_id=1, source_target_pairs={{0,1},{1,2},{2,3},{3,0},{4,5},{5,6},{6,7},{7,4},{8,9},{9,10},{10,1... | collective-permute-start | bytes 1179656 | tf_op jit(solution)/shard_map/ppermute | solution.py:66
  370.9 20.0 %collective-permute-start.40 = (bf16[192,1024]{1,0:T(8,128)(2,1)}, bf16[192,1024]{1,0:T(8,128)(2,1)}, u32[]{:S(2)}, u32[]{:S(2)}) collective-permute-start(bf16[192,1024]{1,0:T(8,128)(2,1)} %get-tuple-element.16), channel_id=1, source_target_pairs={{0,3},{1,0},{2,1},{3,2},{4,7},{5,4},{6,5},{7,6},{8,11},{9,8},{10,9... | collective-permute-start | bytes 1179656 | tf_op jit(solution)/shard_map/ppermute | solution.py:66
  374.2 17.5 %collective-permute-start.39 = (bf16[192,1024]{1,0:T(8,128)(2,1)S(1)}, bf16[192,1024]{1,0:T(8,128)(2,1)}, u32[]{:S(2)}, u32[]{:S(2)}) collective-permute-start(bf16[192,1024]{1,0:T(8,128)(2,1)S(1)} %get-tuple-element.17), channel_id=1, source_target_pairs={{0,2},{1,3},{2,0},{3,1},{4,6},{5,7},{6,4},{7,5},{8,10},{9,11},{10,... | collective-permute-start | bytes 1179656 | tf_op jit(solution)/shard_map/ppermute | solution.py:66
  (36 other events, 697.5 us)

commit v2 on v1

--- a/solution.py
+++ b/solution.py
@@ -276,9 +276,11 @@
                 for h in range(heads):
                     one(h, 0)
 
-        @pl.when((shift > 0) & (shift <= own))
-        def _():
-            fold(False)
+        if max(shifts) > 0:
+
+            @pl.when((shift > 0) & (shift <= own))
+            def _():
+                fold(False)
 
         if diagonal:
 
@@ -420,8 +422,8 @@
         for s in range(1, req_count)
     ]
     place = lax.axis_index("req").astype(jnp.int32).reshape(1)
-    near = [s for s in range(0, req_count, 2)]
-    far = [s for s in range(1, req_count, 2)]
+    near = [0]
+    far = list(range(1, req_count))
     state = causal_attend(
         dec_proj, jnp.stack([earlier[s] for s in near]), near, place, last=False
     )

time: 395 us -> 387 us (0.980)
  local copies, waits for them, and re-layouts: 24 us -> 34.5 us
  other arithmetic: 31.3 us -> 25.5 us
  Pallas kernels: 60.6 us -> 56 us
  waiting for transfers between devices: 208 us -> 204 us
    ppermute x7, waiting for transfers between devices: 68.9 us -> 54.4 us  [per_device(): lax.ppermute(keyvals, 'req', [(j, j + s) for j in range(req_count - s)])]
    ppermute x2, waiting for transfers between devices: 0.01 us -> 13.3 us  [with_halo(): lax.ppermute(head, axis, [((i + 1) % count, i) for i in range(ends)])]
    unnamed x44 -> x54, local copies, waits for them, and re-layouts: 3.84 us -> 14.9 us
    another operation x5 -> x2, other arithmetic: 5.85 us -> 0.31 us  [the longest x1 3.19 us: per_device(): jnp.stack([earlier[s] for s in far])]
    ppermute x6, waiting for transfers between devices: 26.3 us -> 21 us  [received(): lax.ppermute(values, axis, [(j, (j + s) % count) for j in range(count)])]
    ppermute x1, starting transfers between devices: 8.23 us -> 3.04 us  [passed_along(): return lax.ppermute(shard, axis, pairs)]
    ppermute x2, starting transfers between devices: 12.8 us -> 8.22 us  [with_halo(): lax.ppermute(head, axis, [((i + 1) % count, i) for i in range(ends)])]
    pallas_call x2, Pallas kernels: 42 us -> 37.5 us  [causal_attend(): pl.pallas_call(body, grid_spec=grid_spec, out_shape=out_shape)]
  transfers between devices with their start and end apart: 41 -> 41, of which waited for: 26 -> 28; matrix products, arithmetic and copies ran while one was open for 4% -> 6% of each run, Pallas kernels for 8% -> 4%
where the time goes in v2:
time: 387 us; the launch traced here: 386 us
  waiting for transfers between devices  204 us (53%)
  starting transfers between devices  56.1 us (14%)
  Pallas kernels  56 us (14%)
  local copies, waits for them, and re-layouts  34.5 us (9%)
  other arithmetic  25.5 us (7%)
  matrix products  9.46 us (2%)
    ppermute x14, waiting for transfers between devices, flip(): return lax.ppermute(values, axis, [(j, j ^ bit) for j in range(count)])  69.7 us
    ppermute x7, waiting for transfers between devices, per_device(): lax.ppermute(keyvals, 'req', [(j, j + s) for j in range(req_count - s)])  54.4 us
    pallas_call x2, Pallas kernels, causal_attend(): pl.pallas_call(body, grid_spec=grid_spec, out_shape=out_shape)  37.5 us
    ppermute x6, waiting for transfers between devices, scatter_permute(): lax.ppermute(chunk, axis, [(j, (j + s) % count) for j in range(count)])  31.6 us
    ppermute x6, waiting for transfers between devices, received(): lax.ppermute(values, axis, [(j, (j + s) % count) for j in range(count)])  21 us
    pallas_call x2, Pallas kernels, head_project(): pl.pallas_call(body, grid_spec=grid_spec, out_shape=jax.ShapeDtypeStruct(...  18.5 us
    unnamed x54, local copies, waits for them, and re-layouts  14.9 us
    ppermute x2, waiting for transfers between devices, with_halo(): lax.ppermute(head, axis, [((i + 1) % count, i) for i in range(ends)])  13.3 us
  transfers between devices with their start and end apart: 41, of which 28 were waited for; matrix products, arithmetic and copies ran while one was open for 6% of the time, Pallas kernels for 4%

profile of v2, /device:TPU:28, one launch (start us, length us, event | category | flops | bytes accessed | tf_op | source)
XLA Modules:
  0.0 386.1 jit_solution(11030907437264239979)
XLA Ops:
  2.0 4.0 %collective-permute-start = (s32[128,2]{0,1:T(2,128)S(1)}, s32[128,2]{0,1:T(2,128)S(1)}, u32[]{:S(2)}, u32[]{:S(2)}) collective-permute-start(s32[128,2]{0,1:T(2,128)S(1)} %get-tuple-element.34), channel_id=1, source_target_pairs={{0,3},{1,0},{2,1},{3,2},{4,7},{5,4},{6,5},{7,6},{8,11},{9,8},{10,9... | collective-permute-start | bytes 3080 | tf_op jit(solution)/shard_map/ppermute | solution.py:50
  26.6 8.5 %shard_map.154 = bf16[4,512,768]{2,1,0:T(8,128)(2,1)} custom-call(s32[2]{0:T(128)} %pad_add_fusion.2.index_ref, bf16[128,1024]{1,0:T(8,128)(2,1)} %copy-done.8, bf16[128,1024]{1,0:T(8,128)(2,1)} %copy-done.15, bf16[128,1024]{1,0:T(8,128)(2,1)} %copy-done.16, bf16[128,1024]{1,0:T(8,128)(2,1)} %copy-done.17, bf16[1024,1024]{1,0:T(8,128)(2,1)} %refs_4_.2, ...), custom_call_target="tpu_custom_call" | custom-call | tf_op jit(solution)/shard_map/pallas_call | solution.py:197
  49.4 13.3 %collective-permute-done.4 = s32[2,255]{1,0:T(2,128)S(1)} collective-permute-done((s32[2,255]{1,0:T(2,128)S(1)}, s32[2,255]{1,0:T(2,128)S(1)}, u32[]{:S(2)}, u32[]{:S(2)}) %collective-permute-start.4) | collective-permute-done | bytes 2072 | tf_op jit(solution)/shard_map/ppermute | solution.py:23
  66.6 5.5 %collective-permute-start.13 = (bf16[2,255,256]{2,1,0:T(8,128)(2,1)}, bf16[2,255,256]{2,1,0:T(8,128)(2,1)}, u32[]{:S(2)}, u32[]{:S(2)}) collective-permute-start(bf16[2,255,256]{2,1,0:T(8,128)(2,1)} %get-tuple-element.29), channel_id=1, source_target_pairs={{16,0},{32,16},{48,32},{64,48},{80,64},{96,80},{112,96},{17,1},{33... | collective-permute-start | bytes 783368 | tf_op jit(solution)/shard_map/ppermute | solution.py:23
  77.3 6.7 %collective-permute-done.12 = bf16[2,255,256]{2,1,0:T(8,128)(2,1)} collective-permute-done((bf16[2,255,256]{2,1,0:T(8,128)(2,1)S(1)}, bf16[2,255,256]{2,1,0:T(8,128)(2,1)}, u32[]{:S(2)}, u32[]{:S(2)}) %collective-permute-start.12) | collective-permute-done | bytes 261152 | tf_op jit(solution)/shard_map/ppermute | solution.py:21
  94.2 6.0 %collective-permute-done.16 = bf16[512,256]{1,0:T(8,128)(2,1)S(1)} collective-permute-done((bf16[512,256]{1,0:T(8,128)(2,1)S(1)}, bf16[512,256]{1,0:T(8,128)(2,1)S(1)}, u32[]{:S(2)}, u32[]{:S(2)}) %collective-permute-start.16) | collective-permute-done | bytes 262176 | tf_op jit(solution)/shard_map/ppermute | solution.py:138
  100.2 5.0 %collective-permute-done.15 = bf16[512,256]{1,0:T(8,128)(2,1)S(1)} collective-permute-done((bf16[512,256]{1,0:T(8,128)(2,1)S(1)}, bf16[512,256]{1,0:T(8,128)(2,1)S(1)}, u32[]{:S(2)}, u32[]{:S(2)}) %collective-permute-start.15) | collective-permute-done | bytes 262176 | tf_op jit(solution)/shard_map/ppermute | solution.py:138
  118.6 8.4 %collective-permute-done.19 = bf16[128,1024]{1,0:T(8,128)(2,1)} collective-permute-done((bf16[128,1024]{1,0:T(8,128)(2,1)}, bf16[128,1024]{1,0:T(8,128)(2,1)}, u32[]{:S(2)}, u32[]{:S(2)}) %collective-permute-start.19) | collective-permute-done | bytes 262176 | tf_op jit(solution)/shard_map/ppermute | solution.py:66
  127.1 3.7 collective-permute-done.17
  137.2 5.9 %collective-permute-done.20 = bf16[128,1024]{1,0:T(8,128)(2,1)S(1)} collective-permute-done((bf16[128,1024]{1,0:T(8,128)(2,1)}, bf16[128,1024]{1,0:T(8,128)(2,1)S(1)}, u32[]{:S(2)}, u32[]{:S(2)}) %collective-permute-start.20) | collective-permute-done | bytes 262176 | tf_op jit(solution)/shard_map/ppermute | solution.py:33
  153.7 15.6 %collective-permute-done.23.refs_1_ = bf16[192,1024]{1,0:T(8,128)(2,1)S(1)} collective-permute-done((bf16[192,1024]{1,0:T(8,128)(2,1)S(1)}, bf16[192,1024]{1,0:T(8,128)(2,1)S(1)}, u32[]{:S(2)}, u32[]{:S(2)}) %collective-permute-start.23) | collective-permute-done | bytes 393248 | tf_op jit(solution)/shard_map/ppermute | solution.py:162
  170.2 10.1 %shard_map.155 = bf16[4,768,768]{2,1,0:T(8,128)(2,1)} custom-call(s32[2]{0:T(128)} %pad_add_fusion.2.index_ref, bf16[192,1024]{1,0:T(8,128)(2,1)} %copy-done.6, bf16[192,1024]{1,0:T(8,128)(2,1)} %copy-done.11, bf16[192,1024]{1,0:T(8,128)(2,1)} %copy-done.12, bf16[192,1024]{1,0:T(8,128)(2,1)} %collective-permute-done.25.refs_3_, bf16[1024,1024]{1,0:T(8,128)(2,1)} %refs_4_.3, ...), custom_call_target="tpu_custom_call" | custom-call | tf_op jit(solution)/shard_map/pallas_call | solution.py:197
  182.4 4.5 %collective-permute-done.26 = bf16[1536,768]{1,0:T(8,128)(2,1)S(1)} collective-permute-done((bf16[1536,768]{1,0:T(8,128)(2,1)S(1)}, bf16[1536,768]{1,0:T(8,128)(2,1)S(1)}, u32[]{:S(2)}, u32[]{:S(2)}) %collective-permute-start.26) | collective-permute-done | bytes 2359328 | tf_op jit(solution)/shard_map/ppermute | solution.py:138
  188.2 27.1 %collective-permute-done.27 = bf16[768,768]{1,0:T(8,128)(2,1)S(1)} collective-permute-done((bf16[768,768]{1,0:T(8,128)(2,1)S(1)}, bf16[768,768]{1,0:T(8,128)(2,1)S(1)}, u32[]{:S(2)}, u32[]{:S(2)}) %collective-permute-start.27) | collective-permute-done | bytes 1179680 | tf_op jit(solution)/shard_map/ppermute | solution.py:138
  223.7 6.9 %shard_map.156 = (f32[2,768,1]{2,1,0:T(8,128)}, f32[2,768,1]{2,1,0:T(8,128)}, f32[2,768,128]{2,1,0:T(8,128)}) custom-call(s32[1]{0:T(128)} %bitcast.28.place_ref, s32[1]{0:T(128)} %constant.145.clone.shift_ref, bf16[768,768]{1,0:T(8,128)(2,1)} %copy-done.2, bf16[1,768,512]{2,1,0:T(8,128)(2,1)} %get-tuple-element.18.kv_ref), custom_call_target="tpu_custom_call" | custom-call | tf_op jit(solution)/shard_map/pallas_call | solution.py:337
  230.6 9.1 %collective-permute-done.28 = bf16[768,512]{1,0:T(8,128)(2,1)} collective-permute-done((bf16[768,512]{1,0:T(8,128)(2,1)}, bf16[768,512]{1,0:T(8,128)(2,1)}, u32[]{:S(2)}, u32[]{:S(2)}) %collective-permute-start.28) | collective-permute-done | bytes 786464 | tf_op jit(solution)/shard_map/ppermute | solution.py:421
  243.1 16.5 %collective-permute-done.29 = bf16[768,512]{1,0:T(8,128)(2,1)} collective-permute-done((bf16[768,512]{1,0:T(8,128)(2,1)}, bf16[768,512]{1,0:T(8,128)(2,1)}, u32[]{:S(2)}, u32[]{:S(2)}) %collective-permute-start.29) | collective-permute-done | bytes 786464 | tf_op jit(solution)/shard_map/ppermute | solution.py:421
  267.3 9.2 %collective-permute-done.32 = bf16[768,512]{1,0:T(8,128)(2,1)} collective-permute-done((bf16[768,512]{1,0:T(8,128)(2,1)}, bf16[768,512]{1,0:T(8,128)(2,1)}, u32[]{:S(2)}, u32[]{:S(2)}) %collective-permute-start.32) | collective-permute-done | bytes 786464 | tf_op jit(solution)/shard_map/ppermute | solution.py:421
  278.5 19.6 %collective-permute-done.33 = bf16[768,512]{1,0:T(8,128)(2,1)S(1)} collective-permute-done((bf16[768,512]{1,0:T(8,128)(2,1)}, bf16[768,512]{1,0:T(8,128)(2,1)S(1)}, u32[]{:S(2)}, u32[]{:S(2)}) %collective-permute-start.33) | collective-permute-done | bytes 786464 | tf_op jit(solution)/shard_map/ppermute | solution.py:421
  300.1 30.6 %shard_map.157 = bf16[768,256]{1,0:T(8,128)(2,1)} custom-call(s32[1]{0:T(128)} %bitcast.28.place_ref, s32[7]{0:T(128)} %constant.146.clone.shift_ref, bf16[768,768]{1,0:T(8,128)(2,1)} %copy-done.2, bf16[7,768,512]{2,1,0:T(8,128)(2,1)} %bitcast_dynamic-update-slice_fusion.kv_ref, f32[2,768,1]{2,1,0:T(8,128)} %get-tuple-element.8.refs_0_, ...), custom_call_target="tpu_custom_call" | custom-call | tf_op jit(solution)/shard_map/pallas_call | solution.py:337
  332.6 9.5 %collective-permute-done.37 = bf16[768,256]{1,0:T(8,128)(2,1)S(1)} collective-permute-done((bf16[768,256]{1,0:T(8,128)(2,1)}, bf16[768,256]{1,0:T(8,128)(2,1)S(1)}, u32[]{:S(2)}, u32[]{:S(2)}) %collective-permute-start.37) | collective-permute-done | bytes 393248 | tf_op jit(solution)/shard_map/ppermute | solution.py:138
  342.1 8.7 %collective-permute-done.36 = bf16[768,256]{1,0:T(8,128)(2,1)S(1)} collective-permute-done((bf16[768,256]{1,0:T(8,128)(2,1)}, bf16[768,256]{1,0:T(8,128)(2,1)S(1)}, u32[]{:S(2)}, u32[]{:S(2)}) %collective-permute-start.36) | collective-permute-done | bytes 393248 | tf_op jit(solution)/shard_map/ppermute | solution.py:138
  364.2 9.8 %collective-permute-done.40 = bf16[192,1024]{1,0:T(8,128)(2,1)} collective-permute-done((bf16[192,1024]{1,0:T(8,128)(2,1)}, bf16[192,1024]{1,0:T(8,128)(2,1)}, u32[]{:S(2)}, u32[]{:S(2)}) %collective-permute-start.40) | collective-permute-done | bytes 393248 | tf_op jit(solution)/shard_map/ppermute | solution.py:66
  377.2 6.5 %collective-permute-done.38 = bf16[192,1024]{1,0:T(8,128)(2,1)} collective-permute-done((bf16[192,1024]{1,0:T(8,128)(2,1)S(1)}, bf16[192,1024]{1,0:T(8,128)(2,1)}, u32[]{:S(2)}, u32[]{:S(2)}) %collective-permute-start.38) | collective-permute-done | bytes 393248 | tf_op jit(solution)/shard_map/ppermute | solution.py:66
  (191 shorter events, 134.7 us)
Async XLA Ops:
  2.0 35.9 %collective-permute-start = (s32[128,2]{0,1:T(2,128)S(1)}, s32[128,2]{0,1:T(2,128)S(1)}, u32[]{:S(2)}, u32[]{:S(2)}) collective-permute-start(s32[128,2]{0,1:T(2,128)S(1)} %get-tuple-element.34), channel_id=1, source_target_pairs={{0,3},{1,0},{2,1},{3,2},{4,7},{5,4},{6,5},{7,6},{8,11},{9,8},{10,9... | collective-permute-start | bytes 3080 | tf_op jit(solution)/shard_map/ppermute | solution.py:50
  6.0 31.9 %collective-permute-start.1 = (s32[128,2]{0,1:T(2,128)S(1)}, s32[128,2]{0,1:T(2,128)S(1)}, u32[]{:S(2)}, u32[]{:S(2)}) collective-permute-start(s32[128,2]{0,1:T(2,128)S(1)} %get-tuple-element.34), channel_id=1, source_target_pairs={{0,2},{1,3},{2,0},{3,1},{4,6},{5,7},{6,4},{7,5},{8,10},{9,11},{10,... | collective-permute-start | bytes 3080 | tf_op jit(solution)/shard_map/ppermute | solution.py:50
  21.1 16.9 %collective-permute-start.2 = (s32[128,2]{0,1:T(2,128)S(1)}, s32[128,2]{0,1:T(2,128)S(1)}, u32[]{:S(2)}, u32[]{:S(2)}) collective-permute-start(s32[128,2]{0,1:T(2,128)S(1)} %get-tuple-element.34), channel_id=1, source_target_pairs={{0,1},{1,2},{2,3},{3,0},{4,5},{5,6},{6,7},{7,4},{8,9},{9,10},{10,1... | collective-permute-start | bytes 3080 | tf_op jit(solution)/shard_map/ppermute | solution.py:50
  44.0 20.0 %collective-permute-start.11 = (bf16[512,768]{1,0:T(8,128)(2,1)}, bf16[512,768]{1,0:T(8,128)(2,1)S(1)}, u32[]{:S(2)}, u32[]{:S(2)}) collective-permute-start(bf16[512,768]{1,0:T(8,128)(2,1)} %fusion.10), channel_id=1, source_target_pairs={{0,8},{4,12},{8,0},{12,4},{1,9},{5,13},{9,1},{13,5},{2,10},{6,14},... | collective-permute-start | bytes 2359304 | tf_op jit(solution)/shard_map/ppermute | solution.py:138
  45.3 17.4 %collective-permute-start.4 = (s32[2,255]{1,0:T(2,128)S(1)}, s32[2,255]{1,0:T(2,128)S(1)}, u32[]{:S(2)}, u32[]{:S(2)}) collective-permute-start(s32[2,255]{1,0:T(2,128)S(1)} %get-tuple-element.33), channel_id=1, source_target_pairs={{16,0},{32,16},{48,32},{64,48},{80,64},{96,80},{112,96},{17,1},{33... | collective-permute-start | bytes 6128 | tf_op jit(solution)/shard_map/ppermute | solution.py:23
  48.0 15.9 %collective-permute-start.3 = (s32[2,255]{1,0:T(2,128)S(1)}, s32[2,255]{1,0:T(2,128)S(1)}, u32[]{:S(2)}, u32[]{:S(2)}) collective-permute-start(s32[2,255]{1,0:T(2,128)S(1)} %get-tuple-element.32), channel_id=1, source_target_pairs={{0,16},{16,32},{32,48},{48,64},{64,80},{80,96},{96,112},{1,17},{17... | collective-permute-start | bytes 6128 | tf_op jit(solution)/shard_map/ppermute | solution.py:21
  91.6 13.5 %collective-permute-start.15 = (bf16[512,256]{1,0:T(8,128)(2,1)S(1)}, bf16[512,256]{1,0:T(8,128)(2,1)S(1)}, u32[]{:S(2)}, u32[]{:S(2)}) collective-permute-start(bf16[512,256]{1,0:T(8,128)(2,1)S(1)} %copy.23), channel_id=1, source_target_pairs={{0,8},{4,12},{8,0},{12,4},{1,9},{5,13},{9,1},{13,5},{2,10},{6,14},... | collective-permute-start | bytes 786440 | tf_op jit(solution)/shard_map/ppermute | solution.py:138
  112.9 14.2 %collective-permute-start.19 = (bf16[128,1024]{1,0:T(8,128)(2,1)}, bf16[128,1024]{1,0:T(8,128)(2,1)}, u32[]{:S(2)}, u32[]{:S(2)}) collective-permute-start(bf16[128,1024]{1,0:T(8,128)(2,1)} %get-tuple-element.21), channel_id=1, source_target_pairs={{0,3},{1,0},{2,1},{3,2},{4,7},{5,4},{6,5},{7,6},{8,11},{9,8},{10,9... | collective-permute-start | bytes 786440 | tf_op jit(solution)/shard_map/ppermute | solution.py:66
  116.6 14.1 %collective-permute-start.17 = (bf16[128,1024]{1,0:T(8,128)(2,1)}, bf16[128,1024]{1,0:T(8,128)(2,1)}, u32[]{:S(2)}, u32[]{:S(2)}) collective-permute-start(bf16[128,1024]{1,0:T(8,128)(2,1)} %get-tuple-element.20), channel_id=1, source_target_pairs={{0,1},{1,2},{2,3},{3,0},{4,5},{5,6},{6,7},{7,4},{8,9},{9,10},{10,1... | collective-permute-start | bytes 786440 | tf_op jit(solution)/shard_map/ppermute | solution.py:66
  149.5 19.8 %collective-permute-start.23 = (bf16[192,1024]{1,0:T(8,128)(2,1)S(1)}, bf16[192,1024]{1,0:T(8,128)(2,1)S(1)}, u32[]{:S(2)}, u32[]{:S(2)}) collective-permute-start(bf16[192,1024]{1,0:T(8,128)(2,1)S(1)} %multiply_convert_fusion.refs_0_), channel_id=1, source_target_pairs={{0,1},{1,2},{2,3},{3,0},{4,5},{5,6},{6,7},{7,4},{8,9},{9,10},{10,1... | collective-permute-start | bytes 1179656 | tf_op jit(solution)/shard_map/ppermute | solution.py:162
  149.6 19.7 %collective-permute-start.24 = (bf16[192,1024]{1,0:T(8,128)(2,1)S(1)}, bf16[192,1024]{1,0:T(8,128)(2,1)S(1)}, u32[]{:S(2)}, u32[]{:S(2)}) collective-permute-start(bf16[192,1024]{1,0:T(8,128)(2,1)S(1)} %multiply_convert_fusion.refs_0_), channel_id=1, source_target_pairs={{0,2},{1,3},{2,0},{3,1},{4,6},{5,7},{6,4},{7,5},{8,10},{9,11},{10,... | collective-permute-start | bytes 1179656 | tf_op jit(solution)/shard_map/ppermute | solution.py:162
  151.1 18.9 %collective-permute-start.25 = (bf16[192,1024]{1,0:T(8,128)(2,1)S(1)}, bf16[192,1024]{1,0:T(8,128)(2,1)}, u32[]{:S(2)}, u32[]{:S(2)}) collective-permute-start(bf16[192,1024]{1,0:T(8,128)(2,1)S(1)} %multiply_convert_fusion.refs_0_), channel_id=1, source_target_pairs={{0,3},{1,0},{2,1},{3,2},{4,7},{5,4},{6,5},{7,6},{8,11},{9,8},{10,9... | collective-permute-start | bytes 1179656 | tf_op jit(solution)/shard_map/ppermute | solution.py:162
  187.2 28.1 %collective-permute-start.27 = (bf16[768,768]{1,0:T(8,128)(2,1)S(1)}, bf16[768,768]{1,0:T(8,128)(2,1)S(1)}, u32[]{:S(2)}, u32[]{:S(2)}) collective-permute-start(bf16[768,768]{1,0:T(8,128)(2,1)S(1)} %fusion.2), channel_id=1, source_target_pairs={{0,8},{4,12},{8,0},{12,4},{1,9},{5,13},{9,1},{13,5},{2,10},{6,14},... | collective-permute-start | bytes 3538952 | tf_op jit(solution)/shard_map/ppermute | solution.py:138
  217.2 22.5 %collective-permute-start.28 = (bf16[768,512]{1,0:T(8,128)(2,1)}, bf16[768,512]{1,0:T(8,128)(2,1)}, u32[]{:S(2)}, u32[]{:S(2)}) collective-permute-start(bf16[768,512]{1,0:T(8,128)(2,1)} %get-tuple-element.19), channel_id=1, source_target_pairs={{0,16},{16,32},{32,48},{48,64},{64,80},{80,96},{96,112},{1,17},{17... | collective-permute-start | bytes 2359304 | tf_op jit(solution)/shard_map/ppermute | solution.py:421
  218.5 41.0 %collective-permute-start.29 = (bf16[768,512]{1,0:T(8,128)(2,1)}, bf16[768,512]{1,0:T(8,128)(2,1)}, u32[]{:S(2)}, u32[]{:S(2)}) collective-permute-start(bf16[768,512]{1,0:T(8,128)(2,1)} %get-tuple-element.19), channel_id=1, source_target_pairs={{0,32},{16,48},{32,64},{48,80},{64,96},{80,112},{1,33},{17,49},{33... | collective-permute-start | bytes 2359304 | tf_op jit(solution)/shard_map/ppermute | solution.py:421
  219.8 43.3 %collective-permute-start.30 = (bf16[768,512]{1,0:T(8,128)(2,1)}, bf16[768,512]{1,0:T(8,128)(2,1)}, u32[]{:S(2)}, u32[]{:S(2)}) collective-permute-start(bf16[768,512]{1,0:T(8,128)(2,1)} %get-tuple-element.19), channel_id=1, source_target_pairs={{0,48},{16,64},{32,80},{48,96},{64,112},{1,49},{17,65},{33,81},{49... | collective-permute-start | bytes 2359304 | tf_op jit(solution)/shard_map/ppermute | solution.py:421
  221.1 44.1 %collective-permute-start.31 = (bf16[768,512]{1,0:T(8,128)(2,1)}, bf16[768,512]{1,0:T(8,128)(2,1)}, u32[]{:S(2)}, u32[]{:S(2)}) collective-permute-start(bf16[768,512]{1,0:T(8,128)(2,1)} %get-tuple-element.19), channel_id=1, source_target_pairs={{0,64},{16,80},{32,96},{48,112},{1,65},{17,81},{33,97},{49,113},{2... | collective-permute-start | bytes 2359304 | tf_op jit(solution)/shard_map/ppermute | solution.py:421
  222.4 54.1 %collective-permute-start.32 = (bf16[768,512]{1,0:T(8,128)(2,1)}, bf16[768,512]{1,0:T(8,128)(2,1)}, u32[]{:S(2)}, u32[]{:S(2)}) collective-permute-start(bf16[768,512]{1,0:T(8,128)(2,1)} %get-tuple-element.19), channel_id=1, source_target_pairs={{0,80},{16,96},{32,112},{1,81},{17,97},{33,113},{2,82},{18,98},{34... | collective-permute-start | bytes 2359304 | tf_op jit(solution)/shard_map/ppermute | solution.py:421
  239.7 58.5 %collective-permute-start.33 = (bf16[768,512]{1,0:T(8,128)(2,1)}, bf16[768,512]{1,0:T(8,128)(2,1)S(1)}, u32[]{:S(2)}, u32[]{:S(2)}) collective-permute-start(bf16[768,512]{1,0:T(8,128)(2,1)} %get-tuple-element.19), channel_id=1, source_target_pairs={{0,96},{16,112},{1,97},{17,113},{2,98},{18,114},{3,99},{19,115},{4... | collective-permute-start | bytes 2359304 | tf_op jit(solution)/shard_map/ppermute | solution.py:421
  259.6 39.6 %collective-permute-start.34 = (bf16[768,512]{1,0:T(8,128)(2,1)}, bf16[768,512]{1,0:T(8,128)(2,1)S(1)}, u32[]{:S(2)}, u32[]{:S(2)}) collective-permute-start(bf16[768,512]{1,0:T(8,128)(2,1)} %get-tuple-element.19), channel_id=1, source_target_pairs={{0,112},{1,113},{2,114},{3,115},{4,116},{5,117},{6,118},{7,119},{8... | collective-permute-start | bytes 2359304 | tf_op jit(solution)/shard_map/ppermute | solution.py:421
  331.6 19.2 %collective-permute-start.36 = (bf16[768,256]{1,0:T(8,128)(2,1)}, bf16[768,256]{1,0:T(8,128)(2,1)S(1)}, u32[]{:S(2)}, u32[]{:S(2)}) collective-permute-start(bf16[768,256]{1,0:T(8,128)(2,1)} %shard_map.157), channel_id=1, source_target_pairs={{0,8},{4,12},{8,0},{12,4},{1,9},{5,13},{9,1},{13,5},{2,10},{6,14},... | collective-permute-start | bytes 1179656 | tf_op jit(solution)/shard_map/ppermute | solution.py:138
  332.4 18.4 %collective-permute-start.35 = (bf16[768,256]{1,0:T(8,128)(2,1)}, bf16[768,256]{1,0:T(8,128)(2,1)S(1)}, u32[]{:S(2)}, u32[]{:S(2)}) collective-permute-start(bf16[768,256]{1,0:T(8,128)(2,1)} %shard_map.157), channel_id=1, source_target_pairs={{0,4},{4,0},{8,12},{12,8},{1,5},{5,1},{9,13},{13,9},{2,6},{6,2},{1... | collective-permute-start | bytes 1179656 | tf_op jit(solution)/shard_map/ppermute | solution.py:138
  363.4 13.9 %collective-permute-start.39 = (bf16[192,1024]{1,0:T(8,128)(2,1)}, bf16[192,1024]{1,0:T(8,128)(2,1)}, u32[]{:S(2)}, u32[]{:S(2)}) collective-permute-start(bf16[192,1024]{1,0:T(8,128)(2,1)} %get-tuple-element.17), channel_id=1, source_target_pairs={{0,2},{1,3},{2,0},{3,1},{4,6},{5,7},{6,4},{7,5},{8,10},{9,11},{10,... | collective-permute-start | bytes 1179656 | tf_op jit(solution)/shard_map/ppermute | solution.py:66
  363.6 20.1 %collective-permute-start.38 = (bf16[192,1024]{1,0:T(8,128)(2,1)S(1)}, bf16[192,1024]{1,0:T(8,128)(2,1)}, u32[]{:S(2)}, u32[]{:S(2)}) collective-permute-start(bf16[192,1024]{1,0:T(8,128)(2,1)S(1)} %get-tuple-element.15), channel_id=1, source_target_pairs={{0,1},{1,2},{2,3},{3,0},{4,5},{5,6},{6,7},{7,4},{8,9},{9,10},{10,1... | collective-permute-start | bytes 1179656 | tf_op jit(solution)/shard_map/ppermute | solution.py:66
  (38 other events, 645.7 us)

commit v3 on v2

--- a/solution.py
+++ b/solution.py
@@ -364,7 +364,6 @@
     margin = MAXIMG - 1
     piece_ids = gather_permute(jnp.stack([vis_segment, vis_valid], axis=1), "col").T
     piece_len = piece_ids.shape[1]
-    framed_ids = with_halo(piece_ids, (("req", 1),), margin)
     total_slots = piece_len * lax.axis_size("req")
     prompt_rows = text_embed.shape[0]
     prompt_total = prompt_rows * lax.axis_size("req") * col_count
@@ -373,16 +372,19 @@
     window_index = jnp.arange(window_len, dtype=jnp.int32)
     key_slots = window_start + window_index
     inside = (key_slots >= 0) & (key_slots < total_slots)
-    key_segment = framed_ids[0]
-    key_valid = framed_ids[1]
+    vis_cols = received(norm_local(vis_embed, vis_gain), "col")
+    vis_proj = head_project(vis_cols, (vis_wq, vis_wk, vis_wv), "col")
+    id_plane = jnp.concatenate(
+        [piece_ids.T.astype(jnp.bfloat16), jnp.zeros((piece_len, local - 2), jnp.bfloat16)], axis=1
+    )
+    vis_pairs = jnp.stack([vis_proj[:, local : 2 * local], vis_proj[:, 2 * local :], id_plane])
+    framed = with_halo(vis_pairs, (("req", 1),), margin)
+    key_segment = framed[2, :, 0].astype(jnp.int32)
+    key_valid = framed[2, :, 1].astype(jnp.int32)
     begins = jnp.concatenate([jnp.ones((1,), jnp.bool_), key_segment[1:] != key_segment[:-1]])
     begins = begins | (key_slots == 0)
     image_first = lax.cummax(jnp.where(begins, key_slots, window_start), axis=0)
     target_window = image_first * prompt_total // total_slots + key_slots - image_first
-    vis_cols = received(norm_local(vis_embed, vis_gain), "col")
-    vis_proj = head_project(vis_cols, (vis_wq, vis_wk, vis_wv), "col")
-    vis_pairs = jnp.stack([vis_proj[:, local : 2 * local], vis_proj[:, 2 * local :]])
-    framed = with_halo(vis_pairs, (("req", 1),), margin)
     query_local = margin + jnp.arange(piece_len, dtype=jnp.int32)
     query_slots = window_start + query_local
     query_segment = key_segment[query_local]

time: 387 us -> 403 us (1.041)
  waiting for transfers between devices: 204 us -> 222 us
  starting transfers between devices: 56.1 us -> 43.6 us
    ppermute x14, waiting for transfers between devices: 69.7 us -> 84.9 us  [flip(): return lax.ppermute(values, axis, [(j, j ^ bit) for j in range(count)])]
    ppermute x2 -> x1, waiting for transfers between devices: 13.3 us -> 5.38 us  [with_halo(): lax.ppermute(head, axis, [((i + 1) % count, i) for i in range(ends)])]
    ppermute x2 -> x1, starting transfers between devices: 8.22 us -> 2.43 us  [with_halo(): lax.ppermute(head, axis, [((i + 1) % count, i) for i in range(ends)])]
    ppermute x6, waiting for transfers between devices: 21 us -> 25.5 us  [received(): lax.ppermute(values, axis, [(j, (j + s) % count) for j in range(count)])]
    ppermute x3, starting transfers between devices: 7.35 us -> 3.05 us  [gather_permute(): lax.ppermute(values, axis, [(j, (j + s) % count) for j in range(count)])]
    ppermute x2 -> x1, waiting for transfers between devices: 7.91 us -> 11.3 us  [with_halo(): lax.ppermute(tail, axis, [(i, (i + 1) % count) for i in range(ends)])]
    unnamed x54 -> x55, local copies, waits for them, and re-layouts: 14.9 us -> 15.8 us
  transfers between devices with their start and end apart: 41 -> 39, of which waited for: 28 -> 30; matrix products, arithmetic and copies ran while one was open for 6% -> 5% of each run, Pallas kernels for 4% -> 2%
where the time goes in v3:
time: 403 us; the launch traced here: 401 us
  waiting for transfers between devices  222 us (55%)
  Pallas kernels  56.1 us (14%)
  starting transfers between devices  43.6 us (11%)
  local copies, waits for them, and re-layouts  38.1 us (9%)
  other arithmetic  29.4 us (7%)
  matrix products  11.4 us (3%)
    ppermute x14, waiting for transfers between devices, flip(): return lax.ppermute(values, axis, [(j, j ^ bit) for j in range(count)])  84.9 us
    ppermute x7, waiting for transfers between devices, per_device(): lax.ppermute(keyvals, 'req', [(j, j + s) for j in range(req_count - s)])  54.2 us
    pallas_call x2, Pallas kernels, causal_attend(): pl.pallas_call(body, grid_spec=grid_spec, out_shape=out_shape)  37.5 us
    ppermute x6, waiting for transfers between devices, scatter_permute(): lax.ppermute(chunk, axis, [(j, (j + s) % count) for j in range(count)])  31.6 us
    ppermute x6, waiting for transfers between devices, received(): lax.ppermute(values, axis, [(j, (j + s) % count) for j in range(count)])  25.5 us
    pallas_call x2, Pallas kernels, head_project(): pl.pallas_call(body, grid_spec=grid_spec, out_shape=jax.ShapeDtypeStruct(...  18.5 us
    unnamed x55, local copies, waits for them, and re-layouts  15.8 us
    ppermute x1, waiting for transfers between devices, with_halo(): lax.ppermute(tail, axis, [(i, (i + 1) % count) for i in range(ends)])  11.3 us
  transfers between devices with their start and end apart: 39, of which 30 were waited for; matrix products, arithmetic and copies ran while one was open for 5% of the time, Pallas kernels for 2%

profile of v3, /device:TPU:28, one launch (start us, length us, event | category | flops | bytes accessed | tf_op | source)
XLA Modules:
  0.0 401.4 jit_solution(8164239534796894351)
XLA Ops:
  17.5 6.0 %collective-permute-done.3.refs_2_ = bf16[128,1024]{1,0:T(8,128)(2,1)S(1)} collective-permute-done((bf16[128,1024]{1,0:T(8,128)(2,1)S(1)}, bf16[128,1024]{1,0:T(8,128)(2,1)S(1)}, u32[]{:S(2)}, u32[]{:S(2)}) %collective-permute-start.3) | collective-permute-done | bytes 262176 | tf_op jit(solution)/shard_map/ppermute | solution.py:162
  24.9 8.5 %shard_map.154 = bf16[4,512,768]{2,1,0:T(8,128)(2,1)} custom-call(s32[2]{0:T(128)} %pad_add_fusion.1.index_ref, bf16[128,1024]{1,0:T(8,128)(2,1)} %copy-done.11, bf16[128,1024]{1,0:T(8,128)(2,1)} %copy-done.15, bf16[128,1024]{1,0:T(8,128)(2,1)} %copy-done.16, bf16[128,1024]{1,0:T(8,128)(2,1)} %copy-done.17, bf16[1024,1024]{1,0:T(8,128)(2,1)} %refs_4_.2, ...), custom_call_target="tpu_custom_call" | custom-call | tf_op jit(solution)/shard_map/pallas_call | solution.py:197
  46.8 17.3 %collective-permute-done.6 = bf16[512,768]{1,0:T(8,128)(2,1)} collective-permute-done((bf16[512,768]{1,0:T(8,128)(2,1)}, bf16[512,768]{1,0:T(8,128)(2,1)}, u32[]{:S(2)}, u32[]{:S(2)}) %collective-permute-start.6) | collective-permute-done | bytes 786464 | tf_op jit(solution)/shard_map/ppermute | solution.py:138
  71.9 5.4 %collective-permute-done.11 = bf16[3,255,256]{2,1,0:T(8,128)(2,1)S(1)} collective-permute-done((bf16[3,255,256]{2,1,0:T(8,128)(2,1)}, bf16[3,255,256]{2,1,0:T(8,128)(2,1)S(1)}, u32[]{:S(2)}, u32[]{:S(2)}) %collective-permute-start.11) | collective-permute-done | bytes 391712 | tf_op jit(solution)/shard_map/ppermute | solution.py:23
  78.0 11.3 %collective-permute-done.10 = bf16[3,255,256]{2,1,0:T(8,128)(2,1)} collective-permute-done((bf16[3,255,256]{2,1,0:T(8,128)(2,1)}, bf16[3,255,256]{2,1,0:T(8,128)(2,1)}, u32[]{:S(2)}, u32[]{:S(2)}) %collective-permute-start.10) | collective-permute-done | bytes 391712 | tf_op jit(solution)/shard_map/ppermute | solution.py:21
  102.0 5.8 %fusion.65 = (f32[2,512]{1,0:T(2,128)S(1)}, bf16[2,512,1022]{2,1,0:T(8,128)(2,1)S(1)}) fusion(f32[2,512,1022]{2,1,0:T(8,128)} %fusion.36, pred[512,1022]{1,0:T(8,128)(4,1)S(1)} %or_and_fusion), kind=kOutput, calls=%fused_computation.156 | output fusion | flops 8373245 | bytes 6806528 | tf_op jit(solution)/shard_map/sub | solution.py:97
  111.7 5.9 %collective-permute-done.14 = bf16[512,256]{1,0:T(8,128)(2,1)} collective-permute-done((bf16[512,256]{1,0:T(8,128)(2,1)S(1)}, bf16[512,256]{1,0:T(8,128)(2,1)}, u32[]{:S(2)}, u32[]{:S(2)}) %collective-permute-start.14) | collective-permute-done | bytes 262176 | tf_op jit(solution)/shard_map/ppermute | solution.py:138
  117.6 5.1 %collective-permute-done.13 = bf16[512,256]{1,0:T(8,128)(2,1)} collective-permute-done((bf16[512,256]{1,0:T(8,128)(2,1)S(1)}, bf16[512,256]{1,0:T(8,128)(2,1)}, u32[]{:S(2)}, u32[]{:S(2)}) %collective-permute-start.13) | collective-permute-done | bytes 262176 | tf_op jit(solution)/shard_map/ppermute | solution.py:138
  133.8 5.4 %collective-permute-done.17 = bf16[128,1024]{1,0:T(8,128)(2,1)} collective-permute-done((bf16[128,1024]{1,0:T(8,128)(2,1)}, bf16[128,1024]{1,0:T(8,128)(2,1)}, u32[]{:S(2)}, u32[]{:S(2)}) %collective-permute-start.17) | collective-permute-done | bytes 262176 | tf_op jit(solution)/shard_map/ppermute | solution.py:66
  141.4 4.4 %collective-permute-done.15 = bf16[128,1024]{1,0:T(8,128)(2,1)} collective-permute-done((bf16[128,1024]{1,0:T(8,128)(2,1)}, bf16[128,1024]{1,0:T(8,128)(2,1)}, u32[]{:S(2)}, u32[]{:S(2)}) %collective-permute-start.15) | collective-permute-done | bytes 262176 | tf_op jit(solution)/shard_map/ppermute | solution.py:66
  152.4 5.8 %collective-permute-done.18 = bf16[128,1024]{1,0:T(8,128)(2,1)S(1)} collective-permute-done((bf16[128,1024]{1,0:T(8,128)(2,1)}, bf16[128,1024]{1,0:T(8,128)(2,1)S(1)}, u32[]{:S(2)}, u32[]{:S(2)}) %collective-permute-start.18) | collective-permute-done | bytes 262176 | tf_op jit(solution)/shard_map/ppermute | solution.py:33
  168.9 15.5 %collective-permute-done.21.refs_1_ = bf16[192,1024]{1,0:T(8,128)(2,1)S(1)} collective-permute-done((bf16[192,1024]{1,0:T(8,128)(2,1)S(1)}, bf16[192,1024]{1,0:T(8,128)(2,1)S(1)}, u32[]{:S(2)}, u32[]{:S(2)}) %collective-permute-start.21) | collective-permute-done | bytes 393248 | tf_op jit(solution)/shard_map/ppermute | solution.py:162
  185.4 10.1 %shard_map.155 = bf16[4,768,768]{2,1,0:T(8,128)(2,1)} custom-call(s32[2]{0:T(128)} %pad_add_fusion.1.index_ref, bf16[192,1024]{1,0:T(8,128)(2,1)} %copy-done.7, bf16[192,1024]{1,0:T(8,128)(2,1)} %copy-done.13, bf16[192,1024]{1,0:T(8,128)(2,1)} %copy-done.14, bf16[192,1024]{1,0:T(8,128)(2,1)} %collective-permute-done.23.refs_3_, bf16[1024,1024]{1,0:T(8,128)(2,1)} %refs_4_.3, ...), custom_call_target="tpu_custom_call" | custom-call | tf_op jit(solution)/shard_map/pallas_call | solution.py:197
  197.5 4.5 %collective-permute-done.24 = bf16[1536,768]{1,0:T(8,128)(2,1)S(1)} collective-permute-done((bf16[1536,768]{1,0:T(8,128)(2,1)S(1)}, bf16[1536,768]{1,0:T(8,128)(2,1)S(1)}, u32[]{:S(2)}, u32[]{:S(2)}) %collective-permute-start.24) | collective-permute-done | bytes 2359328 | tf_op jit(solution)/shard_map/ppermute | solution.py:138
  203.2 27.2 %collective-permute-done.25 = bf16[768,768]{1,0:T(8,128)(2,1)S(1)} collective-permute-done((bf16[768,768]{1,0:T(8,128)(2,1)S(1)}, bf16[768,768]{1,0:T(8,128)(2,1)S(1)}, u32[]{:S(2)}, u32[]{:S(2)}) %collective-permute-start.25) | collective-permute-done | bytes 1179680 | tf_op jit(solution)/shard_map/ppermute | solution.py:138
  238.8 6.9 %shard_map.156 = (f32[2,768,1]{2,1,0:T(8,128)}, f32[2,768,1]{2,1,0:T(8,128)}, f32[2,768,128]{2,1,0:T(8,128)}) custom-call(s32[1]{0:T(128)} %bitcast.26.place_ref, s32[1]{0:T(128)} %constant.147.clone.shift_ref, bf16[768,768]{1,0:T(8,128)(2,1)} %copy-done.2, bf16[1,768,512]{2,1,0:T(8,128)(2,1)} %get-tuple-element.23.kv_ref), custom_call_target="tpu_custom_call" | custom-call | tf_op jit(solution)/shard_map/pallas_call | solution.py:337
  245.7 9.1 %collective-permute-done.26 = bf16[768,512]{1,0:T(8,128)(2,1)} collective-permute-done((bf16[768,512]{1,0:T(8,128)(2,1)}, bf16[768,512]{1,0:T(8,128)(2,1)}, u32[]{:S(2)}, u32[]{:S(2)}) %collective-permute-start.26) | collective-permute-done | bytes 786464 | tf_op jit(solution)/shard_map/ppermute | solution.py:423
  262.4 11.8 %collective-permute-done.28 = bf16[768,512]{1,0:T(8,128)(2,1)} collective-permute-done((bf16[768,512]{1,0:T(8,128)(2,1)}, bf16[768,512]{1,0:T(8,128)(2,1)}, u32[]{:S(2)}, u32[]{:S(2)}) %collective-permute-start.28) | collective-permute-done | bytes 786464 | tf_op jit(solution)/shard_map/ppermute | solution.py:423
  278.4 13.7 %collective-permute-done.30 = bf16[768,512]{1,0:T(8,128)(2,1)} collective-permute-done((bf16[768,512]{1,0:T(8,128)(2,1)}, bf16[768,512]{1,0:T(8,128)(2,1)}, u32[]{:S(2)}, u32[]{:S(2)}) %collective-permute-start.30) | collective-permute-done | bytes 786464 | tf_op jit(solution)/shard_map/ppermute | solution.py:423
  294.1 18.7 %collective-permute-done.31 = bf16[768,512]{1,0:T(8,128)(2,1)S(1)} collective-permute-done((bf16[768,512]{1,0:T(8,128)(2,1)}, bf16[768,512]{1,0:T(8,128)(2,1)S(1)}, u32[]{:S(2)}, u32[]{:S(2)}) %collective-permute-start.31) | collective-permute-done | bytes 786464 | tf_op jit(solution)/shard_map/ppermute | solution.py:423
  314.7 30.7 %shard_map.157 = bf16[768,256]{1,0:T(8,128)(2,1)} custom-call(s32[1]{0:T(128)} %bitcast.26.place_ref, s32[7]{0:T(128)} %constant.148.clone.shift_ref, bf16[768,768]{1,0:T(8,128)(2,1)} %copy-done.2, bf16[7,768,512]{2,1,0:T(8,128)(2,1)} %bitcast_dynamic-update-slice_fusion.kv_ref, f32[2,768,1]{2,1,0:T(8,128)} %get-tuple-element.8.refs_0_, ...), custom_call_target="tpu_custom_call" | custom-call | tf_op jit(solution)/shard_map/pallas_call | solution.py:337
  347.3 9.6 %collective-permute-done.35 = bf16[768,256]{1,0:T(8,128)(2,1)S(1)} collective-permute-done((bf16[768,256]{1,0:T(8,128)(2,1)}, bf16[768,256]{1,0:T(8,128)(2,1)S(1)}, u32[]{:S(2)}, u32[]{:S(2)}) %collective-permute-start.35) | collective-permute-done | bytes 393248 | tf_op jit(solution)/shard_map/ppermute | solution.py:138
  356.8 8.6 %collective-permute-done.34 = bf16[768,256]{1,0:T(8,128)(2,1)S(1)} collective-permute-done((bf16[768,256]{1,0:T(8,128)(2,1)}, bf16[768,256]{1,0:T(8,128)(2,1)S(1)}, u32[]{:S(2)}, u32[]{:S(2)}) %collective-permute-start.34) | collective-permute-done | bytes 393248 | tf_op jit(solution)/shard_map/ppermute | solution.py:138
  379.4 16.4 %collective-permute-done.38 = bf16[192,1024]{1,0:T(8,128)(2,1)} collective-permute-done((bf16[192,1024]{1,0:T(8,128)(2,1)}, bf16[192,1024]{1,0:T(8,128)(2,1)}, u32[]{:S(2)}, u32[]{:S(2)}) %collective-permute-start.38) | collective-permute-done | bytes 393248 | tf_op jit(solution)/shard_map/ppermute | solution.py:66
  (187 shorter events, 137.1 us)
Async XLA Ops:
  9.1 14.4 %collective-permute-start.3 = (bf16[128,1024]{1,0:T(8,128)(2,1)S(1)}, bf16[128,1024]{1,0:T(8,128)(2,1)S(1)}, u32[]{:S(2)}, u32[]{:S(2)}) collective-permute-start(bf16[128,1024]{1,0:T(8,128)(2,1)S(1)} %fusion.31.refs_0_), channel_id=1, source_target_pairs={{0,2},{1,3},{2,0},{3,1},{4,6},{5,7},{6,4},{7,5},{8,10},{9,11},{10,... | collective-permute-start | bytes 786440 | tf_op jit(solution)/shard_map/ppermute | solution.py:162
  45.3 18.8 %collective-permute-start.6 = (bf16[512,768]{1,0:T(8,128)(2,1)}, bf16[512,768]{1,0:T(8,128)(2,1)}, u32[]{:S(2)}, u32[]{:S(2)}) collective-permute-start(bf16[512,768]{1,0:T(8,128)(2,1)} %fusion.10), channel_id=1, source_target_pairs={{0,8},{4,12},{8,0},{12,4},{1,9},{5,13},{9,1},{13,5},{2,10},{6,14},... | collective-permute-start | bytes 2359304 | tf_op jit(solution)/shard_map/ppermute | solution.py:138
  70.3 19.0 %collective-permute-start.10 = (bf16[3,255,256]{2,1,0:T(8,128)(2,1)}, bf16[3,255,256]{2,1,0:T(8,128)(2,1)}, u32[]{:S(2)}, u32[]{:S(2)}) collective-permute-start(bf16[3,255,256]{2,1,0:T(8,128)(2,1)} %get-tuple-element.31), channel_id=1, source_target_pairs={{0,16},{16,32},{32,48},{48,64},{64,80},{80,96},{96,112},{1,17},{17... | collective-permute-start | bytes 1175048 | tf_op jit(solution)/shard_map/ppermute | solution.py:21
  108.9 13.8 %collective-permute-start.13 = (bf16[512,256]{1,0:T(8,128)(2,1)S(1)}, bf16[512,256]{1,0:T(8,128)(2,1)}, u32[]{:S(2)}, u32[]{:S(2)}) collective-permute-start(bf16[512,256]{1,0:T(8,128)(2,1)S(1)} %copy.35), channel_id=1, source_target_pairs={{0,8},{4,12},{8,0},{12,4},{1,9},{5,13},{9,1},{13,5},{2,10},{6,14},... | collective-permute-start | bytes 786440 | tf_op jit(solution)/shard_map/ppermute | solution.py:138
  110.2 12.5 %collective-permute-start.12 = (bf16[512,256]{1,0:T(8,128)(2,1)S(1)}, bf16[512,256]{1,0:T(8,128)(2,1)}, u32[]{:S(2)}, u32[]{:S(2)}) collective-permute-start(bf16[512,256]{1,0:T(8,128)(2,1)S(1)} %copy.35), channel_id=1, source_target_pairs={{0,4},{4,0},{8,12},{12,8},{1,5},{5,1},{9,13},{13,9},{2,6},{6,2},{1... | collective-permute-start | bytes 786440 | tf_op jit(solution)/shard_map/ppermute | solution.py:138
  130.4 11.1 %collective-permute-start.16 = (bf16[128,1024]{1,0:T(8,128)(2,1)}, bf16[128,1024]{1,0:T(8,128)(2,1)}, u32[]{:S(2)}, u32[]{:S(2)}) collective-permute-start(bf16[128,1024]{1,0:T(8,128)(2,1)} %get-tuple-element.27), channel_id=1, source_target_pairs={{0,2},{1,3},{2,0},{3,1},{4,6},{5,7},{6,4},{7,5},{8,10},{9,11},{10,... | collective-permute-start | bytes 786440 | tf_op jit(solution)/shard_map/ppermute | solution.py:66
  132.3 13.5 %collective-permute-start.15 = (bf16[128,1024]{1,0:T(8,128)(2,1)}, bf16[128,1024]{1,0:T(8,128)(2,1)}, u32[]{:S(2)}, u32[]{:S(2)}) collective-permute-start(bf16[128,1024]{1,0:T(8,128)(2,1)} %get-tuple-element.25), channel_id=1, source_target_pairs={{0,1},{1,2},{2,3},{3,0},{4,5},{5,6},{6,7},{7,4},{8,9},{9,10},{10,1... | collective-permute-start | bytes 786440 | tf_op jit(solution)/shard_map/ppermute | solution.py:66
  164.6 19.8 %collective-permute-start.21 = (bf16[192,1024]{1,0:T(8,128)(2,1)S(1)}, bf16[192,1024]{1,0:T(8,128)(2,1)S(1)}, u32[]{:S(2)}, u32[]{:S(2)}) collective-permute-start(bf16[192,1024]{1,0:T(8,128)(2,1)S(1)} %multiply_convert_fusion.refs_0_), channel_id=1, source_target_pairs={{0,1},{1,2},{2,3},{3,0},{4,5},{5,6},{6,7},{7,4},{8,9},{9,10},{10,1... | collective-permute-start | bytes 1179656 | tf_op jit(solution)/shard_map/ppermute | solution.py:162
  164.7 19.7 %collective-permute-start.22 = (bf16[192,1024]{1,0:T(8,128)(2,1)S(1)}, bf16[192,1024]{1,0:T(8,128)(2,1)S(1)}, u32[]{:S(2)}, u32[]{:S(2)}) collective-permute-start(bf16[192,1024]{1,0:T(8,128)(2,1)S(1)} %multiply_convert_fusion.refs_0_), channel_id=1, source_target_pairs={{0,2},{1,3},{2,0},{3,1},{4,6},{5,7},{6,4},{7,5},{8,10},{9,11},{10,... | collective-permute-start | bytes 1179656 | tf_op jit(solution)/shard_map/ppermute | solution.py:162
  166.6 18.6 %collective-permute-start.23 = (bf16[192,1024]{1,0:T(8,128)(2,1)S(1)}, bf16[192,1024]{1,0:T(8,128)(2,1)}, u32[]{:S(2)}, u32[]{:S(2)}) collective-permute-start(bf16[192,1024]{1,0:T(8,128)(2,1)S(1)} %multiply_convert_fusion.refs_0_), channel_id=1, source_target_pairs={{0,3},{1,0},{2,1},{3,2},{4,7},{5,4},{6,5},{7,6},{8,11},{9,8},{10,9... | collective-permute-start | bytes 1179656 | tf_op jit(solution)/shard_map/ppermute | solution.py:162
  202.3 28.1 %collective-permute-start.25 = (bf16[768,768]{1,0:T(8,128)(2,1)S(1)}, bf16[768,768]{1,0:T(8,128)(2,1)S(1)}, u32[]{:S(2)}, u32[]{:S(2)}) collective-permute-start(bf16[768,768]{1,0:T(8,128)(2,1)S(1)} %fusion.2), channel_id=1, source_target_pairs={{0,8},{4,12},{8,0},{12,4},{1,9},{5,13},{9,1},{13,5},{2,10},{6,14},... | collective-permute-start | bytes 3538952 | tf_op jit(solution)/shard_map/ppermute | solution.py:138
  232.3 22.5 %collective-permute-start.26 = (bf16[768,512]{1,0:T(8,128)(2,1)}, bf16[768,512]{1,0:T(8,128)(2,1)}, u32[]{:S(2)}, u32[]{:S(2)}) collective-permute-start(bf16[768,512]{1,0:T(8,128)(2,1)} %get-tuple-element.24), channel_id=1, source_target_pairs={{0,16},{16,32},{32,48},{48,64},{64,80},{80,96},{96,112},{1,17},{17... | collective-permute-start | bytes 2359304 | tf_op jit(solution)/shard_map/ppermute | solution.py:423
  233.6 25.5 %collective-permute-start.27 = (bf16[768,512]{1,0:T(8,128)(2,1)}, bf16[768,512]{1,0:T(8,128)(2,1)}, u32[]{:S(2)}, u32[]{:S(2)}) collective-permute-start(bf16[768,512]{1,0:T(8,128)(2,1)} %get-tuple-element.24), channel_id=1, source_target_pairs={{0,32},{16,48},{32,64},{48,80},{64,96},{80,112},{1,33},{17,49},{33... | collective-permute-start | bytes 2359304 | tf_op jit(solution)/shard_map/ppermute | solution.py:423
  234.9 39.3 %collective-permute-start.28 = (bf16[768,512]{1,0:T(8,128)(2,1)}, bf16[768,512]{1,0:T(8,128)(2,1)}, u32[]{:S(2)}, u32[]{:S(2)}) collective-permute-start(bf16[768,512]{1,0:T(8,128)(2,1)} %get-tuple-element.24), channel_id=1, source_target_pairs={{0,48},{16,64},{32,80},{48,96},{64,112},{1,49},{17,65},{33,81},{49... | collective-permute-start | bytes 2359304 | tf_op jit(solution)/shard_map/ppermute | solution.py:423
  236.2 40.0 %collective-permute-start.29 = (bf16[768,512]{1,0:T(8,128)(2,1)}, bf16[768,512]{1,0:T(8,128)(2,1)}, u32[]{:S(2)}, u32[]{:S(2)}) collective-permute-start(bf16[768,512]{1,0:T(8,128)(2,1)} %get-tuple-element.24), channel_id=1, source_target_pairs={{0,64},{16,80},{32,96},{48,112},{1,65},{17,81},{33,97},{49,113},{2... | collective-permute-start | bytes 2359304 | tf_op jit(solution)/shard_map/ppermute | solution.py:423
  237.5 54.5 %collective-permute-start.30 = (bf16[768,512]{1,0:T(8,128)(2,1)}, bf16[768,512]{1,0:T(8,128)(2,1)}, u32[]{:S(2)}, u32[]{:S(2)}) collective-permute-start(bf16[768,512]{1,0:T(8,128)(2,1)} %get-tuple-element.24), channel_id=1, source_target_pairs={{0,80},{16,96},{32,112},{1,81},{17,97},{33,113},{2,82},{18,98},{34... | collective-permute-start | bytes 2359304 | tf_op jit(solution)/shard_map/ppermute | solution.py:423
  254.8 58.0 %collective-permute-start.31 = (bf16[768,512]{1,0:T(8,128)(2,1)}, bf16[768,512]{1,0:T(8,128)(2,1)S(1)}, u32[]{:S(2)}, u32[]{:S(2)}) collective-permute-start(bf16[768,512]{1,0:T(8,128)(2,1)} %get-tuple-element.24), channel_id=1, source_target_pairs={{0,96},{16,112},{1,97},{17,113},{2,98},{18,114},{3,99},{19,115},{4... | collective-permute-start | bytes 2359304 | tf_op jit(solution)/shard_map/ppermute | solution.py:423
  259.1 54.7 %collective-permute-start.32 = (bf16[768,512]{1,0:T(8,128)(2,1)}, bf16[768,512]{1,0:T(8,128)(2,1)S(1)}, u32[]{:S(2)}, u32[]{:S(2)}) collective-permute-start(bf16[768,512]{1,0:T(8,128)(2,1)} %get-tuple-element.24), channel_id=1, source_target_pairs={{0,112},{1,113},{2,114},{3,115},{4,116},{5,117},{6,118},{7,119},{8... | collective-permute-start | bytes 2359304 | tf_op jit(solution)/shard_map/ppermute | solution.py:423
  345.4 11.4 %collective-permute-start.35 = (bf16[768,256]{1,0:T(8,128)(2,1)}, bf16[768,256]{1,0:T(8,128)(2,1)S(1)}, u32[]{:S(2)}, u32[]{:S(2)}) collective-permute-start(bf16[768,256]{1,0:T(8,128)(2,1)} %shard_map.157), channel_id=1, source_target_pairs={{0,12},{4,8},{8,4},{12,0},{1,13},{5,9},{9,5},{13,1},{2,14},{6,10},... | collective-permute-start | bytes 1179656 | tf_op jit(solution)/shard_map/ppermute | solution.py:138
  346.6 18.9 %collective-permute-start.34 = (bf16[768,256]{1,0:T(8,128)(2,1)}, bf16[768,256]{1,0:T(8,128)(2,1)S(1)}, u32[]{:S(2)}, u32[]{:S(2)}) collective-permute-start(bf16[768,256]{1,0:T(8,128)(2,1)} %shard_map.157), channel_id=1, source_target_pairs={{0,8},{4,12},{8,0},{12,4},{1,9},{5,13},{9,1},{13,5},{2,10},{6,14},... | collective-permute-start | bytes 1179656 | tf_op jit(solution)/shard_map/ppermute | solution.py:138
  347.1 18.4 %collective-permute-start.33 = (bf16[768,256]{1,0:T(8,128)(2,1)}, bf16[768,256]{1,0:T(8,128)(2,1)S(1)}, u32[]{:S(2)}, u32[]{:S(2)}) collective-permute-start(bf16[768,256]{1,0:T(8,128)(2,1)} %shard_map.157), channel_id=1, source_target_pairs={{0,4},{4,0},{8,12},{12,8},{1,5},{5,1},{9,13},{13,9},{2,6},{6,2},{1... | collective-permute-start | bytes 1179656 | tf_op jit(solution)/shard_map/ppermute | solution.py:138
  376.5 19.3 %collective-permute-start.38 = (bf16[192,1024]{1,0:T(8,128)(2,1)}, bf16[192,1024]{1,0:T(8,128)(2,1)}, u32[]{:S(2)}, u32[]{:S(2)}) collective-permute-start(bf16[192,1024]{1,0:T(8,128)(2,1)} %get-tuple-element.18), channel_id=1, source_target_pairs={{0,3},{1,0},{2,1},{3,2},{4,7},{5,4},{6,5},{7,6},{8,11},{9,8},{10,9... | collective-permute-start | bytes 1179656 | tf_op jit(solution)/shard_map/ppermute | solution.py:66
  378.5 17.2 %collective-permute-start.37 = (bf16[192,1024]{1,0:T(8,128)(2,1)}, bf16[192,1024]{1,0:T(8,128)(2,1)}, u32[]{:S(2)}, u32[]{:S(2)}) collective-permute-start(bf16[192,1024]{1,0:T(8,128)(2,1)} %get-tuple-element.19), channel_id=1, source_target_pairs={{0,2},{1,3},{2,0},{3,1},{4,6},{5,7},{6,4},{7,5},{8,10},{9,11},{10,... | collective-permute-start | bytes 1179656 | tf_op jit(solution)/shard_map/ppermute | solution.py:66
  378.8 20.1 %collective-permute-start.36 = (bf16[192,1024]{1,0:T(8,128)(2,1)S(1)}, bf16[192,1024]{1,0:T(8,128)(2,1)}, u32[]{:S(2)}, u32[]{:S(2)}) collective-permute-start(bf16[192,1024]{1,0:T(8,128)(2,1)S(1)} %get-tuple-element.17), channel_id=1, source_target_pairs={{0,1},{1,2},{2,3},{3,0},{4,5},{5,6},{6,7},{7,4},{8,9},{9,10},{10,1... | collective-permute-start | bytes 1179656 | tf_op jit(solution)/shard_map/ppermute | solution.py:66
  (36 other events, 612.9 us)

commit v4 on v2

--- a/solution.py
+++ b/solution.py
@@ -205,10 +205,50 @@
 
 def out_project_heads(attended, weight):
     row_count = lax.axis_size("row")
-    whole = gather_row(attended)
-    shaped = weight.reshape(row_count, weight.shape[0] // row_count, weight.shape[1])
-    summed = jnp.einsum("rtf,rfo->to", whole, shaped, preferred_element_type=jnp.float32)
-    return scatter_permute(summed.astype(jnp.bfloat16), "col")
+    col_count = lax.axis_size("col")
+    pieces = [attended] + [flip(attended, "row", b) for b in range(1, row_count)]
+    count, width = attended.shape
+    rows = count // col_count
+    index = jnp.stack([lax.axis_index("row"), lax.axis_index("col")]).astype(jnp.int32)
+
+    def body(index_ref, *refs):
+        piece_refs = refs[:row_count]
+        w_ref = refs[row_count]
+        o_ref = refs[-1]
+        own = index_ref[0]
+        place = index_ref[1]
+        for s in range(col_count):
+            start = pl.multiple_of(((place + s) % col_count) * rows, 8)
+            total = None
+            for b in range(row_count):
+                source = (own % 2 + b % 2) % 2 + 2 * ((own // 2 + b // 2) % 2)
+                first = pl.multiple_of(source * width, 8)
+                part = jnp.dot(
+                    piece_refs[b][pl.ds(start, rows), :],
+                    w_ref[pl.ds(first, width), :],
+                    preferred_element_type=jnp.float32,
+                )
+                total = part if total is None else total + part
+            o_ref[s] = total.astype(o_ref.dtype)
+
+    grid_spec = pltpu.PrefetchScalarGridSpec(
+        num_scalar_prefetch=1,
+        grid=(1,),
+        in_specs=[pl.BlockSpec((count, width), lambda i, x: (0, 0)) for _ in pieces]
+        + [pl.BlockSpec(weight.shape, lambda i, x: (0, 0))],
+        out_specs=pl.BlockSpec((col_count, rows, weight.shape[1]), lambda i, x: (0, 0, 0)),
+    )
+    parts = pl.pallas_call(
+        body,
+        grid_spec=grid_spec,
+        out_shape=jax.ShapeDtypeStruct((col_count, rows, weight.shape[1]), jnp.bfloat16),
+    )(index, *pieces, weight)
+    total = parts[0].astype(jnp.float32)
+    for s in range(1, col_count):
+        total = total + lax.ppermute(
+            parts[s], "col", [(j, (j + s) % col_count) for j in range(col_count)]
+        ).astype(jnp.float32)
+    return total
 
 
 def causal_attend(proj, blocks, shifts, place, carry=None, last=True):

time: 387 us -> 374 us (0.966)
  Pallas kernels: 56 us -> 66.6 us
  other arithmetic: 25.5 us -> 17.3 us
  matrix products: 9.46 us -> 1.95 us
  local copies, waits for them, and re-layouts: 34.5 us -> 27.5 us
    pallas_call x0 -> x2, Pallas kernels: none -> 10.6 us  [out_project_heads(): pl.pallas_call(body, grid_spec=grid_spec, out_shape=jax.ShapeDtypeStruct(...]
    dot_general x2 -> x0, matrix products: 6.44 us -> none  [out_project_heads(): jnp.einsum('rtf,rfo->to', whole, shaped, preferred_element_type=jnp.float32)]
    gather x2 -> x0, local copies, waits for them, and re-layouts: 4.82 us -> none  [gather_row(): return jnp.take(stacked, order, axis=0)]
    unnamed x54 -> x58, local copies, waits for them, and re-layouts: 14.9 us -> 13.1 us
  transfers between devices with their start and end apart: 41 -> 41, of which waited for: 28 -> 30; matrix products, arithmetic and copies ran while one was open for 6% -> 6% of each run, Pallas kernels for 4% -> 4%
where the time goes in v4:
time: 374 us; the launch traced here: 373 us
  waiting for transfers between devices  205 us (55%)
  Pallas kernels  66.6 us (18%)
  starting transfers between devices  54.7 us (15%)
  local copies, waits for them, and re-layouts  27.5 us (7%)
  other arithmetic  17.3 us (5%)
    ppermute x14, waiting for transfers between devices, flip(): return lax.ppermute(values, axis, [(j, j ^ bit) for j in range(count)])  70.5 us
    ppermute x7, waiting for transfers between devices, per_device(): lax.ppermute(keyvals, 'req', [(j, j + s) for j in range(req_count - s)])  57 us
    pallas_call x2, Pallas kernels, causal_attend(): pl.pallas_call(body, grid_spec=grid_spec, out_shape=out_shape)  37.5 us
    ppermute x6, waiting for transfers between devices, out_project_heads(): lax.ppermute(parts[s], 'col', [(j, (j + s) % col_count) for j in range(co...  32.1 us
    ppermute x6, waiting for transfers between devices, received(): lax.ppermute(values, axis, [(j, (j + s) % count) for j in range(count)])  18.6 us
    pallas_call x2, Pallas kernels, head_project(): pl.pallas_call(body, grid_spec=grid_spec, out_shape=jax.ShapeDtypeStruct(...  18.5 us
    unnamed x58, local copies, waits for them, and re-layouts  13.1 us
    ppermute x2, waiting for transfers between devices, with_halo(): lax.ppermute(head, axis, [((i + 1) % count, i) for i in range(ends)])  12.7 us
  transfers between devices with their start and end apart: 41, of which 30 were waited for; matrix products, arithmetic and copies ran while one was open for 6% of the time, Pallas kernels for 4%

profile of v4, /device:TPU:28, one launch (start us, length us, event | category | flops | bytes accessed | tf_op | source)
XLA Modules:
  0.0 373.2 jit_solution(2047282734606932729)
XLA Ops:
  24.8 8.5 %shard_map.154 = bf16[4,512,768]{2,1,0:T(8,128)(2,1)} custom-call(s32[2]{0:T(128)} %pad_add_fusion.3.index_ref, bf16[128,1024]{1,0:T(8,128)(2,1)} %copy-done.6, bf16[128,1024]{1,0:T(8,128)(2,1)} %copy-done.16, bf16[128,1024]{1,0:T(8,128)(2,1)} %copy-done.17, bf16[128,1024]{1,0:T(8,128)(2,1)} %copy-done.18, bf16[1024,1024]{1,0:T(8,128)(2,1)} %refs_4_.4, ...), custom_call_target="tpu_custom_call" | custom-call | tf_op jit(solution)/shard_map/pallas_call | solution.py:197
  47.2 12.4 %collective-permute-done.4 = s32[2,255]{1,0:T(2,128)S(1)} collective-permute-done((s32[2,255]{1,0:T(2,128)S(1)}, s32[2,255]{1,0:T(2,128)S(1)}, u32[]{:S(2)}, u32[]{:S(2)}) %collective-permute-start.4) | collective-permute-done | bytes 2072 | tf_op jit(solution)/shard_map/ppermute | solution.py:23
  62.6 4.8 %collective-permute-start.13 = (bf16[2,255,256]{2,1,0:T(8,128)(2,1)S(1)}, bf16[2,255,256]{2,1,0:T(8,128)(2,1)S(1)}, u32[]{:S(2)}, u32[]{:S(2)}) collective-permute-start(bf16[2,255,256]{2,1,0:T(8,128)(2,1)S(1)} %get-tuple-element.29), channel_id=1, source_target_pairs={{16,0},{32,16},{48,32},{64,48},{80,64},{96,80},{112,96},{17,1},{33... | collective-permute-start | bytes 783368 | tf_op jit(solution)/shard_map/ppermute | solution.py:23
  72.2 7.6 %collective-permute-done.12 = bf16[2,255,256]{2,1,0:T(8,128)(2,1)S(1)} collective-permute-done((bf16[2,255,256]{2,1,0:T(8,128)(2,1)S(1)}, bf16[2,255,256]{2,1,0:T(8,128)(2,1)S(1)}, u32[]{:S(2)}, u32[]{:S(2)}) %collective-permute-start.12) | collective-permute-done | bytes 261152 | tf_op jit(solution)/shard_map/ppermute | solution.py:21
  87.6 6.7 %collective-permute-done.15.refs_2_ = bf16[512,256]{1,0:T(8,128)(2,1)S(1)} collective-permute-done((bf16[512,256]{1,0:T(8,128)(2,1)S(1)}, bf16[512,256]{1,0:T(8,128)(2,1)S(1)}, u32[]{:S(2)}, u32[]{:S(2)}) %collective-permute-start.15) | collective-permute-done | bytes 262176 | tf_op jit(solution)/shard_map/ppermute | solution.py:138
  94.4 4.7 %collective-permute-done.16.refs_3_ = bf16[512,256]{1,0:T(8,128)(2,1)S(1)} collective-permute-done((bf16[512,256]{1,0:T(8,128)(2,1)S(1)}, bf16[512,256]{1,0:T(8,128)(2,1)S(1)}, u32[]{:S(2)}, u32[]{:S(2)}) %collective-permute-start.16) | collective-permute-done | bytes 262176 | tf_op jit(solution)/shard_map/ppermute | solution.py:138
  99.7 4.8 %shard_map.155 = bf16[4,128,1024]{2,1,0:T(8,128)(2,1)} custom-call(s32[2]{0:T(128)} %pad_add_fusion.2.index_ref, bf16[512,256]{1,0:T(8,128)(2,1)} %copy-done.5, bf16[512,256]{1,0:T(8,128)(2,1)} %copy-done.13, bf16[512,256]{1,0:T(8,128)(2,1)} %copy-done.14, bf16[512,256]{1,0:T(8,128)(2,1)} %copy-done.15, bf16[1024,1024]{1,0:T(8,128)(2,1)} %refs_4_.5), custom_call_target="tpu_custom_call" | custom-call | tf_op jit(solution)/shard_map/pallas_call | solution.py:241
  110.3 4.7 %collective-permute-done.19 = bf16[128,1024]{1,0:T(8,128)(2,1)S(1)} collective-permute-done((bf16[128,1024]{1,0:T(8,128)(2,1)S(1)}, bf16[128,1024]{1,0:T(8,128)(2,1)S(1)}, u32[]{:S(2)}, u32[]{:S(2)}) %collective-permute-start.19) | collective-permute-done | bytes 262176 | tf_op jit(solution)/shard_map/ppermute | solution.py:248
  118.1 4.6 %collective-permute-done.17 = bf16[128,1024]{1,0:T(8,128)(2,1)S(1)} collective-permute-done((bf16[128,1024]{1,0:T(8,128)(2,1)S(1)}, bf16[128,1024]{1,0:T(8,128)(2,1)S(1)}, u32[]{:S(2)}, u32[]{:S(2)}) %collective-permute-start.17) | collective-permute-done | bytes 262176 | tf_op jit(solution)/shard_map/ppermute | solution.py:248
  129.2 4.8 %collective-permute-done.20 = bf16[128,1024]{1,0:T(8,128)(2,1)S(1)} collective-permute-done((bf16[128,1024]{1,0:T(8,128)(2,1)S(1)}, bf16[128,1024]{1,0:T(8,128)(2,1)S(1)}, u32[]{:S(2)}, u32[]{:S(2)}) %collective-permute-start.20) | collective-permute-done | bytes 262176 | tf_op jit(solution)/shard_map/ppermute | solution.py:33
  143.2 15.9 %collective-permute-done.23.refs_1_ = bf16[192,1024]{1,0:T(8,128)(2,1)S(1)} collective-permute-done((bf16[192,1024]{1,0:T(8,128)(2,1)S(1)}, bf16[192,1024]{1,0:T(8,128)(2,1)S(1)}, u32[]{:S(2)}, u32[]{:S(2)}) %collective-permute-start.23) | collective-permute-done | bytes 393248 | tf_op jit(solution)/shard_map/ppermute | solution.py:162
  160.8 10.1 %shard_map.156 = bf16[4,768,768]{2,1,0:T(8,128)(2,1)} custom-call(s32[2]{0:T(128)} %pad_add_fusion.3.index_ref, bf16[192,1024]{1,0:T(8,128)(2,1)} %copy-done.4, bf16[192,1024]{1,0:T(8,128)(2,1)} %copy-done.7, bf16[192,1024]{1,0:T(8,128)(2,1)} %copy-done.8, bf16[192,1024]{1,0:T(8,128)(2,1)} %copy-done.9, bf16[1024,1024]{1,0:T(8,128)(2,1)} %refs_4_.6, ...), custom_call_target="tpu_custom_call" | custom-call | tf_op jit(solution)/shard_map/pallas_call | solution.py:197
  179.0 26.9 %collective-permute-done.27 = bf16[768,768]{1,0:T(8,128)(2,1)S(1)} collective-permute-done((bf16[768,768]{1,0:T(8,128)(2,1)S(1)}, bf16[768,768]{1,0:T(8,128)(2,1)S(1)}, u32[]{:S(2)}, u32[]{:S(2)}) %collective-permute-start.27) | collective-permute-done | bytes 1179680 | tf_op jit(solution)/shard_map/ppermute | solution.py:138
  214.2 6.8 %shard_map.157 = (f32[2,768,1]{2,1,0:T(8,128)}, f32[2,768,1]{2,1,0:T(8,128)}, f32[2,768,128]{2,1,0:T(8,128)}) custom-call(s32[1]{0:T(128)} %bitcast.25.place_ref, s32[1]{0:T(128)} %constant.96.clone.shift_ref, bf16[768,768]{1,0:T(8,128)(2,1)} %copy-done.1, bf16[1,768,512]{2,1,0:T(8,128)(2,1)} %get-tuple-element.18.kv_ref), custom_call_target="tpu_custom_call" | custom-call | tf_op jit(solution)/shard_map/pallas_call | solution.py:377
  221.0 9.4 %collective-permute-done.28 = bf16[768,512]{1,0:T(8,128)(2,1)} collective-permute-done((bf16[768,512]{1,0:T(8,128)(2,1)}, bf16[768,512]{1,0:T(8,128)(2,1)}, u32[]{:S(2)}, u32[]{:S(2)}) %collective-permute-start.28) | collective-permute-done | bytes 786464 | tf_op jit(solution)/shard_map/ppermute | solution.py:461
  233.7 16.6 %collective-permute-done.29 = bf16[768,512]{1,0:T(8,128)(2,1)} collective-permute-done((bf16[768,512]{1,0:T(8,128)(2,1)}, bf16[768,512]{1,0:T(8,128)(2,1)}, u32[]{:S(2)}, u32[]{:S(2)}) %collective-permute-start.29) | collective-permute-done | bytes 786464 | tf_op jit(solution)/shard_map/ppermute | solution.py:461
  256.9 10.0 %collective-permute-done.32 = bf16[768,512]{1,0:T(8,128)(2,1)S(1)} collective-permute-done((bf16[768,512]{1,0:T(8,128)(2,1)}, bf16[768,512]{1,0:T(8,128)(2,1)S(1)}, u32[]{:S(2)}, u32[]{:S(2)}) %collective-permute-start.32) | collective-permute-done | bytes 786464 | tf_op jit(solution)/shard_map/ppermute | solution.py:461
  267.9 21.1 %collective-permute-done.33 = bf16[768,512]{1,0:T(8,128)(2,1)S(1)} collective-permute-done((bf16[768,512]{1,0:T(8,128)(2,1)}, bf16[768,512]{1,0:T(8,128)(2,1)S(1)}, u32[]{:S(2)}, u32[]{:S(2)}) %collective-permute-start.33) | collective-permute-done | bytes 786464 | tf_op jit(solution)/shard_map/ppermute | solution.py:461
  290.8 30.7 %shard_map.158.refs_0_ = bf16[768,256]{1,0:T(8,128)(2,1)} custom-call(s32[1]{0:T(128)} %bitcast.25.place_ref, s32[7]{0:T(128)} %constant.97.clone.shift_ref, bf16[768,768]{1,0:T(8,128)(2,1)} %copy-done.1, bf16[7,768,512]{2,1,0:T(8,128)(2,1)} %bitcast_dynamic-update-slice_fusion.kv_ref, f32[2,768,1]{2,1,0:T(8,128)} %get-tuple-element.8.refs_0_, ...), custom_call_target="tpu_custom_call" | custom-call | tf_op jit(solution)/shard_map/pallas_call | solution.py:377
  323.4 10.2 %collective-permute-done.36.refs_2_ = bf16[768,256]{1,0:T(8,128)(2,1)S(1)} collective-permute-done((bf16[768,256]{1,0:T(8,128)(2,1)}, bf16[768,256]{1,0:T(8,128)(2,1)S(1)}, u32[]{:S(2)}, u32[]{:S(2)}) %collective-permute-start.36) | collective-permute-done | bytes 393248 | tf_op jit(solution)/shard_map/ppermute | solution.py:138
  333.6 7.6 %collective-permute-done.37.refs_3_ = bf16[768,256]{1,0:T(8,128)(2,1)S(1)} collective-permute-done((bf16[768,256]{1,0:T(8,128)(2,1)}, bf16[768,256]{1,0:T(8,128)(2,1)S(1)}, u32[]{:S(2)}, u32[]{:S(2)}) %collective-permute-start.37) | collective-permute-done | bytes 393248 | tf_op jit(solution)/shard_map/ppermute | solution.py:138
  342.0 5.7 %shard_map.159 = bf16[4,192,1024]{2,1,0:T(8,128)(2,1)} custom-call(s32[2]{0:T(128)} %pad_add_fusion.2.index_ref, bf16[768,256]{1,0:T(8,128)(2,1)} %shard_map.158.refs_0_, bf16[768,256]{1,0:T(8,128)(2,1)} %copy-done.10, bf16[768,256]{1,0:T(8,128)(2,1)} %copy-done.11, bf16[768,256]{1,0:T(8,128)(2,1)} %copy-done.12, bf16[1024,1024]{1,0:T(8,128)(2,1)} %refs_4_.7), custom_call_target="tpu_custom_call" | custom-call | tf_op jit(solution)/shard_map/pallas_call | solution.py:241
  351.5 9.6 %collective-permute-done.40 = bf16[192,1024]{1,0:T(8,128)(2,1)S(1)} collective-permute-done((bf16[192,1024]{1,0:T(8,128)(2,1)S(1)}, bf16[192,1024]{1,0:T(8,128)(2,1)S(1)}, u32[]{:S(2)}, u32[]{:S(2)}) %collective-permute-start.40) | collective-permute-done | bytes 393248 | tf_op jit(solution)/shard_map/ppermute | solution.py:248
  364.1 7.1 %collective-permute-done.38 = bf16[192,1024]{1,0:T(8,128)(2,1)S(1)} collective-permute-done((bf16[192,1024]{1,0:T(8,128)(2,1)S(1)}, bf16[192,1024]{1,0:T(8,128)(2,1)S(1)}, u32[]{:S(2)}, u32[]{:S(2)}) %collective-permute-start.38) | collective-permute-done | bytes 393248 | tf_op jit(solution)/shard_map/ppermute | solution.py:248
  (188 shorter events, 121.4 us)
Async XLA Ops:
  8.9 14.5 %collective-permute-start.8 = (bf16[128,1024]{1,0:T(8,128)(2,1)S(1)}, bf16[128,1024]{1,0:T(8,128)(2,1)S(1)}, u32[]{:S(2)}, u32[]{:S(2)}) collective-permute-start(bf16[128,1024]{1,0:T(8,128)(2,1)S(1)} %fusion.30.refs_0_), channel_id=1, source_target_pairs={{0,2},{1,3},{2,0},{3,1},{4,6},{5,7},{6,4},{7,5},{8,10},{9,11},{10,... | collective-permute-start | bytes 786440 | tf_op jit(solution)/shard_map/ppermute | solution.py:162
  14.2 22.0 %collective-permute-start = (s32[128,2]{0,1:T(2,128)S(1)}, s32[128,2]{0,1:T(2,128)S(1)}, u32[]{:S(2)}, u32[]{:S(2)}) collective-permute-start(s32[128,2]{0,1:T(2,128)S(1)} %get-tuple-element.34), channel_id=1, source_target_pairs={{0,3},{1,0},{2,1},{3,2},{4,7},{5,4},{6,5},{7,6},{8,11},{9,8},{10,9... | collective-permute-start | bytes 3080 | tf_op jit(solution)/shard_map/ppermute | solution.py:50
  14.2 22.0 %collective-permute-start.1 = (s32[128,2]{0,1:T(2,128)S(1)}, s32[128,2]{0,1:T(2,128)S(1)}, u32[]{:S(2)}, u32[]{:S(2)}) collective-permute-start(s32[128,2]{0,1:T(2,128)S(1)} %get-tuple-element.34), channel_id=1, source_target_pairs={{0,2},{1,3},{2,0},{3,1},{4,6},{5,7},{6,4},{7,5},{8,10},{9,11},{10,... | collective-permute-start | bytes 3080 | tf_op jit(solution)/shard_map/ppermute | solution.py:50
  17.9 18.3 %collective-permute-start.2 = (s32[128,2]{0,1:T(2,128)S(1)}, s32[128,2]{0,1:T(2,128)S(1)}, u32[]{:S(2)}, u32[]{:S(2)}) collective-permute-start(s32[128,2]{0,1:T(2,128)S(1)} %get-tuple-element.34), channel_id=1, source_target_pairs={{0,1},{1,2},{2,3},{3,0},{4,5},{5,6},{6,7},{7,4},{8,9},{9,10},{10,1... | collective-permute-start | bytes 3080 | tf_op jit(solution)/shard_map/ppermute | solution.py:50
  41.1 19.9 %collective-permute-start.11 = (bf16[512,768]{1,0:T(8,128)(2,1)S(1)}, bf16[512,768]{1,0:T(8,128)(2,1)S(1)}, u32[]{:S(2)}, u32[]{:S(2)}) collective-permute-start(bf16[512,768]{1,0:T(8,128)(2,1)S(1)} %fusion.10), channel_id=1, source_target_pairs={{0,8},{4,12},{8,0},{12,4},{1,9},{5,13},{9,1},{13,5},{2,10},{6,14},... | collective-permute-start | bytes 2359304 | tf_op jit(solution)/shard_map/ppermute | solution.py:138
  42.5 17.1 %collective-permute-start.4 = (s32[2,255]{1,0:T(2,128)S(1)}, s32[2,255]{1,0:T(2,128)S(1)}, u32[]{:S(2)}, u32[]{:S(2)}) collective-permute-start(s32[2,255]{1,0:T(2,128)S(1)} %get-tuple-element.33), channel_id=1, source_target_pairs={{16,0},{32,16},{48,32},{64,48},{80,64},{96,80},{112,96},{17,1},{33... | collective-permute-start | bytes 6128 | tf_op jit(solution)/shard_map/ppermute | solution.py:23
  45.2 15.7 %collective-permute-start.3 = (s32[2,255]{1,0:T(2,128)S(1)}, s32[2,255]{1,0:T(2,128)S(1)}, u32[]{:S(2)}, u32[]{:S(2)}) collective-permute-start(s32[2,255]{1,0:T(2,128)S(1)} %get-tuple-element.32), channel_id=1, source_target_pairs={{0,16},{16,32},{32,48},{48,64},{64,80},{80,96},{96,112},{1,17},{17... | collective-permute-start | bytes 6128 | tf_op jit(solution)/shard_map/ppermute | solution.py:21
  67.5 12.3 %collective-permute-start.12 = (bf16[2,255,256]{2,1,0:T(8,128)(2,1)S(1)}, bf16[2,255,256]{2,1,0:T(8,128)(2,1)S(1)}, u32[]{:S(2)}, u32[]{:S(2)}) collective-permute-start(bf16[2,255,256]{2,1,0:T(8,128)(2,1)S(1)} %get-tuple-element.28), channel_id=1, source_target_pairs={{0,16},{16,32},{32,48},{48,64},{64,80},{80,96},{96,112},{1,17},{17... | collective-permute-start | bytes 783368 | tf_op jit(solution)/shard_map/ppermute | solution.py:21
  86.4 12.7 %collective-permute-start.16 = (bf16[512,256]{1,0:T(8,128)(2,1)S(1)}, bf16[512,256]{1,0:T(8,128)(2,1)S(1)}, u32[]{:S(2)}, u32[]{:S(2)}) collective-permute-start(bf16[512,256]{1,0:T(8,128)(2,1)S(1)} %copy.26.refs_0_), channel_id=1, source_target_pairs={{0,12},{4,8},{8,4},{12,0},{1,13},{5,9},{9,5},{13,1},{2,14},{6,10},... | collective-permute-start | bytes 786440 | tf_op jit(solution)/shard_map/ppermute | solution.py:138
  108.5 14.2 %collective-permute-start.17 = (bf16[128,1024]{1,0:T(8,128)(2,1)S(1)}, bf16[128,1024]{1,0:T(8,128)(2,1)S(1)}, u32[]{:S(2)}, u32[]{:S(2)}) collective-permute-start(bf16[128,1024]{1,0:T(8,128)(2,1)S(1)} %get-tuple-element.20), channel_id=1, source_target_pairs={{0,1},{1,2},{2,3},{3,0},{4,5},{5,6},{6,7},{7,4},{8,9},{9,10},{10,1... | collective-permute-start | bytes 786440 | tf_op jit(solution)/shard_map/ppermute | solution.py:248
  139.4 19.8 %collective-permute-start.23 = (bf16[192,1024]{1,0:T(8,128)(2,1)S(1)}, bf16[192,1024]{1,0:T(8,128)(2,1)S(1)}, u32[]{:S(2)}, u32[]{:S(2)}) collective-permute-start(bf16[192,1024]{1,0:T(8,128)(2,1)S(1)} %multiply_convert_fusion.refs_0_), channel_id=1, source_target_pairs={{0,1},{1,2},{2,3},{3,0},{4,5},{5,6},{6,7},{7,4},{8,9},{9,10},{10,1... | collective-permute-start | bytes 1179656 | tf_op jit(solution)/shard_map/ppermute | solution.py:162
  139.4 19.7 %collective-permute-start.24 = (bf16[192,1024]{1,0:T(8,128)(2,1)S(1)}, bf16[192,1024]{1,0:T(8,128)(2,1)S(1)}, u32[]{:S(2)}, u32[]{:S(2)}) collective-permute-start(bf16[192,1024]{1,0:T(8,128)(2,1)S(1)} %multiply_convert_fusion.refs_0_), channel_id=1, source_target_pairs={{0,2},{1,3},{2,0},{3,1},{4,6},{5,7},{6,4},{7,5},{8,10},{9,11},{10,... | collective-permute-start | bytes 1179656 | tf_op jit(solution)/shard_map/ppermute | solution.py:162
  140.7 19.1 %collective-permute-start.25 = (bf16[192,1024]{1,0:T(8,128)(2,1)S(1)}, bf16[192,1024]{1,0:T(8,128)(2,1)S(1)}, u32[]{:S(2)}, u32[]{:S(2)}) collective-permute-start(bf16[192,1024]{1,0:T(8,128)(2,1)S(1)} %multiply_convert_fusion.refs_0_), channel_id=1, source_target_pairs={{0,3},{1,0},{2,1},{3,2},{4,7},{5,4},{6,5},{7,6},{8,11},{9,8},{10,9... | collective-permute-start | bytes 1179656 | tf_op jit(solution)/shard_map/ppermute | solution.py:162
  177.7 28.1 %collective-permute-start.27 = (bf16[768,768]{1,0:T(8,128)(2,1)S(1)}, bf16[768,768]{1,0:T(8,128)(2,1)S(1)}, u32[]{:S(2)}, u32[]{:S(2)}) collective-permute-start(bf16[768,768]{1,0:T(8,128)(2,1)S(1)} %fusion.2), channel_id=1, source_target_pairs={{0,8},{4,12},{8,0},{12,4},{1,9},{5,13},{9,1},{13,5},{2,10},{6,14},... | collective-permute-start | bytes 3538952 | tf_op jit(solution)/shard_map/ppermute | solution.py:138
  207.7 22.7 %collective-permute-start.28 = (bf16[768,512]{1,0:T(8,128)(2,1)}, bf16[768,512]{1,0:T(8,128)(2,1)}, u32[]{:S(2)}, u32[]{:S(2)}) collective-permute-start(bf16[768,512]{1,0:T(8,128)(2,1)} %get-tuple-element.19), channel_id=1, source_target_pairs={{0,16},{16,32},{32,48},{48,64},{64,80},{80,96},{96,112},{1,17},{17... | collective-permute-start | bytes 2359304 | tf_op jit(solution)/shard_map/ppermute | solution.py:461
  209.0 41.3 %collective-permute-start.29 = (bf16[768,512]{1,0:T(8,128)(2,1)}, bf16[768,512]{1,0:T(8,128)(2,1)}, u32[]{:S(2)}, u32[]{:S(2)}) collective-permute-start(bf16[768,512]{1,0:T(8,128)(2,1)} %get-tuple-element.19), channel_id=1, source_target_pairs={{0,32},{16,48},{32,64},{48,80},{64,96},{80,112},{1,33},{17,49},{33... | collective-permute-start | bytes 2359304 | tf_op jit(solution)/shard_map/ppermute | solution.py:461
  210.3 43.7 %collective-permute-start.30 = (bf16[768,512]{1,0:T(8,128)(2,1)}, bf16[768,512]{1,0:T(8,128)(2,1)}, u32[]{:S(2)}, u32[]{:S(2)}) collective-permute-start(bf16[768,512]{1,0:T(8,128)(2,1)} %get-tuple-element.19), channel_id=1, source_target_pairs={{0,48},{16,64},{32,80},{48,96},{64,112},{1,49},{17,65},{33,81},{49... | collective-permute-start | bytes 2359304 | tf_op jit(solution)/shard_map/ppermute | solution.py:461
  211.6 44.4 %collective-permute-start.31 = (bf16[768,512]{1,0:T(8,128)(2,1)}, bf16[768,512]{1,0:T(8,128)(2,1)S(1)}, u32[]{:S(2)}, u32[]{:S(2)}) collective-permute-start(bf16[768,512]{1,0:T(8,128)(2,1)} %get-tuple-element.19), channel_id=1, source_target_pairs={{0,64},{16,80},{32,96},{48,112},{1,65},{17,81},{33,97},{49,113},{2... | collective-permute-start | bytes 2359304 | tf_op jit(solution)/shard_map/ppermute | solution.py:461
  212.9 54.0 %collective-permute-start.32 = (bf16[768,512]{1,0:T(8,128)(2,1)}, bf16[768,512]{1,0:T(8,128)(2,1)S(1)}, u32[]{:S(2)}, u32[]{:S(2)}) collective-permute-start(bf16[768,512]{1,0:T(8,128)(2,1)} %get-tuple-element.19), channel_id=1, source_target_pairs={{0,80},{16,96},{32,112},{1,81},{17,97},{33,113},{2,82},{18,98},{34... | collective-permute-start | bytes 2359304 | tf_op jit(solution)/shard_map/ppermute | solution.py:461
  230.4 58.6 %collective-permute-start.33 = (bf16[768,512]{1,0:T(8,128)(2,1)}, bf16[768,512]{1,0:T(8,128)(2,1)S(1)}, u32[]{:S(2)}, u32[]{:S(2)}) collective-permute-start(bf16[768,512]{1,0:T(8,128)(2,1)} %get-tuple-element.19), channel_id=1, source_target_pairs={{0,96},{16,112},{1,97},{17,113},{2,98},{18,114},{3,99},{19,115},{4... | collective-permute-start | bytes 2359304 | tf_op jit(solution)/shard_map/ppermute | solution.py:461
  250.3 39.6 %collective-permute-start.34 = (bf16[768,512]{1,0:T(8,128)(2,1)}, bf16[768,512]{1,0:T(8,128)(2,1)S(1)}, u32[]{:S(2)}, u32[]{:S(2)}) collective-permute-start(bf16[768,512]{1,0:T(8,128)(2,1)} %get-tuple-element.19), channel_id=1, source_target_pairs={{0,112},{1,113},{2,114},{3,115},{4,116},{5,117},{6,118},{7,119},{8... | collective-permute-start | bytes 2359304 | tf_op jit(solution)/shard_map/ppermute | solution.py:461
  322.4 18.8 %collective-permute-start.37 = (bf16[768,256]{1,0:T(8,128)(2,1)}, bf16[768,256]{1,0:T(8,128)(2,1)S(1)}, u32[]{:S(2)}, u32[]{:S(2)}) collective-permute-start(bf16[768,256]{1,0:T(8,128)(2,1)} %shard_map.158.refs_0_), channel_id=1, source_target_pairs={{0,12},{4,8},{8,4},{12,0},{1,13},{5,9},{9,5},{13,1},{2,14},{6,10},... | collective-permute-start | bytes 1179656 | tf_op jit(solution)/shard_map/ppermute | solution.py:138
  350.6 13.5 %collective-permute-start.39 = (bf16[192,1024]{1,0:T(8,128)(2,1)S(1)}, bf16[192,1024]{1,0:T(8,128)(2,1)S(1)}, u32[]{:S(2)}, u32[]{:S(2)}) collective-permute-start(bf16[192,1024]{1,0:T(8,128)(2,1)S(1)} %get-tuple-element.17), channel_id=1, source_target_pairs={{0,2},{1,3},{2,0},{3,1},{4,6},{5,7},{6,4},{7,5},{8,10},{9,11},{10,... | collective-permute-start | bytes 1179656 | tf_op jit(solution)/shard_map/ppermute | solution.py:248
  350.6 20.6 %collective-permute-start.38 = (bf16[192,1024]{1,0:T(8,128)(2,1)S(1)}, bf16[192,1024]{1,0:T(8,128)(2,1)S(1)}, u32[]{:S(2)}, u32[]{:S(2)}) collective-permute-start(bf16[192,1024]{1,0:T(8,128)(2,1)S(1)} %get-tuple-element.15), channel_id=1, source_target_pairs={{0,1},{1,2},{2,3},{3,0},{4,5},{5,6},{6,7},{7,4},{8,9},{9,10},{10,1... | collective-permute-start | bytes 1179656 | tf_op jit(solution)/shard_map/ppermute | solution.py:248
  (40 other events, 315.3 us)

commit v5 on v4

--- a/solution.py
+++ b/solution.py
@@ -138,12 +138,10 @@
     return lax.ppermute(values, axis, [(j, j ^ bit) for j in range(count)])
 
 
-def scatter_row(values):
-    rows = values.shape[0] // 4
-    chunk = [values[k * rows : (k + 1) * rows] for k in range(4)]
-    sent = flip(jnp.concatenate([chunk[1], chunk[3]], axis=0), "row", 1)
-    near = chunk[0].astype(jnp.float32) + sent[:rows].astype(jnp.float32)
-    far = (chunk[2].astype(jnp.float32) + sent[rows:].astype(jnp.float32)).astype(jnp.bfloat16)
+def scatter_row(keep, send):
+    sent = flip(send, "row", 1)
+    near = keep[0].astype(jnp.float32) + sent[0].astype(jnp.float32)
+    far = (keep[1].astype(jnp.float32) + sent[1].astype(jnp.float32)).astype(jnp.bfloat16)
     return (near + flip(far, "row", 2).astype(jnp.float32)).astype(jnp.bfloat16)
 
 
@@ -175,32 +173,42 @@
     def body(index_ref, *refs):
         x_refs = refs[:count]
         w_refs = refs[count : count + groups]
-        o_ref = refs[-1]
+        keep_ref, send_ref = refs[-2:]
         own = index_ref[0]
+        low = index_ref[1] % 2
         for s in range(count):
             start = pl.multiple_of(((own - s + count) % count) * rows, 8)
             for g in range(groups):
-                o_ref[0, pl.ds(start, rows), g * part : (g + 1) * part] = jnp.dot(
-                    x_refs[s][...], w_refs[g][...], preferred_element_type=jnp.float32
-                ).astype(o_ref.dtype)
-
+                both = jnp.dot(x_refs[s][...], w_refs[g][...], preferred_element_type=jnp.float32)
+                first, second = both[:, :part], both[:, part:]
+                kept = jnp.where(low == 0, first, second)
+                given = jnp.where(low == 0, second, first)
+                keep_ref[0, pl.ds(start, rows), g * part : (g + 1) * part] = kept.astype(
+                    keep_ref.dtype
+                )
+                send_ref[0, pl.ds(start, rows), g * part : (g + 1) * part] = given.astype(
+                    send_ref.dtype
+                )
+
+    half = row_count // 2
+    block = pl.BlockSpec((1, count * rows, groups * part), lambda g, i: (g, 0, 0))
     grid_spec = pltpu.PrefetchScalarGridSpec(
         num_scalar_prefetch=1,
-        grid=(row_count,),
-        in_specs=[pl.BlockSpec((rows, depth), lambda r, i: (0, 0)) for _ in pieces]
-        + [pl.BlockSpec((depth, part), lambda r, i: (0, r)) for _ in weights],
-        out_specs=pl.BlockSpec(
-            (1, count * rows, groups * part),
-            lambda r, i: ((r % 2 + i[1] % 2) % 2 + 2 * ((r // 2 + i[1] // 2) % 2), 0, 0),
-        ),
-    )
-    summed = pl.pallas_call(
+        grid=(half,),
+        in_specs=[pl.BlockSpec((rows, depth), lambda g, i: (0, 0)) for _ in pieces]
+        + [
+            pl.BlockSpec((depth, 2 * part), lambda g, i: (0, (i[1] // 2 + g) % 2))
+            for _ in weights
+        ],
+        out_specs=[block, block],
+    )
+    shape = jax.ShapeDtypeStruct((half, count * rows, groups * part), jnp.bfloat16)
+    keep, send = pl.pallas_call(
         body,
         grid_spec=grid_spec,
-        out_shape=jax.ShapeDtypeStruct((row_count, count * rows, groups * part), jnp.bfloat16),
+        out_shape=[shape, shape],
     )(index, *pieces, *weights)
-    summed = summed.reshape(row_count * count * rows, groups * part)
-    return scatter_row(summed)
+    return scatter_row(keep, send)
 
 
 def out_project_heads(attended, weight):

time: 374 us -> 372 us (level)
  starting transfers between devices: 54.7 us -> 64.7 us
  waiting for transfers between devices: 205 us -> 196 us
    ppermute x2, waiting for transfers between devices: 12.7 us -> 0.93 us  [with_halo(): lax.ppermute(head, axis, [((i + 1) % count, i) for i in range(ends)])]
    ppermute x2, starting transfers between devices: 7.52 us -> 12.3 us  [with_halo(): lax.ppermute(head, axis, [((i + 1) % count, i) for i in range(ends)])]
    ppermute x1, starting transfers between devices: 3.96 us -> 8.51 us  [passed_along(): return lax.ppermute(shard, axis, pairs)]
    ppermute x7, waiting for transfers between devices: 57 us -> 60.9 us  [per_device(): lax.ppermute(keyvals, 'req', [(j, j + s) for j in range(req_count - s)])]
  transfers between devices with their start and end apart: 41 -> 41, of which waited for: 30 -> 28; matrix products, arithmetic and copies ran while one was open for 6% -> 5% of each run, Pallas kernels for 4% -> 4%
where the time goes in v5:
time: 372 us; the launch traced here: 371 us
  waiting for transfers between devices  196 us (53%)
  Pallas kernels  66.1 us (18%)
  starting transfers between devices  64.7 us (17%)
  local copies, waits for them, and re-layouts  24.2 us (7%)
  other arithmetic  17.4 us (5%)
    ppermute x14, waiting for transfers between devices, flip(): return lax.ppermute(values, axis, [(j, j ^ bit) for j in range(count)])  71.2 us
    ppermute x7, waiting for transfers between devices, per_device(): lax.ppermute(keyvals, 'req', [(j, j + s) for j in range(req_count - s)])  60.9 us
    pallas_call x2, Pallas kernels, causal_attend(): pl.pallas_call(body, grid_spec=grid_spec, out_shape=out_shape)  37.5 us
    ppermute x6, waiting for transfers between devices, out_project_heads(): lax.ppermute(parts[s], 'col', [(j, (j + s) % col_count) for j in range(co...  28.5 us
    ppermute x6, waiting for transfers between devices, received(): lax.ppermute(values, axis, [(j, (j + s) % count) for j in range(count)])  19.2 us
    pallas_call x2, Pallas kernels, head_project(): pl.pallas_call(body, grid_spec=grid_spec, out_shape=[shape, shape])  18 us
    unnamed x58, local copies, waits for them, and re-layouts  13.1 us
    ppermute x2, starting transfers between devices, with_halo(): lax.ppermute(head, axis, [((i + 1) % count, i) for i in range(ends)])  12.3 us
  transfers between devices with their start and end apart: 41, of which 28 were waited for; matrix products, arithmetic and copies ran while one was open for 5% of the time, Pallas kernels for 4%

profile of v5, /device:TPU:28, one launch (start us, length us, event | category | flops | bytes accessed | tf_op | source)
XLA Modules:
  0.0 370.6 jit_solution(354842478198141700)
XLA Ops:
  24.8 8.0 %shard_map.154 = (bf16[2,512,768]{2,1,0:T(8,128)(2,1)}, bf16[2,512,768]{2,1,0:T(8,128)(2,1)}) custom-call(s32[2]{0:T(128)} %pad_add_fusion.3.index_ref, bf16[128,1024]{1,0:T(8,128)(2,1)} %copy-done.6, bf16[128,1024]{1,0:T(8,128)(2,1)} %copy-done.16, bf16[128,1024]{1,0:T(8,128)(2,1)} %copy-done.17, bf16[128,1024]{1,0:T(8,128)(2,1)} %copy-done.18, ...), custom_call_target="tpu_custom_call" | custom-call | tf_op jit(solution)/shard_map/pallas_call | solution.py:206
  40.8 6.1 %collective-permute-start.4 = (s32[2,255]{1,0:T(2,128)S(1)}, s32[2,255]{1,0:T(2,128)S(1)}, u32[]{:S(2)}, u32[]{:S(2)}) collective-permute-start(s32[2,255]{1,0:T(2,128)S(1)} %get-tuple-element.37), channel_id=1, source_target_pairs={{16,0},{32,16},{48,32},{64,48},{80,64},{96,80},{112,96},{17,1},{33... | collective-permute-start | bytes 6128 | tf_op jit(solution)/shard_map/ppermute | solution.py:23
  47.5 10.3 %collective-permute-done.3 = s32[2,255]{1,0:T(2,128)S(1)} collective-permute-done((s32[2,255]{1,0:T(2,128)S(1)}, s32[2,255]{1,0:T(2,128)S(1)}, u32[]{:S(2)}, u32[]{:S(2)}) %collective-permute-start.3) | collective-permute-done | bytes 2072 | tf_op jit(solution)/shard_map/ppermute | solution.py:21
  60.9 6.2 %collective-permute-start.13 = (bf16[2,255,256]{2,1,0:T(8,128)(2,1)S(1)}, bf16[2,255,256]{2,1,0:T(8,128)(2,1)S(1)}, u32[]{:S(2)}, u32[]{:S(2)}) collective-permute-start(bf16[2,255,256]{2,1,0:T(8,128)(2,1)S(1)} %get-tuple-element.33), channel_id=1, source_target_pairs={{16,0},{32,16},{48,32},{64,48},{80,64},{96,80},{112,96},{17,1},{33... | collective-permute-start | bytes 783368 | tf_op jit(solution)/shard_map/ppermute | solution.py:23
  79.3 6.7 %collective-permute-done.15.refs_2_ = bf16[512,256]{1,0:T(8,128)(2,1)S(1)} collective-permute-done((bf16[512,256]{1,0:T(8,128)(2,1)S(1)}, bf16[512,256]{1,0:T(8,128)(2,1)S(1)}, u32[]{:S(2)}, u32[]{:S(2)}) %collective-permute-start.15) | collective-permute-done | bytes 262176 | tf_op jit(solution)/shard_map/ppermute | solution.py:138
  86.0 4.7 %collective-permute-done.16.refs_3_ = bf16[512,256]{1,0:T(8,128)(2,1)S(1)} collective-permute-done((bf16[512,256]{1,0:T(8,128)(2,1)S(1)}, bf16[512,256]{1,0:T(8,128)(2,1)S(1)}, u32[]{:S(2)}, u32[]{:S(2)}) %collective-permute-start.16) | collective-permute-done | bytes 262176 | tf_op jit(solution)/shard_map/ppermute | solution.py:138
  91.4 4.8 %shard_map.155 = bf16[4,128,1024]{2,1,0:T(8,128)(2,1)} custom-call(s32[2]{0:T(128)} %pad_add_fusion.2.index_ref, bf16[512,256]{1,0:T(8,128)(2,1)} %copy-done.5, bf16[512,256]{1,0:T(8,128)(2,1)} %copy-done.13, bf16[512,256]{1,0:T(8,128)(2,1)} %copy-done.14, bf16[512,256]{1,0:T(8,128)(2,1)} %copy-done.15, bf16[1024,1024]{1,0:T(8,128)(2,1)} %refs_4_.5), custom_call_target="tpu_custom_call" | custom-call | tf_op jit(solution)/shard_map/pallas_call | solution.py:249
  103.2 9.7 %collective-permute-done.17 = bf16[128,1024]{1,0:T(8,128)(2,1)S(1)} collective-permute-done((bf16[128,1024]{1,0:T(8,128)(2,1)S(1)}, bf16[128,1024]{1,0:T(8,128)(2,1)S(1)}, u32[]{:S(2)}, u32[]{:S(2)}) %collective-permute-start.17) | collective-permute-done | bytes 262176 | tf_op jit(solution)/shard_map/ppermute | solution.py:256
  114.7 8.5 %collective-permute-start.20 = (bf16[128,1024]{1,0:T(8,128)(2,1)S(1)}, bf16[128,1024]{1,0:T(8,128)(2,1)S(1)}, u32[]{:S(2)}, u32[]{:S(2)}) collective-permute-start(bf16[128,1024]{1,0:T(8,128)(2,1)S(1)} %fusion.29), channel_id=1, source_target_pairs={{1,0},{2,1},{3,2},{16,3},{17,16},{18,17},{19,18},{32,19},{33,32},{... | collective-permute-start | bytes 786440 | tf_op jit(solution)/shard_map/ppermute | solution.py:33
  124.6 4.3 %collective-permute-done.20 = bf16[128,1024]{1,0:T(8,128)(2,1)S(1)} collective-permute-done((bf16[128,1024]{1,0:T(8,128)(2,1)S(1)}, bf16[128,1024]{1,0:T(8,128)(2,1)S(1)}, u32[]{:S(2)}, u32[]{:S(2)}) %collective-permute-start.20) | collective-permute-done | bytes 262176 | tf_op jit(solution)/shard_map/ppermute | solution.py:33
  137.6 16.5 %collective-permute-done.23.refs_1_ = bf16[192,1024]{1,0:T(8,128)(2,1)S(1)} collective-permute-done((bf16[192,1024]{1,0:T(8,128)(2,1)S(1)}, bf16[192,1024]{1,0:T(8,128)(2,1)S(1)}, u32[]{:S(2)}, u32[]{:S(2)}) %collective-permute-start.23) | collective-permute-done | bytes 393248 | tf_op jit(solution)/shard_map/ppermute | solution.py:160
  155.7 10.0 %shard_map.156 = (bf16[2,768,768]{2,1,0:T(8,128)(2,1)}, bf16[2,768,768]{2,1,0:T(8,128)(2,1)}) custom-call(s32[2]{0:T(128)} %pad_add_fusion.3.index_ref, bf16[192,1024]{1,0:T(8,128)(2,1)} %copy-done.3, bf16[192,1024]{1,0:T(8,128)(2,1)} %copy-done.7, bf16[192,1024]{1,0:T(8,128)(2,1)} %copy-done.8, bf16[192,1024]{1,0:T(8,128)(2,1)} %copy-done.9, ...), custom_call_target="tpu_custom_call" | custom-call | tf_op jit(solution)/shard_map/pallas_call | solution.py:206
  165.7 4.7 %collective-permute-done.26 = bf16[2,768,768]{2,1,0:T(8,128)(2,1)S(1)} collective-permute-done((bf16[2,768,768]{2,1,0:T(8,128)(2,1)}, bf16[2,768,768]{2,1,0:T(8,128)(2,1)S(1)}, u32[]{:S(2)}, u32[]{:S(2)}) %collective-permute-start.26) | collective-permute-done | bytes 2359328 | tf_op jit(solution)/shard_map/ppermute | solution.py:138
  173.1 27.1 %collective-permute-done.27 = bf16[768,768]{1,0:T(8,128)(2,1)S(1)} collective-permute-done((bf16[768,768]{1,0:T(8,128)(2,1)S(1)}, bf16[768,768]{1,0:T(8,128)(2,1)S(1)}, u32[]{:S(2)}, u32[]{:S(2)}) %collective-permute-start.27) | collective-permute-done | bytes 1179680 | tf_op jit(solution)/shard_map/ppermute | solution.py:138
  208.5 6.8 %shard_map.157 = (f32[2,768,1]{2,1,0:T(8,128)}, f32[2,768,1]{2,1,0:T(8,128)}, f32[2,768,128]{2,1,0:T(8,128)}) custom-call(s32[1]{0:T(128)} %bitcast.23.place_ref, s32[1]{0:T(128)} %constant.96.clone.shift_ref, bf16[768,768]{1,0:T(8,128)(2,1)} %copy-done, bf16[1,768,512]{2,1,0:T(8,128)(2,1)} %get-tuple-element.22.kv_ref), custom_call_target="tpu_custom_call" | custom-call | tf_op jit(solution)/shard_map/pallas_call | solution.py:385
  215.3 10.7 %collective-permute-done.28 = bf16[768,512]{1,0:T(8,128)(2,1)} collective-permute-done((bf16[768,512]{1,0:T(8,128)(2,1)}, bf16[768,512]{1,0:T(8,128)(2,1)}, u32[]{:S(2)}, u32[]{:S(2)}) %collective-permute-start.28) | collective-permute-done | bytes 786464 | tf_op jit(solution)/shard_map/ppermute | solution.py:469
  234.5 13.2 %collective-permute-done.30 = bf16[768,512]{1,0:T(8,128)(2,1)} collective-permute-done((bf16[768,512]{1,0:T(8,128)(2,1)}, bf16[768,512]{1,0:T(8,128)(2,1)}, u32[]{:S(2)}, u32[]{:S(2)}) %collective-permute-start.30) | collective-permute-done | bytes 786464 | tf_op jit(solution)/shard_map/ppermute | solution.py:469
  250.8 15.4 %collective-permute-done.32 = bf16[768,512]{1,0:T(8,128)(2,1)S(1)} collective-permute-done((bf16[768,512]{1,0:T(8,128)(2,1)}, bf16[768,512]{1,0:T(8,128)(2,1)S(1)}, u32[]{:S(2)}, u32[]{:S(2)}) %collective-permute-start.32) | collective-permute-done | bytes 786464 | tf_op jit(solution)/shard_map/ppermute | solution.py:469
  267.1 19.8 %collective-permute-done.33 = bf16[768,512]{1,0:T(8,128)(2,1)S(1)} collective-permute-done((bf16[768,512]{1,0:T(8,128)(2,1)}, bf16[768,512]{1,0:T(8,128)(2,1)S(1)}, u32[]{:S(2)}, u32[]{:S(2)}) %collective-permute-start.33) | collective-permute-done | bytes 786464 | tf_op jit(solution)/shard_map/ppermute | solution.py:469
  288.8 30.7 %shard_map.158.refs_0_ = bf16[768,256]{1,0:T(8,128)(2,1)} custom-call(s32[1]{0:T(128)} %bitcast.23.place_ref, s32[7]{0:T(128)} %constant.97.clone.shift_ref, bf16[768,768]{1,0:T(8,128)(2,1)} %copy-done, bf16[7,768,512]{2,1,0:T(8,128)(2,1)} %bitcast_dynamic-update-slice_fusion.kv_ref, f32[2,768,1]{2,1,0:T(8,128)} %get-tuple-element.16.refs_0_, ...), custom_call_target="tpu_custom_call" | custom-call | tf_op jit(solution)/shard_map/pallas_call | solution.py:385
  321.4 10.2 %collective-permute-done.36.refs_2_ = bf16[768,256]{1,0:T(8,128)(2,1)S(1)} collective-permute-done((bf16[768,256]{1,0:T(8,128)(2,1)}, bf16[768,256]{1,0:T(8,128)(2,1)S(1)}, u32[]{:S(2)}, u32[]{:S(2)}) %collective-permute-start.36) | collective-permute-done | bytes 393248 | tf_op jit(solution)/shard_map/ppermute | solution.py:138
  331.6 7.7 %collective-permute-done.37.refs_3_ = bf16[768,256]{1,0:T(8,128)(2,1)S(1)} collective-permute-done((bf16[768,256]{1,0:T(8,128)(2,1)}, bf16[768,256]{1,0:T(8,128)(2,1)S(1)}, u32[]{:S(2)}, u32[]{:S(2)}) %collective-permute-start.37) | collective-permute-done | bytes 393248 | tf_op jit(solution)/shard_map/ppermute | solution.py:138
  340.0 5.7 %shard_map.159 = bf16[4,192,1024]{2,1,0:T(8,128)(2,1)} custom-call(s32[2]{0:T(128)} %pad_add_fusion.2.index_ref, bf16[768,256]{1,0:T(8,128)(2,1)} %shard_map.158.refs_0_, bf16[768,256]{1,0:T(8,128)(2,1)} %copy-done.10, bf16[768,256]{1,0:T(8,128)(2,1)} %copy-done.11, bf16[768,256]{1,0:T(8,128)(2,1)} %copy-done.12, bf16[1024,1024]{1,0:T(8,128)(2,1)} %refs_4_.7), custom_call_target="tpu_custom_call" | custom-call | tf_op jit(solution)/shard_map/pallas_call | solution.py:249
  350.4 17.6 %collective-permute-done.38 = bf16[192,1024]{1,0:T(8,128)(2,1)S(1)} collective-permute-done((bf16[192,1024]{1,0:T(8,128)(2,1)S(1)}, bf16[192,1024]{1,0:T(8,128)(2,1)S(1)}, u32[]{:S(2)}, u32[]{:S(2)}) %collective-permute-start.38) | collective-permute-done | bytes 393248 | tf_op jit(solution)/shard_map/ppermute | solution.py:256
  (184 shorter events, 104.6 us)
Async XLA Ops:
  8.9 14.5 %collective-permute-start.8 = (bf16[128,1024]{1,0:T(8,128)(2,1)S(1)}, bf16[128,1024]{1,0:T(8,128)(2,1)S(1)}, u32[]{:S(2)}, u32[]{:S(2)}) collective-permute-start(bf16[128,1024]{1,0:T(8,128)(2,1)S(1)} %fusion.28.refs_0_), channel_id=1, source_target_pairs={{0,2},{1,3},{2,0},{3,1},{4,6},{5,7},{6,4},{7,5},{8,10},{9,11},{10,... | collective-permute-start | bytes 786440 | tf_op jit(solution)/shard_map/ppermute | solution.py:160
  14.2 18.8 %collective-permute-start = (s32[128,2]{0,1:T(2,128)S(1)}, s32[128,2]{0,1:T(2,128)S(1)}, u32[]{:S(2)}, u32[]{:S(2)}) collective-permute-start(s32[128,2]{0,1:T(2,128)S(1)} %get-tuple-element.38), channel_id=1, source_target_pairs={{0,3},{1,0},{2,1},{3,2},{4,7},{5,4},{6,5},{7,6},{8,11},{9,8},{10,9... | collective-permute-start | bytes 3080 | tf_op jit(solution)/shard_map/ppermute | solution.py:50
  14.2 18.8 %collective-permute-start.1 = (s32[128,2]{0,1:T(2,128)S(1)}, s32[128,2]{0,1:T(2,128)S(1)}, u32[]{:S(2)}, u32[]{:S(2)}) collective-permute-start(s32[128,2]{0,1:T(2,128)S(1)} %get-tuple-element.38), channel_id=1, source_target_pairs={{0,2},{1,3},{2,0},{3,1},{4,6},{5,7},{6,4},{7,5},{8,10},{9,11},{10,... | collective-permute-start | bytes 3080 | tf_op jit(solution)/shard_map/ppermute | solution.py:50
  17.9 15.1 %collective-permute-start.2 = (s32[128,2]{0,1:T(2,128)S(1)}, s32[128,2]{0,1:T(2,128)S(1)}, u32[]{:S(2)}, u32[]{:S(2)}) collective-permute-start(s32[128,2]{0,1:T(2,128)S(1)} %get-tuple-element.38), channel_id=1, source_target_pairs={{0,1},{1,2},{2,3},{3,0},{4,5},{5,6},{6,7},{7,4},{8,9},{9,10},{10,1... | collective-permute-start | bytes 3080 | tf_op jit(solution)/shard_map/ppermute | solution.py:50
  38.1 19.8 %collective-permute-start.11 = (bf16[512,768]{1,0:T(8,128)(2,1)S(1)}, bf16[512,768]{1,0:T(8,128)(2,1)S(1)}, u32[]{:S(2)}, u32[]{:S(2)}) collective-permute-start(bf16[512,768]{1,0:T(8,128)(2,1)S(1)} %fusion.21), channel_id=1, source_target_pairs={{0,8},{4,12},{8,0},{12,4},{1,9},{5,13},{9,1},{13,5},{2,10},{6,14},... | collective-permute-start | bytes 2359304 | tf_op jit(solution)/shard_map/ppermute | solution.py:138
  39.5 18.4 %collective-permute-start.3 = (s32[2,255]{1,0:T(2,128)S(1)}, s32[2,255]{1,0:T(2,128)S(1)}, u32[]{:S(2)}, u32[]{:S(2)}) collective-permute-start(s32[2,255]{1,0:T(2,128)S(1)} %get-tuple-element.36), channel_id=1, source_target_pairs={{0,16},{16,32},{32,48},{48,64},{64,80},{80,96},{96,112},{1,17},{17... | collective-permute-start | bytes 6128 | tf_op jit(solution)/shard_map/ppermute | solution.py:21
  40.8 17.1 %collective-permute-start.4 = (s32[2,255]{1,0:T(2,128)S(1)}, s32[2,255]{1,0:T(2,128)S(1)}, u32[]{:S(2)}, u32[]{:S(2)}) collective-permute-start(s32[2,255]{1,0:T(2,128)S(1)} %get-tuple-element.37), channel_id=1, source_target_pairs={{16,0},{32,16},{48,32},{64,48},{80,64},{96,80},{112,96},{17,1},{33... | collective-permute-start | bytes 6128 | tf_op jit(solution)/shard_map/ppermute | solution.py:23
  97.5 15.4 %collective-permute-start.17 = (bf16[128,1024]{1,0:T(8,128)(2,1)S(1)}, bf16[128,1024]{1,0:T(8,128)(2,1)S(1)}, u32[]{:S(2)}, u32[]{:S(2)}) collective-permute-start(bf16[128,1024]{1,0:T(8,128)(2,1)S(1)} %get-tuple-element.24), channel_id=1, source_target_pairs={{0,1},{1,2},{2,3},{3,0},{4,5},{5,6},{6,7},{7,4},{8,9},{9,10},{10,1... | collective-permute-start | bytes 786440 | tf_op jit(solution)/shard_map/ppermute | solution.py:256
  98.1 14.8 %collective-permute-start.18 = (bf16[128,1024]{1,0:T(8,128)(2,1)S(1)}, bf16[128,1024]{1,0:T(8,128)(2,1)S(1)}, u32[]{:S(2)}, u32[]{:S(2)}) collective-permute-start(bf16[128,1024]{1,0:T(8,128)(2,1)S(1)} %get-tuple-element.26), channel_id=1, source_target_pairs={{0,2},{1,3},{2,0},{3,1},{4,6},{5,7},{6,4},{7,5},{8,10},{9,11},{10,... | collective-permute-start | bytes 786440 | tf_op jit(solution)/shard_map/ppermute | solution.py:256
  134.3 19.8 %collective-permute-start.23 = (bf16[192,1024]{1,0:T(8,128)(2,1)S(1)}, bf16[192,1024]{1,0:T(8,128)(2,1)S(1)}, u32[]{:S(2)}, u32[]{:S(2)}) collective-permute-start(bf16[192,1024]{1,0:T(8,128)(2,1)S(1)} %multiply_convert_fusion.refs_0_), channel_id=1, source_target_pairs={{0,1},{1,2},{2,3},{3,0},{4,5},{5,6},{6,7},{7,4},{8,9},{9,10},{10,1... | collective-permute-start | bytes 1179656 | tf_op jit(solution)/shard_map/ppermute | solution.py:160
  134.3 19.7 %collective-permute-start.24 = (bf16[192,1024]{1,0:T(8,128)(2,1)S(1)}, bf16[192,1024]{1,0:T(8,128)(2,1)S(1)}, u32[]{:S(2)}, u32[]{:S(2)}) collective-permute-start(bf16[192,1024]{1,0:T(8,128)(2,1)S(1)} %multiply_convert_fusion.refs_0_), channel_id=1, source_target_pairs={{0,2},{1,3},{2,0},{3,1},{4,6},{5,7},{6,4},{7,5},{8,10},{9,11},{10,... | collective-permute-start | bytes 1179656 | tf_op jit(solution)/shard_map/ppermute | solution.py:160
  134.4 20.2 %collective-permute-start.25 = (bf16[192,1024]{1,0:T(8,128)(2,1)S(1)}, bf16[192,1024]{1,0:T(8,128)(2,1)S(1)}, u32[]{:S(2)}, u32[]{:S(2)}) collective-permute-start(bf16[192,1024]{1,0:T(8,128)(2,1)S(1)} %multiply_convert_fusion.refs_0_), channel_id=1, source_target_pairs={{0,3},{1,0},{2,1},{3,2},{4,7},{5,4},{6,5},{7,6},{8,11},{9,8},{10,9... | collective-permute-start | bytes 1179656 | tf_op jit(solution)/shard_map/ppermute | solution.py:160
  172.0 28.1 %collective-permute-start.27 = (bf16[768,768]{1,0:T(8,128)(2,1)S(1)}, bf16[768,768]{1,0:T(8,128)(2,1)S(1)}, u32[]{:S(2)}, u32[]{:S(2)}) collective-permute-start(bf16[768,768]{1,0:T(8,128)(2,1)S(1)} %fusion.20), channel_id=1, source_target_pairs={{0,8},{4,12},{8,0},{12,4},{1,9},{5,13},{9,1},{13,5},{2,10},{6,14},... | collective-permute-start | bytes 3538952 | tf_op jit(solution)/shard_map/ppermute | solution.py:138
  202.0 24.0 %collective-permute-start.28 = (bf16[768,512]{1,0:T(8,128)(2,1)}, bf16[768,512]{1,0:T(8,128)(2,1)}, u32[]{:S(2)}, u32[]{:S(2)}) collective-permute-start(bf16[768,512]{1,0:T(8,128)(2,1)} %get-tuple-element.23), channel_id=1, source_target_pairs={{0,16},{16,32},{32,48},{48,64},{64,80},{80,96},{96,112},{1,17},{17... | collective-permute-start | bytes 2359304 | tf_op jit(solution)/shard_map/ppermute | solution.py:469
  203.3 27.9 %collective-permute-start.29 = (bf16[768,512]{1,0:T(8,128)(2,1)}, bf16[768,512]{1,0:T(8,128)(2,1)}, u32[]{:S(2)}, u32[]{:S(2)}) collective-permute-start(bf16[768,512]{1,0:T(8,128)(2,1)} %get-tuple-element.23), channel_id=1, source_target_pairs={{0,32},{16,48},{32,64},{48,80},{64,96},{80,112},{1,33},{17,49},{33... | collective-permute-start | bytes 2359304 | tf_op jit(solution)/shard_map/ppermute | solution.py:469
  204.6 43.2 %collective-permute-start.30 = (bf16[768,512]{1,0:T(8,128)(2,1)}, bf16[768,512]{1,0:T(8,128)(2,1)}, u32[]{:S(2)}, u32[]{:S(2)}) collective-permute-start(bf16[768,512]{1,0:T(8,128)(2,1)} %get-tuple-element.23), channel_id=1, source_target_pairs={{0,48},{16,64},{32,80},{48,96},{64,112},{1,49},{17,65},{33,81},{49... | collective-permute-start | bytes 2359304 | tf_op jit(solution)/shard_map/ppermute | solution.py:469
  205.9 44.0 %collective-permute-start.31 = (bf16[768,512]{1,0:T(8,128)(2,1)}, bf16[768,512]{1,0:T(8,128)(2,1)S(1)}, u32[]{:S(2)}, u32[]{:S(2)}) collective-permute-start(bf16[768,512]{1,0:T(8,128)(2,1)} %get-tuple-element.23), channel_id=1, source_target_pairs={{0,64},{16,80},{32,96},{48,112},{1,65},{17,81},{33,97},{49,113},{2... | collective-permute-start | bytes 2359304 | tf_op jit(solution)/shard_map/ppermute | solution.py:469
  207.2 59.0 %collective-permute-start.32 = (bf16[768,512]{1,0:T(8,128)(2,1)}, bf16[768,512]{1,0:T(8,128)(2,1)S(1)}, u32[]{:S(2)}, u32[]{:S(2)}) collective-permute-start(bf16[768,512]{1,0:T(8,128)(2,1)} %get-tuple-element.23), channel_id=1, source_target_pairs={{0,80},{16,96},{32,112},{1,81},{17,97},{33,113},{2,82},{18,98},{34... | collective-permute-start | bytes 2359304 | tf_op jit(solution)/shard_map/ppermute | solution.py:469
  226.0 61.0 %collective-permute-start.33 = (bf16[768,512]{1,0:T(8,128)(2,1)}, bf16[768,512]{1,0:T(8,128)(2,1)S(1)}, u32[]{:S(2)}, u32[]{:S(2)}) collective-permute-start(bf16[768,512]{1,0:T(8,128)(2,1)} %get-tuple-element.23), channel_id=1, source_target_pairs={{0,96},{16,112},{1,97},{17,113},{2,98},{18,114},{3,99},{19,115},{4... | collective-permute-start | bytes 2359304 | tf_op jit(solution)/shard_map/ppermute | solution.py:469
  231.1 56.7 %collective-permute-start.34 = (bf16[768,512]{1,0:T(8,128)(2,1)}, bf16[768,512]{1,0:T(8,128)(2,1)S(1)}, u32[]{:S(2)}, u32[]{:S(2)}) collective-permute-start(bf16[768,512]{1,0:T(8,128)(2,1)} %get-tuple-element.23), channel_id=1, source_target_pairs={{0,112},{1,113},{2,114},{3,115},{4,116},{5,117},{6,118},{7,119},{8... | collective-permute-start | bytes 2359304 | tf_op jit(solution)/shard_map/ppermute | solution.py:469
  320.4 18.9 %collective-permute-start.37 = (bf16[768,256]{1,0:T(8,128)(2,1)}, bf16[768,256]{1,0:T(8,128)(2,1)S(1)}, u32[]{:S(2)}, u32[]{:S(2)}) collective-permute-start(bf16[768,256]{1,0:T(8,128)(2,1)} %shard_map.158.refs_0_), channel_id=1, source_target_pairs={{0,12},{4,8},{8,4},{12,0},{1,13},{5,9},{9,5},{13,1},{2,14},{6,10},... | collective-permute-start | bytes 1179656 | tf_op jit(solution)/shard_map/ppermute | solution.py:138
  347.1 20.9 %collective-permute-start.38 = (bf16[192,1024]{1,0:T(8,128)(2,1)S(1)}, bf16[192,1024]{1,0:T(8,128)(2,1)S(1)}, u32[]{:S(2)}, u32[]{:S(2)}) collective-permute-start(bf16[192,1024]{1,0:T(8,128)(2,1)S(1)} %get-tuple-element.19), channel_id=1, source_target_pairs={{0,1},{1,2},{2,3},{3,0},{4,5},{5,6},{6,7},{7,4},{8,9},{9,10},{10,1... | collective-permute-start | bytes 1179656 | tf_op jit(solution)/shard_map/ppermute | solution.py:256
  347.1 20.8 %collective-permute-start.39 = (bf16[192,1024]{1,0:T(8,128)(2,1)S(1)}, bf16[192,1024]{1,0:T(8,128)(2,1)S(1)}, u32[]{:S(2)}, u32[]{:S(2)}) collective-permute-start(bf16[192,1024]{1,0:T(8,128)(2,1)S(1)} %get-tuple-element.21), channel_id=1, source_target_pairs={{0,2},{1,3},{2,0},{3,1},{4,6},{5,7},{6,4},{7,5},{8,10},{9,11},{10,... | collective-permute-start | bytes 1179656 | tf_op jit(solution)/shard_map/ppermute | solution.py:256
  350.0 18.6 %collective-permute-start.40 = (bf16[192,1024]{1,0:T(8,128)(2,1)S(1)}, bf16[192,1024]{1,0:T(8,128)(2,1)S(1)}, u32[]{:S(2)}, u32[]{:S(2)}) collective-permute-start(bf16[192,1024]{1,0:T(8,128)(2,1)S(1)} %get-tuple-element.20), channel_id=1, source_target_pairs={{0,3},{1,0},{2,1},{3,2},{4,7},{5,4},{6,5},{7,6},{8,11},{9,8},{10,9... | collective-permute-start | bytes 1179656 | tf_op jit(solution)/shard_map/ppermute | solution.py:256
  (40 other events, 406.4 us)

commit v6 on v5

--- a/solution.py
+++ b/solution.py
@@ -222,7 +222,6 @@
     def body(index_ref, *refs):
         piece_refs = refs[:row_count]
         w_ref = refs[row_count]
-        o_ref = refs[-1]
         own = index_ref[0]
         place = index_ref[1]
         for s in range(col_count):
@@ -237,19 +236,19 @@
                     preferred_element_type=jnp.float32,
                 )
                 total = part if total is None else total + part
-            o_ref[s] = total.astype(o_ref.dtype)
+            refs[row_count + 1 + s][...] = total.astype(jnp.bfloat16)
 
     grid_spec = pltpu.PrefetchScalarGridSpec(
         num_scalar_prefetch=1,
         grid=(1,),
         in_specs=[pl.BlockSpec((count, width), lambda i, x: (0, 0)) for _ in pieces]
         + [pl.BlockSpec(weight.shape, lambda i, x: (0, 0))],
-        out_specs=pl.BlockSpec((col_count, rows, weight.shape[1]), lambda i, x: (0, 0, 0)),
+        out_specs=[pl.BlockSpec((rows, weight.shape[1]), lambda i, x: (0, 0)) for _ in range(col_count)],
     )
     parts = pl.pallas_call(
         body,
         grid_spec=grid_spec,
-        out_shape=jax.ShapeDtypeStruct((col_count, rows, weight.shape[1]), jnp.bfloat16),
+        out_shape=[jax.ShapeDtypeStruct((rows, weight.shape[1]), jnp.bfloat16) for _ in range(col_count)],
     )(index, *pieces, weight)
     total = parts[0].astype(jnp.float32)
     for s in range(1, col_count):

time: 372 us -> 369 us (level)
  no operation moved by 1% of the time
where the time goes in v6:
time: 369 us; the launch traced here: 368 us
  waiting for transfers between devices  196 us (53%)
  Pallas kernels  65.4 us (18%)
  starting transfers between devices  64.5 us (17%)
  local copies, waits for them, and re-layouts  21.7 us (6%)
  other arithmetic  17.3 us (5%)
    ppermute x14, waiting for transfers between devices, flip(): return lax.ppermute(values, axis, [(j, j ^ bit) for j in range(count)])  71.2 us
    ppermute x7, waiting for transfers between devices, per_device(): lax.ppermute(keyvals, 'req', [(j, j + s) for j in range(req_count - s)])  61 us
    pallas_call x2, Pallas kernels, causal_attend(): pl.pallas_call(body, grid_spec=grid_spec, out_shape=out_shape)  37.4 us
    ppermute x6, waiting for transfers between devices, out_project_heads(): lax.ppermute(parts[s], 'col', [(j, (j + s) % col_count) for j in range(co...  29 us
    ppermute x6, waiting for transfers between devices, received(): lax.ppermute(values, axis, [(j, (j + s) % count) for j in range(count)])  19.2 us
    pallas_call x2, Pallas kernels, head_project(): pl.pallas_call(body, grid_spec=grid_spec, out_shape=[shape, shape])  18 us
    unnamed x58, local copies, waits for them, and re-layouts  13.1 us
    ppermute x2, starting transfers between devices, with_halo(): lax.ppermute(head, axis, [((i + 1) % count, i) for i in range(ends)])  12.3 us
  transfers between devices with their start and end apart: 41, of which 28 were waited for; matrix products, arithmetic and copies ran while one was open for 5% of the time, Pallas kernels for 4%

profile of v6, /device:TPU:28, one launch (start us, length us, event | category | flops | bytes accessed | tf_op | source)
XLA Modules:
  0.0 367.8 jit_solution(980303746116632457)
XLA Ops:
  24.8 8.0 %shard_map.154 = (bf16[2,512,768]{2,1,0:T(8,128)(2,1)}, bf16[2,512,768]{2,1,0:T(8,128)(2,1)}) custom-call(s32[2]{0:T(128)} %pad_add_fusion.3.index_ref, bf16[128,1024]{1,0:T(8,128)(2,1)} %copy-done.6, bf16[128,1024]{1,0:T(8,128)(2,1)} %copy-done.16, bf16[128,1024]{1,0:T(8,128)(2,1)} %copy-done.17, bf16[128,1024]{1,0:T(8,128)(2,1)} %copy-done.18, ...), custom_call_target="tpu_custom_call" | custom-call | tf_op jit(solution)/shard_map/pallas_call | solution.py:206
  40.8 6.1 %collective-permute-start.4 = (s32[2,255]{1,0:T(2,128)S(1)}, s32[2,255]{1,0:T(2,128)S(1)}, u32[]{:S(2)}, u32[]{:S(2)}) collective-permute-start(s32[2,255]{1,0:T(2,128)S(1)} %get-tuple-element.47), channel_id=1, source_target_pairs={{16,0},{32,16},{48,32},{64,48},{80,64},{96,80},{112,96},{17,1},{33... | collective-permute-start | bytes 6128 | tf_op jit(solution)/shard_map/ppermute | solution.py:23
  47.4 10.4 %collective-permute-done.3 = s32[2,255]{1,0:T(2,128)S(1)} collective-permute-done((s32[2,255]{1,0:T(2,128)S(1)}, s32[2,255]{1,0:T(2,128)S(1)}, u32[]{:S(2)}, u32[]{:S(2)}) %collective-permute-start.3) | collective-permute-done | bytes 2072 | tf_op jit(solution)/shard_map/ppermute | solution.py:21
  60.9 6.2 %collective-permute-start.13 = (bf16[2,255,256]{2,1,0:T(8,128)(2,1)S(1)}, bf16[2,255,256]{2,1,0:T(8,128)(2,1)S(1)}, u32[]{:S(2)}, u32[]{:S(2)}) collective-permute-start(bf16[2,255,256]{2,1,0:T(8,128)(2,1)S(1)} %get-tuple-element.43), channel_id=1, source_target_pairs={{16,0},{32,16},{48,32},{64,48},{80,64},{96,80},{112,96},{17,1},{33... | collective-permute-start | bytes 783368 | tf_op jit(solution)/shard_map/ppermute | solution.py:23
  79.3 6.7 %collective-permute-done.15.refs_2_ = bf16[512,256]{1,0:T(8,128)(2,1)S(1)} collective-permute-done((bf16[512,256]{1,0:T(8,128)(2,1)S(1)}, bf16[512,256]{1,0:T(8,128)(2,1)S(1)}, u32[]{:S(2)}, u32[]{:S(2)}) %collective-permute-start.15) | collective-permute-done | bytes 262176 | tf_op jit(solution)/shard_map/ppermute | solution.py:138
  86.0 4.7 %collective-permute-done.16.refs_3_ = bf16[512,256]{1,0:T(8,128)(2,1)S(1)} collective-permute-done((bf16[512,256]{1,0:T(8,128)(2,1)S(1)}, bf16[512,256]{1,0:T(8,128)(2,1)S(1)}, u32[]{:S(2)}, u32[]{:S(2)}) %collective-permute-start.16) | collective-permute-done | bytes 262176 | tf_op jit(solution)/shard_map/ppermute | solution.py:138
  91.4 4.6 %shard_map.155 = (bf16[128,1024]{1,0:T(8,128)(2,1)}, bf16[128,1024]{1,0:T(8,128)(2,1)}, bf16[128,1024]{1,0:T(8,128)(2,1)}, bf16[128,1024]{1,0:T(8,128)(2,1)}) custom-call(s32[2]{0:T(128)} %pad_add_fusion.2.index_ref, bf16[512,256]{1,0:T(8,128)(2,1)} %copy-done.5, bf16[512,256]{1,0:T(8,128)(2,1)} %copy-done.13, bf16[512,256]{1,0:T(8,128)(2,1)} %copy-done.14, ...), custom_call_target="tpu_custom_call" | custom-call | tf_op jit(solution)/shard_map/pallas_call | solution.py:248
  101.6 9.9 %collective-permute-done.17 = bf16[128,1024]{1,0:T(8,128)(2,1)S(1)} collective-permute-done((bf16[128,1024]{1,0:T(8,128)(2,1)}, bf16[128,1024]{1,0:T(8,128)(2,1)S(1)}, u32[]{:S(2)}, u32[]{:S(2)}) %collective-permute-start.17) | collective-permute-done | bytes 262176 | tf_op jit(solution)/shard_map/ppermute | solution.py:255
  113.3 8.5 %collective-permute-start.20 = (bf16[128,1024]{1,0:T(8,128)(2,1)S(1)}, bf16[128,1024]{1,0:T(8,128)(2,1)S(1)}, u32[]{:S(2)}, u32[]{:S(2)}) collective-permute-start(bf16[128,1024]{1,0:T(8,128)(2,1)S(1)} %fusion.25), channel_id=1, source_target_pairs={{1,0},{2,1},{3,2},{16,3},{17,16},{18,17},{19,18},{32,19},{33,32},{... | collective-permute-start | bytes 786440 | tf_op jit(solution)/shard_map/ppermute | solution.py:33
  123.2 4.3 %collective-permute-done.20 = bf16[128,1024]{1,0:T(8,128)(2,1)S(1)} collective-permute-done((bf16[128,1024]{1,0:T(8,128)(2,1)S(1)}, bf16[128,1024]{1,0:T(8,128)(2,1)S(1)}, u32[]{:S(2)}, u32[]{:S(2)}) %collective-permute-start.20) | collective-permute-done | bytes 262176 | tf_op jit(solution)/shard_map/ppermute | solution.py:33
  136.2 16.5 %collective-permute-done.23.refs_1_ = bf16[192,1024]{1,0:T(8,128)(2,1)S(1)} collective-permute-done((bf16[192,1024]{1,0:T(8,128)(2,1)S(1)}, bf16[192,1024]{1,0:T(8,128)(2,1)S(1)}, u32[]{:S(2)}, u32[]{:S(2)}) %collective-permute-start.23) | collective-permute-done | bytes 393248 | tf_op jit(solution)/shard_map/ppermute | solution.py:160
  154.3 10.0 %shard_map.156 = (bf16[2,768,768]{2,1,0:T(8,128)(2,1)}, bf16[2,768,768]{2,1,0:T(8,128)(2,1)}) custom-call(s32[2]{0:T(128)} %pad_add_fusion.3.index_ref, bf16[192,1024]{1,0:T(8,128)(2,1)} %copy-done.3, bf16[192,1024]{1,0:T(8,128)(2,1)} %copy-done.7, bf16[192,1024]{1,0:T(8,128)(2,1)} %copy-done.8, bf16[192,1024]{1,0:T(8,128)(2,1)} %copy-done.9, ...), custom_call_target="tpu_custom_call" | custom-call | tf_op jit(solution)/shard_map/pallas_call | solution.py:206
  164.4 4.7 %collective-permute-done.26 = bf16[2,768,768]{2,1,0:T(8,128)(2,1)S(1)} collective-permute-done((bf16[2,768,768]{2,1,0:T(8,128)(2,1)}, bf16[2,768,768]{2,1,0:T(8,128)(2,1)S(1)}, u32[]{:S(2)}, u32[]{:S(2)}) %collective-permute-start.26) | collective-permute-done | bytes 2359328 | tf_op jit(solution)/shard_map/ppermute | solution.py:138
  171.7 27.1 %collective-permute-done.27 = bf16[768,768]{1,0:T(8,128)(2,1)S(1)} collective-permute-done((bf16[768,768]{1,0:T(8,128)(2,1)S(1)}, bf16[768,768]{1,0:T(8,128)(2,1)S(1)}, u32[]{:S(2)}, u32[]{:S(2)}) %collective-permute-start.27) | collective-permute-done | bytes 1179680 | tf_op jit(solution)/shard_map/ppermute | solution.py:138
  207.2 6.8 %shard_map.157 = (f32[2,768,1]{2,1,0:T(8,128)}, f32[2,768,1]{2,1,0:T(8,128)}, f32[2,768,128]{2,1,0:T(8,128)}) custom-call(s32[1]{0:T(128)} %bitcast.19.place_ref, s32[1]{0:T(128)} %constant.96.clone.shift_ref, bf16[768,768]{1,0:T(8,128)(2,1)} %copy-done, bf16[1,768,512]{2,1,0:T(8,128)(2,1)} %get-tuple-element.35.kv_ref), custom_call_target="tpu_custom_call" | custom-call | tf_op jit(solution)/shard_map/pallas_call | solution.py:384
  214.0 10.7 %collective-permute-done.28 = bf16[768,512]{1,0:T(8,128)(2,1)} collective-permute-done((bf16[768,512]{1,0:T(8,128)(2,1)}, bf16[768,512]{1,0:T(8,128)(2,1)}, u32[]{:S(2)}, u32[]{:S(2)}) %collective-permute-start.28) | collective-permute-done | bytes 786464 | tf_op jit(solution)/shard_map/ppermute | solution.py:468
  233.2 13.2 %collective-permute-done.30 = bf16[768,512]{1,0:T(8,128)(2,1)} collective-permute-done((bf16[768,512]{1,0:T(8,128)(2,1)}, bf16[768,512]{1,0:T(8,128)(2,1)}, u32[]{:S(2)}, u32[]{:S(2)}) %collective-permute-start.30) | collective-permute-done | bytes 786464 | tf_op jit(solution)/shard_map/ppermute | solution.py:468
  249.4 15.4 %collective-permute-done.32 = bf16[768,512]{1,0:T(8,128)(2,1)S(1)} collective-permute-done((bf16[768,512]{1,0:T(8,128)(2,1)}, bf16[768,512]{1,0:T(8,128)(2,1)S(1)}, u32[]{:S(2)}, u32[]{:S(2)}) %collective-permute-start.32) | collective-permute-done | bytes 786464 | tf_op jit(solution)/shard_map/ppermute | solution.py:468
  265.8 19.8 %collective-permute-done.33 = bf16[768,512]{1,0:T(8,128)(2,1)S(1)} collective-permute-done((bf16[768,512]{1,0:T(8,128)(2,1)}, bf16[768,512]{1,0:T(8,128)(2,1)S(1)}, u32[]{:S(2)}, u32[]{:S(2)}) %collective-permute-start.33) | collective-permute-done | bytes 786464 | tf_op jit(solution)/shard_map/ppermute | solution.py:468
  287.5 30.6 %shard_map.158.refs_0_ = bf16[768,256]{1,0:T(8,128)(2,1)} custom-call(s32[1]{0:T(128)} %bitcast.19.place_ref, s32[7]{0:T(128)} %constant.97.clone.shift_ref, bf16[768,768]{1,0:T(8,128)(2,1)} %copy-done, bf16[7,768,512]{2,1,0:T(8,128)(2,1)} %bitcast_dynamic-update-slice_fusion.kv_ref, f32[2,768,1]{2,1,0:T(8,128)} %get-tuple-element.28.refs_0_, ...), custom_call_target="tpu_custom_call" | custom-call | tf_op jit(solution)/shard_map/pallas_call | solution.py:384
  320.1 10.2 %collective-permute-done.36.refs_2_ = bf16[768,256]{1,0:T(8,128)(2,1)S(1)} collective-permute-done((bf16[768,256]{1,0:T(8,128)(2,1)}, bf16[768,256]{1,0:T(8,128)(2,1)S(1)}, u32[]{:S(2)}, u32[]{:S(2)}) %collective-permute-start.36) | collective-permute-done | bytes 393248 | tf_op jit(solution)/shard_map/ppermute | solution.py:138
  330.2 7.7 %collective-permute-done.37.refs_3_ = bf16[768,256]{1,0:T(8,128)(2,1)S(1)} collective-permute-done((bf16[768,256]{1,0:T(8,128)(2,1)}, bf16[768,256]{1,0:T(8,128)(2,1)S(1)}, u32[]{:S(2)}, u32[]{:S(2)}) %collective-permute-start.37) | collective-permute-done | bytes 393248 | tf_op jit(solution)/shard_map/ppermute | solution.py:138
  338.7 5.4 %shard_map.159 = (bf16[192,1024]{1,0:T(8,128)(2,1)}, bf16[192,1024]{1,0:T(8,128)(2,1)}, bf16[192,1024]{1,0:T(8,128)(2,1)}, bf16[192,1024]{1,0:T(8,128)(2,1)}) custom-call(s32[2]{0:T(128)} %pad_add_fusion.2.index_ref, bf16[768,256]{1,0:T(8,128)(2,1)} %shard_map.158.refs_0_, bf16[768,256]{1,0:T(8,128)(2,1)} %copy-done.10, bf16[768,256]{1,0:T(8,128)(2,1)} %copy-done.11, ...), custom_call_target="tpu_custom_call" | custom-call | tf_op jit(solution)/shard_map/pallas_call | solution.py:248
  347.3 17.8 %collective-permute-done.38 = bf16[192,1024]{1,0:T(8,128)(2,1)S(1)} collective-permute-done((bf16[192,1024]{1,0:T(8,128)(2,1)}, bf16[192,1024]{1,0:T(8,128)(2,1)S(1)}, u32[]{:S(2)}, u32[]{:S(2)}) %collective-permute-start.38) | collective-permute-done | bytes 393248 | tf_op jit(solution)/shard_map/ppermute | solution.py:255
  (182 shorter events, 101.8 us)
Async XLA Ops:
  8.9 14.5 %collective-permute-start.8 = (bf16[128,1024]{1,0:T(8,128)(2,1)S(1)}, bf16[128,1024]{1,0:T(8,128)(2,1)S(1)}, u32[]{:S(2)}, u32[]{:S(2)}) collective-permute-start(bf16[128,1024]{1,0:T(8,128)(2,1)S(1)} %fusion.24.refs_0_), channel_id=1, source_target_pairs={{0,2},{1,3},{2,0},{3,1},{4,6},{5,7},{6,4},{7,5},{8,10},{9,11},{10,... | collective-permute-start | bytes 786440 | tf_op jit(solution)/shard_map/ppermute | solution.py:160
  14.2 18.8 %collective-permute-start = (s32[128,2]{0,1:T(2,128)S(1)}, s32[128,2]{0,1:T(2,128)S(1)}, u32[]{:S(2)}, u32[]{:S(2)}) collective-permute-start(s32[128,2]{0,1:T(2,128)S(1)} %get-tuple-element.48), channel_id=1, source_target_pairs={{0,3},{1,0},{2,1},{3,2},{4,7},{5,4},{6,5},{7,6},{8,11},{9,8},{10,9... | collective-permute-start | bytes 3080 | tf_op jit(solution)/shard_map/ppermute | solution.py:50
  14.2 18.8 %collective-permute-start.1 = (s32[128,2]{0,1:T(2,128)S(1)}, s32[128,2]{0,1:T(2,128)S(1)}, u32[]{:S(2)}, u32[]{:S(2)}) collective-permute-start(s32[128,2]{0,1:T(2,128)S(1)} %get-tuple-element.48), channel_id=1, source_target_pairs={{0,2},{1,3},{2,0},{3,1},{4,6},{5,7},{6,4},{7,5},{8,10},{9,11},{10,... | collective-permute-start | bytes 3080 | tf_op jit(solution)/shard_map/ppermute | solution.py:50
  17.9 15.1 %collective-permute-start.2 = (s32[128,2]{0,1:T(2,128)S(1)}, s32[128,2]{0,1:T(2,128)S(1)}, u32[]{:S(2)}, u32[]{:S(2)}) collective-permute-start(s32[128,2]{0,1:T(2,128)S(1)} %get-tuple-element.48), channel_id=1, source_target_pairs={{0,1},{1,2},{2,3},{3,0},{4,5},{5,6},{6,7},{7,4},{8,9},{9,10},{10,1... | collective-permute-start | bytes 3080 | tf_op jit(solution)/shard_map/ppermute | solution.py:50
  38.1 19.8 %collective-permute-start.11 = (bf16[512,768]{1,0:T(8,128)(2,1)S(1)}, bf16[512,768]{1,0:T(8,128)(2,1)S(1)}, u32[]{:S(2)}, u32[]{:S(2)}) collective-permute-start(bf16[512,768]{1,0:T(8,128)(2,1)S(1)} %fusion.21), channel_id=1, source_target_pairs={{0,8},{4,12},{8,0},{12,4},{1,9},{5,13},{9,1},{13,5},{2,10},{6,14},... | collective-permute-start | bytes 2359304 | tf_op jit(solution)/shard_map/ppermute | solution.py:138
  39.5 18.4 %collective-permute-start.3 = (s32[2,255]{1,0:T(2,128)S(1)}, s32[2,255]{1,0:T(2,128)S(1)}, u32[]{:S(2)}, u32[]{:S(2)}) collective-permute-start(s32[2,255]{1,0:T(2,128)S(1)} %get-tuple-element.46), channel_id=1, source_target_pairs={{0,16},{16,32},{32,48},{48,64},{64,80},{80,96},{96,112},{1,17},{17... | collective-permute-start | bytes 6128 | tf_op jit(solution)/shard_map/ppermute | solution.py:21
  40.8 17.1 %collective-permute-start.4 = (s32[2,255]{1,0:T(2,128)S(1)}, s32[2,255]{1,0:T(2,128)S(1)}, u32[]{:S(2)}, u32[]{:S(2)}) collective-permute-start(s32[2,255]{1,0:T(2,128)S(1)} %get-tuple-element.47), channel_id=1, source_target_pairs={{16,0},{32,16},{48,32},{64,48},{80,64},{96,80},{112,96},{17,1},{33... | collective-permute-start | bytes 6128 | tf_op jit(solution)/shard_map/ppermute | solution.py:23
  96.0 15.5 %collective-permute-start.17 = (bf16[128,1024]{1,0:T(8,128)(2,1)}, bf16[128,1024]{1,0:T(8,128)(2,1)S(1)}, u32[]{:S(2)}, u32[]{:S(2)}) collective-permute-start(bf16[128,1024]{1,0:T(8,128)(2,1)} %get-tuple-element.23), channel_id=1, source_target_pairs={{0,1},{1,2},{2,3},{3,0},{4,5},{5,6},{6,7},{7,4},{8,9},{9,10},{10,1... | collective-permute-start | bytes 786440 | tf_op jit(solution)/shard_map/ppermute | solution.py:255
  96.5 15.0 %collective-permute-start.18 = (bf16[128,1024]{1,0:T(8,128)(2,1)}, bf16[128,1024]{1,0:T(8,128)(2,1)S(1)}, u32[]{:S(2)}, u32[]{:S(2)}) collective-permute-start(bf16[128,1024]{1,0:T(8,128)(2,1)} %get-tuple-element.24), channel_id=1, source_target_pairs={{0,2},{1,3},{2,0},{3,1},{4,6},{5,7},{6,4},{7,5},{8,10},{9,11},{10,... | collective-permute-start | bytes 786440 | tf_op jit(solution)/shard_map/ppermute | solution.py:255
  132.9 19.8 %collective-permute-start.23 = (bf16[192,1024]{1,0:T(8,128)(2,1)S(1)}, bf16[192,1024]{1,0:T(8,128)(2,1)S(1)}, u32[]{:S(2)}, u32[]{:S(2)}) collective-permute-start(bf16[192,1024]{1,0:T(8,128)(2,1)S(1)} %multiply_convert_fusion.refs_0_), channel_id=1, source_target_pairs={{0,1},{1,2},{2,3},{3,0},{4,5},{5,6},{6,7},{7,4},{8,9},{9,10},{10,1... | collective-permute-start | bytes 1179656 | tf_op jit(solution)/shard_map/ppermute | solution.py:160
  133.0 19.7 %collective-permute-start.24 = (bf16[192,1024]{1,0:T(8,128)(2,1)S(1)}, bf16[192,1024]{1,0:T(8,128)(2,1)S(1)}, u32[]{:S(2)}, u32[]{:S(2)}) collective-permute-start(bf16[192,1024]{1,0:T(8,128)(2,1)S(1)} %multiply_convert_fusion.refs_0_), channel_id=1, source_target_pairs={{0,2},{1,3},{2,0},{3,1},{4,6},{5,7},{6,4},{7,5},{8,10},{9,11},{10,... | collective-permute-start | bytes 1179656 | tf_op jit(solution)/shard_map/ppermute | solution.py:160
  133.1 20.2 %collective-permute-start.25 = (bf16[192,1024]{1,0:T(8,128)(2,1)S(1)}, bf16[192,1024]{1,0:T(8,128)(2,1)S(1)}, u32[]{:S(2)}, u32[]{:S(2)}) collective-permute-start(bf16[192,1024]{1,0:T(8,128)(2,1)S(1)} %multiply_convert_fusion.refs_0_), channel_id=1, source_target_pairs={{0,3},{1,0},{2,1},{3,2},{4,7},{5,4},{6,5},{7,6},{8,11},{9,8},{10,9... | collective-permute-start | bytes 1179656 | tf_op jit(solution)/shard_map/ppermute | solution.py:160
  170.7 28.1 %collective-permute-start.27 = (bf16[768,768]{1,0:T(8,128)(2,1)S(1)}, bf16[768,768]{1,0:T(8,128)(2,1)S(1)}, u32[]{:S(2)}, u32[]{:S(2)}) collective-permute-start(bf16[768,768]{1,0:T(8,128)(2,1)S(1)} %fusion.20), channel_id=1, source_target_pairs={{0,8},{4,12},{8,0},{12,4},{1,9},{5,13},{9,1},{13,5},{2,10},{6,14},... | collective-permute-start | bytes 3538952 | tf_op jit(solution)/shard_map/ppermute | solution.py:138
  200.7 24.0 %collective-permute-start.28 = (bf16[768,512]{1,0:T(8,128)(2,1)}, bf16[768,512]{1,0:T(8,128)(2,1)}, u32[]{:S(2)}, u32[]{:S(2)}) collective-permute-start(bf16[768,512]{1,0:T(8,128)(2,1)} %get-tuple-element.36), channel_id=1, source_target_pairs={{0,16},{16,32},{32,48},{48,64},{64,80},{80,96},{96,112},{1,17},{17... | collective-permute-start | bytes 2359304 | tf_op jit(solution)/shard_map/ppermute | solution.py:468
  202.0 27.8 %collective-permute-start.29 = (bf16[768,512]{1,0:T(8,128)(2,1)}, bf16[768,512]{1,0:T(8,128)(2,1)}, u32[]{:S(2)}, u32[]{:S(2)}) collective-permute-start(bf16[768,512]{1,0:T(8,128)(2,1)} %get-tuple-element.36), channel_id=1, source_target_pairs={{0,32},{16,48},{32,64},{48,80},{64,96},{80,112},{1,33},{17,49},{33... | collective-permute-start | bytes 2359304 | tf_op jit(solution)/shard_map/ppermute | solution.py:468
  203.3 43.2 %collective-permute-start.30 = (bf16[768,512]{1,0:T(8,128)(2,1)}, bf16[768,512]{1,0:T(8,128)(2,1)}, u32[]{:S(2)}, u32[]{:S(2)}) collective-permute-start(bf16[768,512]{1,0:T(8,128)(2,1)} %get-tuple-element.36), channel_id=1, source_target_pairs={{0,48},{16,64},{32,80},{48,96},{64,112},{1,49},{17,65},{33,81},{49... | collective-permute-start | bytes 2359304 | tf_op jit(solution)/shard_map/ppermute | solution.py:468
  204.6 43.9 %collective-permute-start.31 = (bf16[768,512]{1,0:T(8,128)(2,1)}, bf16[768,512]{1,0:T(8,128)(2,1)S(1)}, u32[]{:S(2)}, u32[]{:S(2)}) collective-permute-start(bf16[768,512]{1,0:T(8,128)(2,1)} %get-tuple-element.36), channel_id=1, source_target_pairs={{0,64},{16,80},{32,96},{48,112},{1,65},{17,81},{33,97},{49,113},{2... | collective-permute-start | bytes 2359304 | tf_op jit(solution)/shard_map/ppermute | solution.py:468
  205.9 59.0 %collective-permute-start.32 = (bf16[768,512]{1,0:T(8,128)(2,1)}, bf16[768,512]{1,0:T(8,128)(2,1)S(1)}, u32[]{:S(2)}, u32[]{:S(2)}) collective-permute-start(bf16[768,512]{1,0:T(8,128)(2,1)} %get-tuple-element.36), channel_id=1, source_target_pairs={{0,80},{16,96},{32,112},{1,81},{17,97},{33,113},{2,82},{18,98},{34... | collective-permute-start | bytes 2359304 | tf_op jit(solution)/shard_map/ppermute | solution.py:468
  224.6 61.0 %collective-permute-start.33 = (bf16[768,512]{1,0:T(8,128)(2,1)}, bf16[768,512]{1,0:T(8,128)(2,1)S(1)}, u32[]{:S(2)}, u32[]{:S(2)}) collective-permute-start(bf16[768,512]{1,0:T(8,128)(2,1)} %get-tuple-element.36), channel_id=1, source_target_pairs={{0,96},{16,112},{1,97},{17,113},{2,98},{18,114},{3,99},{19,115},{4... | collective-permute-start | bytes 2359304 | tf_op jit(solution)/shard_map/ppermute | solution.py:468
  229.8 56.7 %collective-permute-start.34 = (bf16[768,512]{1,0:T(8,128)(2,1)}, bf16[768,512]{1,0:T(8,128)(2,1)S(1)}, u32[]{:S(2)}, u32[]{:S(2)}) collective-permute-start(bf16[768,512]{1,0:T(8,128)(2,1)} %get-tuple-element.36), channel_id=1, source_target_pairs={{0,112},{1,113},{2,114},{3,115},{4,116},{5,117},{6,118},{7,119},{8... | collective-permute-start | bytes 2359304 | tf_op jit(solution)/shard_map/ppermute | solution.py:468
  319.1 18.8 %collective-permute-start.37 = (bf16[768,256]{1,0:T(8,128)(2,1)}, bf16[768,256]{1,0:T(8,128)(2,1)S(1)}, u32[]{:S(2)}, u32[]{:S(2)}) collective-permute-start(bf16[768,256]{1,0:T(8,128)(2,1)} %shard_map.158.refs_0_), channel_id=1, source_target_pairs={{0,12},{4,8},{8,4},{12,0},{1,13},{5,9},{9,5},{13,1},{2,14},{6,10},... | collective-permute-start | bytes 1179656 | tf_op jit(solution)/shard_map/ppermute | solution.py:138
  344.0 21.1 %collective-permute-start.38 = (bf16[192,1024]{1,0:T(8,128)(2,1)}, bf16[192,1024]{1,0:T(8,128)(2,1)S(1)}, u32[]{:S(2)}, u32[]{:S(2)}) collective-permute-start(bf16[192,1024]{1,0:T(8,128)(2,1)} %get-tuple-element.32), channel_id=1, source_target_pairs={{0,1},{1,2},{2,3},{3,0},{4,5},{5,6},{6,7},{7,4},{8,9},{9,10},{10,1... | collective-permute-start | bytes 1179656 | tf_op jit(solution)/shard_map/ppermute | solution.py:255
  344.0 21.1 %collective-permute-start.39 = (bf16[192,1024]{1,0:T(8,128)(2,1)}, bf16[192,1024]{1,0:T(8,128)(2,1)S(1)}, u32[]{:S(2)}, u32[]{:S(2)}) collective-permute-start(bf16[192,1024]{1,0:T(8,128)(2,1)} %get-tuple-element.33), channel_id=1, source_target_pairs={{0,2},{1,3},{2,0},{3,1},{4,6},{5,7},{6,4},{7,5},{8,10},{9,11},{10,... | collective-permute-start | bytes 1179656 | tf_op jit(solution)/shard_map/ppermute | solution.py:255
  347.0 18.8 %collective-permute-start.40 = (bf16[192,1024]{1,0:T(8,128)(2,1)}, bf16[192,1024]{1,0:T(8,128)(2,1)S(1)}, u32[]{:S(2)}, u32[]{:S(2)}) collective-permute-start(bf16[192,1024]{1,0:T(8,128)(2,1)} %get-tuple-element.34), channel_id=1, source_target_pairs={{0,3},{1,0},{2,1},{3,2},{4,7},{5,4},{6,5},{7,6},{8,11},{9,8},{10,9... | collective-permute-start | bytes 1179656 | tf_op jit(solution)/shard_map/ppermute | solution.py:255
  (40 other events, 424.1 us)

commit v7 on v6

--- a/solution.py
+++ b/solution.py
@@ -138,11 +138,14 @@
     return lax.ppermute(values, axis, [(j, j ^ bit) for j in range(count)])
 
 
-def scatter_row(keep, send):
+def scatter_row(keep, send, cut=None):
     sent = flip(send, "row", 1)
     near = keep[0].astype(jnp.float32) + sent[0].astype(jnp.float32)
     far = (keep[1].astype(jnp.float32) + sent[1].astype(jnp.float32)).astype(jnp.bfloat16)
-    return (near + flip(far, "row", 2).astype(jnp.float32)).astype(jnp.bfloat16)
+    total = near + flip(far, "row", 2).astype(jnp.float32)
+    if cut is None:
+        return total.astype(jnp.bfloat16)
+    return total[:, :cut].astype(jnp.bfloat16), total[:, cut:].astype(jnp.bfloat16)
 
 
 def gather_row(values):
@@ -162,7 +165,7 @@
     ]
 
 
-def head_project(pieces, weights, axis):
+def head_project(pieces, weights, axis, cut=None):
     row_count = lax.axis_size("row")
     count = len(pieces)
     rows, depth = pieces[0].shape
@@ -208,7 +211,7 @@
         grid_spec=grid_spec,
         out_shape=[shape, shape],
     )(index, *pieces, *weights)
-    return scatter_row(keep, send)
+    return scatter_row(keep, send, cut)
 
 
 def out_project_heads(attended, weight):
@@ -261,7 +264,7 @@
 def causal_attend(proj, blocks, shifts, place, carry=None, last=True):
     diagonal = 0 in shifts
     count = proj.shape[0]
-    heads = proj.shape[1] // (3 * HD)
+    heads = proj.shape[1] // HD
     steps = blocks.shape[0]
     scale = HD ** (-0.5)
     shift_table = jnp.asarray(shifts, jnp.int32)
@@ -460,9 +463,8 @@
     carried = jnp.dot(onehot, near_rows, preferred_element_type=jnp.float32)
     mixed = (text_embed.astype(jnp.float32) + carried).astype(jnp.bfloat16)
     dec_cols = received(norm_local(mixed, dec_gain), "col")
-    dec_proj = head_project(dec_cols, (dec_wq, dec_wk, dec_wv), "col")
+    dec_proj, keyvals = head_project(dec_cols, (dec_wq, dec_wk, dec_wv), "col", local)
     dec_rows = dec_proj.shape[0]
-    keyvals = dec_proj[:, local:]
     req_count = lax.axis_size("req")
     earlier = [keyvals] + [
         lax.ppermute(keyvals, "req", [(j, j + s) for j in range(req_count - s)])

time: 369 us -> 368 us (level)
  starting transfers between devices: 64.5 us -> 54.2 us
  waiting for transfers between devices: 196 us -> 206 us
    ppermute x2, waiting for transfers between devices: 0.93 us -> 12.6 us  [with_halo(): lax.ppermute(head, axis, [((i + 1) % count, i) for i in range(ends)])]
    ppermute x2, starting transfers between devices: 12.3 us -> 7.52 us  [with_halo(): lax.ppermute(head, axis, [((i + 1) % count, i) for i in range(ends)])]
    ppermute x1, starting transfers between devices: 8.5 us -> 3.96 us  [passed_along(): return lax.ppermute(shard, axis, pairs)]
    unnamed x58 -> x56, local copies, waits for them, and re-layouts: 13.1 us -> 12 us
  transfers between devices with their start and end apart: 41 -> 41, of which waited for: 28 -> 30; matrix products, arithmetic and copies ran while one was open for 5% -> 5% of each run, Pallas kernels for 4% -> 4%
where the time goes in v7:
time: 368 us; the launch traced here: 367 us
  waiting for transfers between devices  206 us (56%)
  Pallas kernels  65.5 us (18%)
  starting transfers between devices  54.2 us (15%)
  local copies, waits for them, and re-layouts  21.3 us (6%)
  other arithmetic  17.3 us (5%)
    ppermute x14, waiting for transfers between devices, flip(): return lax.ppermute(values, axis, [(j, j ^ bit) for j in range(count)])  70.7 us
    ppermute x7, waiting for transfers between devices, per_device(): lax.ppermute(keyvals, 'req', [(j, j + s) for j in range(req_count - s)])  58.3 us
    pallas_call x2, Pallas kernels, causal_attend(): pl.pallas_call(body, grid_spec=grid_spec, out_shape=out_shape)  37.5 us
    ppermute x6, waiting for transfers between devices, out_project_heads(): lax.ppermute(parts[s], 'col', [(j, (j + s) % col_count) for j in range(co...  32.6 us
    ppermute x6, waiting for transfers between devices, received(): lax.ppermute(values, axis, [(j, (j + s) % count) for j in range(count)])  18.6 us
    pallas_call x2, Pallas kernels, head_project(): pl.pallas_call(body, grid_spec=grid_spec, out_shape=[shape, shape])  18.1 us
    ppermute x2, waiting for transfers between devices, with_halo(): lax.ppermute(head, axis, [((i + 1) % count, i) for i in range(ends)])  12.6 us
    unnamed x56, local copies, waits for them, and re-layouts  12 us
  transfers between devices with their start and end apart: 41, of which 30 were waited for; matrix products, arithmetic and copies ran while one was open for 5% of the time, Pallas kernels for 4%

profile of v7, /device:TPU:28, one launch (start us, length us, event | category | flops | bytes accessed | tf_op | source)
XLA Modules:
  0.0 367.3 jit_solution(8487377601130188047)
XLA Ops:
  24.8 8.0 %shard_map.154 = (bf16[2,512,768]{2,1,0:T(8,128)(2,1)}, bf16[2,512,768]{2,1,0:T(8,128)(2,1)}) custom-call(s32[2]{0:T(128)} %pad_add_fusion.3.index_ref, bf16[128,1024]{1,0:T(8,128)(2,1)} %copy-done.5, bf16[128,1024]{1,0:T(8,128)(2,1)} %copy-done.15, bf16[128,1024]{1,0:T(8,128)(2,1)} %copy-done.16, bf16[128,1024]{1,0:T(8,128)(2,1)} %copy-done.17, ...), custom_call_target="tpu_custom_call" | custom-call | tf_op jit(solution)/shard_map/pallas_call | solution.py:209
  44.1 12.5 %collective-permute-done.4 = s32[2,255]{1,0:T(2,128)S(1)} collective-permute-done((s32[2,255]{1,0:T(2,128)S(1)}, s32[2,255]{1,0:T(2,128)S(1)}, u32[]{:S(2)}, u32[]{:S(2)}) %collective-permute-start.4) | collective-permute-done | bytes 2072 | tf_op jit(solution)/shard_map/ppermute | solution.py:23
  59.6 4.8 %collective-permute-start.13 = (bf16[2,255,256]{2,1,0:T(8,128)(2,1)S(1)}, bf16[2,255,256]{2,1,0:T(8,128)(2,1)S(1)}, u32[]{:S(2)}, u32[]{:S(2)}) collective-permute-start(bf16[2,255,256]{2,1,0:T(8,128)(2,1)S(1)} %get-tuple-element.43), channel_id=1, source_target_pairs={{16,0},{32,16},{48,32},{64,48},{80,64},{96,80},{112,96},{17,1},{33... | collective-permute-start | bytes 783368 | tf_op jit(solution)/shard_map/ppermute | solution.py:23
  69.1 7.6 %collective-permute-done.12 = bf16[2,255,256]{2,1,0:T(8,128)(2,1)S(1)} collective-permute-done((bf16[2,255,256]{2,1,0:T(8,128)(2,1)S(1)}, bf16[2,255,256]{2,1,0:T(8,128)(2,1)S(1)}, u32[]{:S(2)}, u32[]{:S(2)}) %collective-permute-start.12) | collective-permute-done | bytes 261152 | tf_op jit(solution)/shard_map/ppermute | solution.py:21
  84.4 6.7 %collective-permute-done.15.refs_2_ = bf16[512,256]{1,0:T(8,128)(2,1)S(1)} collective-permute-done((bf16[512,256]{1,0:T(8,128)(2,1)S(1)}, bf16[512,256]{1,0:T(8,128)(2,1)S(1)}, u32[]{:S(2)}, u32[]{:S(2)}) %collective-permute-start.15) | collective-permute-done | bytes 262176 | tf_op jit(solution)/shard_map/ppermute | solution.py:138
  91.2 4.7 %collective-permute-done.16.refs_3_ = bf16[512,256]{1,0:T(8,128)(2,1)S(1)} collective-permute-done((bf16[512,256]{1,0:T(8,128)(2,1)S(1)}, bf16[512,256]{1,0:T(8,128)(2,1)S(1)}, u32[]{:S(2)}, u32[]{:S(2)}) %collective-permute-start.16) | collective-permute-done | bytes 262176 | tf_op jit(solution)/shard_map/ppermute | solution.py:138
  105.6 4.9 %collective-permute-done.19 = bf16[128,1024]{1,0:T(8,128)(2,1)S(1)} collective-permute-done((bf16[128,1024]{1,0:T(8,128)(2,1)}, bf16[128,1024]{1,0:T(8,128)(2,1)S(1)}, u32[]{:S(2)}, u32[]{:S(2)}) %collective-permute-start.19) | collective-permute-done | bytes 262176 | tf_op jit(solution)/shard_map/ppermute | solution.py:258
  113.5 4.6 %collective-permute-done.17 = bf16[128,1024]{1,0:T(8,128)(2,1)S(1)} collective-permute-done((bf16[128,1024]{1,0:T(8,128)(2,1)}, bf16[128,1024]{1,0:T(8,128)(2,1)S(1)}, u32[]{:S(2)}, u32[]{:S(2)}) %collective-permute-start.17) | collective-permute-done | bytes 262176 | tf_op jit(solution)/shard_map/ppermute | solution.py:258
  124.7 4.8 %collective-permute-done.20 = bf16[128,1024]{1,0:T(8,128)(2,1)S(1)} collective-permute-done((bf16[128,1024]{1,0:T(8,128)(2,1)S(1)}, bf16[128,1024]{1,0:T(8,128)(2,1)S(1)}, u32[]{:S(2)}, u32[]{:S(2)}) %collective-permute-start.20) | collective-permute-done | bytes 262176 | tf_op jit(solution)/shard_map/ppermute | solution.py:33
  138.7 15.9 %collective-permute-done.23.refs_1_ = bf16[192,1024]{1,0:T(8,128)(2,1)S(1)} collective-permute-done((bf16[192,1024]{1,0:T(8,128)(2,1)S(1)}, bf16[192,1024]{1,0:T(8,128)(2,1)S(1)}, u32[]{:S(2)}, u32[]{:S(2)}) %collective-permute-start.23) | collective-permute-done | bytes 393248 | tf_op jit(solution)/shard_map/ppermute | solution.py:163
  156.3 10.1 %shard_map.156 = (bf16[2,768,768]{2,1,0:T(8,128)(2,1)}, bf16[2,768,768]{2,1,0:T(8,128)(2,1)}) custom-call(s32[2]{0:T(128)} %pad_add_fusion.3.index_ref, bf16[192,1024]{1,0:T(8,128)(2,1)} %copy-done.2, bf16[192,1024]{1,0:T(8,128)(2,1)} %copy-done.6, bf16[192,1024]{1,0:T(8,128)(2,1)} %copy-done.7, bf16[192,1024]{1,0:T(8,128)(2,1)} %copy-done.8, ...), custom_call_target="tpu_custom_call" | custom-call | tf_op jit(solution)/shard_map/pallas_call | solution.py:209
  166.4 4.7 %collective-permute-done.26 = bf16[2,768,768]{2,1,0:T(8,128)(2,1)S(1)} collective-permute-done((bf16[2,768,768]{2,1,0:T(8,128)(2,1)}, bf16[2,768,768]{2,1,0:T(8,128)(2,1)S(1)}, u32[]{:S(2)}, u32[]{:S(2)}) %collective-permute-start.26) | collective-permute-done | bytes 2359328 | tf_op jit(solution)/shard_map/ppermute | solution.py:138
  173.9 26.9 %collective-permute-done.27 = bf16[768,768]{1,0:T(8,128)(2,1)S(1)} collective-permute-done((bf16[768,768]{1,0:T(8,128)(2,1)S(1)}, bf16[768,768]{1,0:T(8,128)(2,1)S(1)}, u32[]{:S(2)}, u32[]{:S(2)}) %collective-permute-start.27) | collective-permute-done | bytes 1179680 | tf_op jit(solution)/shard_map/ppermute | solution.py:138
  209.8 6.8 %shard_map.157 = (f32[2,768,1]{2,1,0:T(8,128)}, f32[2,768,1]{2,1,0:T(8,128)}, f32[2,768,128]{2,1,0:T(8,128)}) custom-call(s32[1]{0:T(128)} %bitcast.19.place_ref, s32[1]{0:T(128)} %constant.96.clone.shift_ref, bf16[768,256]{1,0:T(8,128)(2,1)} %slice.135.q_ref, bf16[1,768,512]{2,1,0:T(8,128)(2,1)} %get-tuple-element.35.kv_ref), custom_call_target="tpu_custom_call" | custom-call | tf_op jit(solution)/shard_map/pallas_call | solution.py:387
  216.6 8.6 %collective-permute-done.28 = bf16[768,512]{1,0:T(8,128)(2,1)} collective-permute-done((bf16[768,512]{1,0:T(8,128)(2,1)}, bf16[768,512]{1,0:T(8,128)(2,1)}, u32[]{:S(2)}, u32[]{:S(2)}) %collective-permute-start.28) | collective-permute-done | bytes 786464 | tf_op jit(solution)/shard_map/ppermute | solution.py:470
  228.6 16.6 %collective-permute-done.29 = bf16[768,512]{1,0:T(8,128)(2,1)} collective-permute-done((bf16[768,512]{1,0:T(8,128)(2,1)}, bf16[768,512]{1,0:T(8,128)(2,1)}, u32[]{:S(2)}, u32[]{:S(2)}) %collective-permute-start.29) | collective-permute-done | bytes 786464 | tf_op jit(solution)/shard_map/ppermute | solution.py:470
  250.4 11.4 %collective-permute-done.32 = bf16[768,512]{1,0:T(8,128)(2,1)S(1)} collective-permute-done((bf16[768,512]{1,0:T(8,128)(2,1)}, bf16[768,512]{1,0:T(8,128)(2,1)S(1)}, u32[]{:S(2)}, u32[]{:S(2)}) %collective-permute-start.32) | collective-permute-done | bytes 786464 | tf_op jit(solution)/shard_map/ppermute | solution.py:470
  262.7 21.8 %collective-permute-done.33 = bf16[768,512]{1,0:T(8,128)(2,1)S(1)} collective-permute-done((bf16[768,512]{1,0:T(8,128)(2,1)}, bf16[768,512]{1,0:T(8,128)(2,1)S(1)}, u32[]{:S(2)}, u32[]{:S(2)}) %collective-permute-start.33) | collective-permute-done | bytes 786464 | tf_op jit(solution)/shard_map/ppermute | solution.py:470
  286.4 30.7 %shard_map.158.refs_0_ = bf16[768,256]{1,0:T(8,128)(2,1)} custom-call(s32[1]{0:T(128)} %bitcast.19.place_ref, s32[7]{0:T(128)} %constant.97.clone.shift_ref, bf16[768,256]{1,0:T(8,128)(2,1)} %slice.135.q_ref, bf16[7,768,512]{2,1,0:T(8,128)(2,1)} %bitcast_dynamic-update-slice_fusion.kv_ref, f32[2,768,1]{2,1,0:T(8,128)} %get-tuple-element.28.refs_0_, ...), custom_call_target="tpu_custom_call" | custom-call | tf_op jit(solution)/shard_map/pallas_call | solution.py:387
  319.0 10.2 %collective-permute-done.36.refs_2_ = bf16[768,256]{1,0:T(8,128)(2,1)S(1)} collective-permute-done((bf16[768,256]{1,0:T(8,128)(2,1)}, bf16[768,256]{1,0:T(8,128)(2,1)S(1)}, u32[]{:S(2)}, u32[]{:S(2)}) %collective-permute-start.36) | collective-permute-done | bytes 393248 | tf_op jit(solution)/shard_map/ppermute | solution.py:138
  329.2 7.6 %collective-permute-done.37.refs_3_ = bf16[768,256]{1,0:T(8,128)(2,1)S(1)} collective-permute-done((bf16[768,256]{1,0:T(8,128)(2,1)}, bf16[768,256]{1,0:T(8,128)(2,1)S(1)}, u32[]{:S(2)}, u32[]{:S(2)}) %collective-permute-start.37) | collective-permute-done | bytes 393248 | tf_op jit(solution)/shard_map/ppermute | solution.py:138
  337.6 5.4 %shard_map.159 = (bf16[192,1024]{1,0:T(8,128)(2,1)}, bf16[192,1024]{1,0:T(8,128)(2,1)}, bf16[192,1024]{1,0:T(8,128)(2,1)}, bf16[192,1024]{1,0:T(8,128)(2,1)}) custom-call(s32[2]{0:T(128)} %pad_add_fusion.2.index_ref, bf16[768,256]{1,0:T(8,128)(2,1)} %shard_map.158.refs_0_, bf16[768,256]{1,0:T(8,128)(2,1)} %copy-done.9, bf16[768,256]{1,0:T(8,128)(2,1)} %copy-done.10, ...), custom_call_target="tpu_custom_call" | custom-call | tf_op jit(solution)/shard_map/pallas_call | solution.py:251
  345.3 9.9 %collective-permute-done.40 = bf16[192,1024]{1,0:T(8,128)(2,1)S(1)} collective-permute-done((bf16[192,1024]{1,0:T(8,128)(2,1)}, bf16[192,1024]{1,0:T(8,128)(2,1)S(1)}, u32[]{:S(2)}, u32[]{:S(2)}) %collective-permute-start.40) | collective-permute-done | bytes 393248 | tf_op jit(solution)/shard_map/ppermute | solution.py:258
  358.2 7.1 %collective-permute-done.38 = bf16[192,1024]{1,0:T(8,128)(2,1)S(1)} collective-permute-done((bf16[192,1024]{1,0:T(8,128)(2,1)}, bf16[192,1024]{1,0:T(8,128)(2,1)S(1)}, u32[]{:S(2)}, u32[]{:S(2)}) %collective-permute-start.38) | collective-permute-done | bytes 393248 | tf_op jit(solution)/shard_map/ppermute | solution.py:258
  (181 shorter events, 114.6 us)
Async XLA Ops:
  8.9 14.5 %collective-permute-start.8 = (bf16[128,1024]{1,0:T(8,128)(2,1)S(1)}, bf16[128,1024]{1,0:T(8,128)(2,1)S(1)}, u32[]{:S(2)}, u32[]{:S(2)}) collective-permute-start(bf16[128,1024]{1,0:T(8,128)(2,1)S(1)} %fusion.24.refs_0_), channel_id=1, source_target_pairs={{0,2},{1,3},{2,0},{3,1},{4,6},{5,7},{6,4},{7,5},{8,10},{9,11},{10,... | collective-permute-start | bytes 786440 | tf_op jit(solution)/shard_map/ppermute | solution.py:163
  14.2 18.8 %collective-permute-start = (s32[128,2]{0,1:T(2,128)S(1)}, s32[128,2]{0,1:T(2,128)S(1)}, u32[]{:S(2)}, u32[]{:S(2)}) collective-permute-start(s32[128,2]{0,1:T(2,128)S(1)} %get-tuple-element.48), channel_id=1, source_target_pairs={{0,3},{1,0},{2,1},{3,2},{4,7},{5,4},{6,5},{7,6},{8,11},{9,8},{10,9... | collective-permute-start | bytes 3080 | tf_op jit(solution)/shard_map/ppermute | solution.py:50
  14.2 18.8 %collective-permute-start.1 = (s32[128,2]{0,1:T(2,128)S(1)}, s32[128,2]{0,1:T(2,128)S(1)}, u32[]{:S(2)}, u32[]{:S(2)}) collective-permute-start(s32[128,2]{0,1:T(2,128)S(1)} %get-tuple-element.48), channel_id=1, source_target_pairs={{0,2},{1,3},{2,0},{3,1},{4,6},{5,7},{6,4},{7,5},{8,10},{9,11},{10,... | collective-permute-start | bytes 3080 | tf_op jit(solution)/shard_map/ppermute | solution.py:50
  17.9 15.0 %collective-permute-start.2 = (s32[128,2]{0,1:T(2,128)S(1)}, s32[128,2]{0,1:T(2,128)S(1)}, u32[]{:S(2)}, u32[]{:S(2)}) collective-permute-start(s32[128,2]{0,1:T(2,128)S(1)} %get-tuple-element.48), channel_id=1, source_target_pairs={{0,1},{1,2},{2,3},{3,0},{4,5},{5,6},{6,7},{7,4},{8,9},{9,10},{10,1... | collective-permute-start | bytes 3080 | tf_op jit(solution)/shard_map/ppermute | solution.py:50
  38.1 19.9 %collective-permute-start.11 = (bf16[512,768]{1,0:T(8,128)(2,1)S(1)}, bf16[512,768]{1,0:T(8,128)(2,1)S(1)}, u32[]{:S(2)}, u32[]{:S(2)}) collective-permute-start(bf16[512,768]{1,0:T(8,128)(2,1)S(1)} %fusion.21), channel_id=1, source_target_pairs={{0,8},{4,12},{8,0},{12,4},{1,9},{5,13},{9,1},{13,5},{2,10},{6,14},... | collective-permute-start | bytes 2359304 | tf_op jit(solution)/shard_map/ppermute | solution.py:138
  39.5 17.1 %collective-permute-start.4 = (s32[2,255]{1,0:T(2,128)S(1)}, s32[2,255]{1,0:T(2,128)S(1)}, u32[]{:S(2)}, u32[]{:S(2)}) collective-permute-start(s32[2,255]{1,0:T(2,128)S(1)} %get-tuple-element.47), channel_id=1, source_target_pairs={{16,0},{32,16},{48,32},{64,48},{80,64},{96,80},{112,96},{17,1},{33... | collective-permute-start | bytes 6128 | tf_op jit(solution)/shard_map/ppermute | solution.py:23
  42.2 15.7 %collective-permute-start.3 = (s32[2,255]{1,0:T(2,128)S(1)}, s32[2,255]{1,0:T(2,128)S(1)}, u32[]{:S(2)}, u32[]{:S(2)}) collective-permute-start(s32[2,255]{1,0:T(2,128)S(1)} %get-tuple-element.46), channel_id=1, source_target_pairs={{0,16},{16,32},{32,48},{48,64},{64,80},{80,96},{96,112},{1,17},{17... | collective-permute-start | bytes 6128 | tf_op jit(solution)/shard_map/ppermute | solution.py:21
  64.4 12.3 %collective-permute-start.12 = (bf16[2,255,256]{2,1,0:T(8,128)(2,1)S(1)}, bf16[2,255,256]{2,1,0:T(8,128)(2,1)S(1)}, u32[]{:S(2)}, u32[]{:S(2)}) collective-permute-start(bf16[2,255,256]{2,1,0:T(8,128)(2,1)S(1)} %get-tuple-element.42), channel_id=1, source_target_pairs={{0,16},{16,32},{32,48},{48,64},{64,80},{80,96},{96,112},{1,17},{17... | collective-permute-start | bytes 783368 | tf_op jit(solution)/shard_map/ppermute | solution.py:21
  83.2 12.7 %collective-permute-start.16 = (bf16[512,256]{1,0:T(8,128)(2,1)S(1)}, bf16[512,256]{1,0:T(8,128)(2,1)S(1)}, u32[]{:S(2)}, u32[]{:S(2)}) collective-permute-start(bf16[512,256]{1,0:T(8,128)(2,1)S(1)} %copy.26.refs_0_), channel_id=1, source_target_pairs={{0,12},{4,8},{8,4},{12,0},{1,13},{5,9},{9,5},{13,1},{2,14},{6,10},... | collective-permute-start | bytes 786440 | tf_op jit(solution)/shard_map/ppermute | solution.py:138
  103.8 14.4 %collective-permute-start.17 = (bf16[128,1024]{1,0:T(8,128)(2,1)}, bf16[128,1024]{1,0:T(8,128)(2,1)S(1)}, u32[]{:S(2)}, u32[]{:S(2)}) collective-permute-start(bf16[128,1024]{1,0:T(8,128)(2,1)} %get-tuple-element.23), channel_id=1, source_target_pairs={{0,1},{1,2},{2,3},{3,0},{4,5},{5,6},{6,7},{7,4},{8,9},{9,10},{10,1... | collective-permute-start | bytes 786440 | tf_op jit(solution)/shard_map/ppermute | solution.py:258
  134.8 19.8 %collective-permute-start.23 = (bf16[192,1024]{1,0:T(8,128)(2,1)S(1)}, bf16[192,1024]{1,0:T(8,128)(2,1)S(1)}, u32[]{:S(2)}, u32[]{:S(2)}) collective-permute-start(bf16[192,1024]{1,0:T(8,128)(2,1)S(1)} %multiply_convert_fusion.refs_0_), channel_id=1, source_target_pairs={{0,1},{1,2},{2,3},{3,0},{4,5},{5,6},{6,7},{7,4},{8,9},{9,10},{10,1... | collective-permute-start | bytes 1179656 | tf_op jit(solution)/shard_map/ppermute | solution.py:163
  134.9 19.7 %collective-permute-start.24 = (bf16[192,1024]{1,0:T(8,128)(2,1)S(1)}, bf16[192,1024]{1,0:T(8,128)(2,1)S(1)}, u32[]{:S(2)}, u32[]{:S(2)}) collective-permute-start(bf16[192,1024]{1,0:T(8,128)(2,1)S(1)} %multiply_convert_fusion.refs_0_), channel_id=1, source_target_pairs={{0,2},{1,3},{2,0},{3,1},{4,6},{5,7},{6,4},{7,5},{8,10},{9,11},{10,... | collective-permute-start | bytes 1179656 | tf_op jit(solution)/shard_map/ppermute | solution.py:163
  136.2 19.1 %collective-permute-start.25 = (bf16[192,1024]{1,0:T(8,128)(2,1)S(1)}, bf16[192,1024]{1,0:T(8,128)(2,1)S(1)}, u32[]{:S(2)}, u32[]{:S(2)}) collective-permute-start(bf16[192,1024]{1,0:T(8,128)(2,1)S(1)} %multiply_convert_fusion.refs_0_), channel_id=1, source_target_pairs={{0,3},{1,0},{2,1},{3,2},{4,7},{5,4},{6,5},{7,6},{8,11},{9,8},{10,9... | collective-permute-start | bytes 1179656 | tf_op jit(solution)/shard_map/ppermute | solution.py:163
  172.7 28.1 %collective-permute-start.27 = (bf16[768,768]{1,0:T(8,128)(2,1)S(1)}, bf16[768,768]{1,0:T(8,128)(2,1)S(1)}, u32[]{:S(2)}, u32[]{:S(2)}) collective-permute-start(bf16[768,768]{1,0:T(8,128)(2,1)S(1)} %fusion.20), channel_id=1, source_target_pairs={{0,8},{4,12},{8,0},{12,4},{1,9},{5,13},{9,1},{13,5},{2,10},{6,14},... | collective-permute-start | bytes 3538952 | tf_op jit(solution)/shard_map/ppermute | solution.py:138
  202.6 22.6 %collective-permute-start.28 = (bf16[768,512]{1,0:T(8,128)(2,1)}, bf16[768,512]{1,0:T(8,128)(2,1)}, u32[]{:S(2)}, u32[]{:S(2)}) collective-permute-start(bf16[768,512]{1,0:T(8,128)(2,1)} %get-tuple-element.36), channel_id=1, source_target_pairs={{0,16},{16,32},{32,48},{48,64},{64,80},{80,96},{96,112},{1,17},{17... | collective-permute-start | bytes 2359304 | tf_op jit(solution)/shard_map/ppermute | solution.py:470
  203.8 41.3 %collective-permute-start.29 = (bf16[768,512]{1,0:T(8,128)(2,1)}, bf16[768,512]{1,0:T(8,128)(2,1)}, u32[]{:S(2)}, u32[]{:S(2)}) collective-permute-start(bf16[768,512]{1,0:T(8,128)(2,1)} %get-tuple-element.36), channel_id=1, source_target_pairs={{0,32},{16,48},{32,64},{48,80},{64,96},{80,112},{1,33},{17,49},{33... | collective-permute-start | bytes 2359304 | tf_op jit(solution)/shard_map/ppermute | solution.py:470
  205.2 43.4 %collective-permute-start.30 = (bf16[768,512]{1,0:T(8,128)(2,1)}, bf16[768,512]{1,0:T(8,128)(2,1)S(1)}, u32[]{:S(2)}, u32[]{:S(2)}) collective-permute-start(bf16[768,512]{1,0:T(8,128)(2,1)} %get-tuple-element.36), channel_id=1, source_target_pairs={{0,48},{16,64},{32,80},{48,96},{64,112},{1,49},{17,65},{33,81},{49... | collective-permute-start | bytes 2359304 | tf_op jit(solution)/shard_map/ppermute | solution.py:470
  207.2 42.3 %collective-permute-start.31 = (bf16[768,512]{1,0:T(8,128)(2,1)}, bf16[768,512]{1,0:T(8,128)(2,1)S(1)}, u32[]{:S(2)}, u32[]{:S(2)}) collective-permute-start(bf16[768,512]{1,0:T(8,128)(2,1)} %get-tuple-element.36), channel_id=1, source_target_pairs={{0,64},{16,80},{32,96},{48,112},{1,65},{17,81},{33,97},{49,113},{2... | collective-permute-start | bytes 2359304 | tf_op jit(solution)/shard_map/ppermute | solution.py:470
  208.5 53.2 %collective-permute-start.32 = (bf16[768,512]{1,0:T(8,128)(2,1)}, bf16[768,512]{1,0:T(8,128)(2,1)S(1)}, u32[]{:S(2)}, u32[]{:S(2)}) collective-permute-start(bf16[768,512]{1,0:T(8,128)(2,1)} %get-tuple-element.36), channel_id=1, source_target_pairs={{0,80},{16,96},{32,112},{1,81},{17,97},{33,113},{2,82},{18,98},{34... | collective-permute-start | bytes 2359304 | tf_op jit(solution)/shard_map/ppermute | solution.py:470
  225.2 59.3 %collective-permute-start.33 = (bf16[768,512]{1,0:T(8,128)(2,1)}, bf16[768,512]{1,0:T(8,128)(2,1)S(1)}, u32[]{:S(2)}, u32[]{:S(2)}) collective-permute-start(bf16[768,512]{1,0:T(8,128)(2,1)} %get-tuple-element.36), channel_id=1, source_target_pairs={{0,96},{16,112},{1,97},{17,113},{2,98},{18,114},{3,99},{19,115},{4... | collective-permute-start | bytes 2359304 | tf_op jit(solution)/shard_map/ppermute | solution.py:470
  245.2 40.3 %collective-permute-start.34 = (bf16[768,512]{1,0:T(8,128)(2,1)}, bf16[768,512]{1,0:T(8,128)(2,1)S(1)}, u32[]{:S(2)}, u32[]{:S(2)}) collective-permute-start(bf16[768,512]{1,0:T(8,128)(2,1)} %get-tuple-element.36), channel_id=1, source_target_pairs={{0,112},{1,113},{2,114},{3,115},{4,116},{5,117},{6,118},{7,119},{8... | collective-permute-start | bytes 2359304 | tf_op jit(solution)/shard_map/ppermute | solution.py:470
  318.0 18.8 %collective-permute-start.37 = (bf16[768,256]{1,0:T(8,128)(2,1)}, bf16[768,256]{1,0:T(8,128)(2,1)S(1)}, u32[]{:S(2)}, u32[]{:S(2)}) collective-permute-start(bf16[768,256]{1,0:T(8,128)(2,1)} %shard_map.158.refs_0_), channel_id=1, source_target_pairs={{0,12},{4,8},{8,4},{12,0},{1,13},{5,9},{9,5},{13,1},{2,14},{6,10},... | collective-permute-start | bytes 1179656 | tf_op jit(solution)/shard_map/ppermute | solution.py:138
  344.5 13.7 %collective-permute-start.39 = (bf16[192,1024]{1,0:T(8,128)(2,1)}, bf16[192,1024]{1,0:T(8,128)(2,1)S(1)}, u32[]{:S(2)}, u32[]{:S(2)}) collective-permute-start(bf16[192,1024]{1,0:T(8,128)(2,1)} %get-tuple-element.33), channel_id=1, source_target_pairs={{0,2},{1,3},{2,0},{3,1},{4,6},{5,7},{6,4},{7,5},{8,10},{9,11},{10,... | collective-permute-start | bytes 1179656 | tf_op jit(solution)/shard_map/ppermute | solution.py:258
  344.5 20.9 %collective-permute-start.38 = (bf16[192,1024]{1,0:T(8,128)(2,1)}, bf16[192,1024]{1,0:T(8,128)(2,1)S(1)}, u32[]{:S(2)}, u32[]{:S(2)}) collective-permute-start(bf16[192,1024]{1,0:T(8,128)(2,1)} %get-tuple-element.32), channel_id=1, source_target_pairs={{0,1},{1,2},{2,3},{3,0},{4,5},{5,6},{6,7},{7,4},{8,9},{9,10},{10,1... | collective-permute-start | bytes 1179656 | tf_op jit(solution)/shard_map/ppermute | solution.py:258
  (39 other events, 402.3 us)
